TPU v7x, 512 devices: a whole 4x4x16 slice. The times are simulated.
512 devices in a mesh: expert: 128 (over x, z, core), dp: 4 (over y).
Axes of the slice: x: 4, y: 4, z: 16, core: 2. Of those that a mesh axis runs over, the one named last changes fastest.
Arguments:
- tokens: bfloat16 [16384, 3584], P('expert', 'dp'), may hold values from -6 to 6
- routes: int32 [16384, 2], P('expert'), may hold values from 0 to 63, all different within a row; in each aligned block of 128 rows (0 to 127, 128 to 255, ...) at most 6 rows name the same one
- logits: float32 [16384, 2], P('expert'), may hold values from -6 to 6
- cotangent: bfloat16 [16384, 3584], P('expert', 'dp'), may hold values from -6 to 6
- pair_flags: int32 [32], replicated, may hold values from -1000 to 999
- w_up: bfloat16 [3584, 65536], P('dp', 'expert'), may hold values from -0.09375 to 0.09375
- w_down: bfloat16 [3584, 65536], P('dp', 'expert'), may hold values from -0.1875 to 0.1875
Outputs:
- grad_tokens: bfloat16 [16384, 3584], P('expert', 'dp')
- grad_logits: float32 [16384, 2], P('expert')
- grad_up: bfloat16 [3584, 65536], P('dp', 'expert')
- grad_down: bfloat16 [3584, 65536], P('dp', 'expert')
Inputs may be any that keep to these rules, and one draw needn't show every extreme that they name: `routes`: among the 128 tokens of one index of the expert axis no expert is named more than 6 times, a bound that some block reaches; a token names 2 distinct experts.
All inputs are finite; a program needn't handle non-finite values.
Results may differ from a plain program's by a relative error of at most 0.02.
Values may be sent and summed in bfloat16 or wider, within the bound.
No kernel may reach another device: no remote copies, remote signals or barrier semaphores. Data moves between devices by JAX's collectives and lax.ppermute only.
A program may use at most 64 MiB of HBM per device.

v0:
```python
import jax
import jax.numpy as jnp
from jax import lax
from jax.sharding import PartitionSpec as P


def passed_along(value, axis, steps):
    count = lax.axis_size(axis)
    pairs = [(source, (source + steps) % count) for source in range(count)]
    return lax.ppermute(value, axis, pairs)


def pick_pair(swapped_here, theirs, ours):
    return tuple(
        (
            jnp.where(swapped_here, other_part, mine_part)
            for other_part, mine_part in zip(theirs, ours)
        )
    )


def activate(up_pre, grad_hidden):
    up_sig = jax.nn.sigmoid(up_pre)
    hidden = (up_pre * up_sig).astype(jnp.bfloat16)
    pairing_part = jnp.sum(hidden.astype(jnp.float32) * grad_hidden, -1)
    grad_pre = (grad_hidden * up_sig * (1.0 + up_pre * (1.0 - up_sig))).astype(jnp.bfloat16)
    return (hidden, pairing_part, grad_pre)


def local(tokens, routes, logits, cotangent, pair_flags, w_up, w_down):
    devices_ex = lax.axis_size("expert")
    experts = devices_ex // 2
    half_way = experts // 2
    here_index = lax.axis_index("expert")
    slot_here = here_index // 2
    tok_rows, top_count = routes.shape
    quarter = tokens.shape[1]
    capacity = max(2, 2 * (3 * tok_rows * top_count // (4 * experts)))
    expert_ids = jnp.arange(experts, dtype=jnp.int32)
    paired = jnp.concatenate([pair_flags, pair_flags]) > 0
    owner_slot = jnp.where(paired, (expert_ids + half_way) % experts, expert_ids)
    swapped_here = paired[slot_here]
    affinity = jax.nn.sigmoid(logits)
    weights = affinity / jnp.sum(affinity, -1, keepdims=True)
    scaled = (weights[:, :, None] * cotangent[:, None, :].astype(jnp.float32)).astype(jnp.bfloat16)
    scaled = scaled.reshape(-1, quarter)
    flat_routes = routes.reshape(-1)
    onehot = (flat_routes[:, None] == expert_ids[None, :]).astype(jnp.int32)
    slot_rank = jnp.sum(jnp.cumsum(onehot, 0) * onehot, 1) - 1
    own_weights = (w_up, w_down)
    shifted = passed_along((w_up, w_down), "expert", devices_ex // 2)
    resident = pick_pair(swapped_here, shifted, own_weights)
    target = owner_slot[flat_routes]
    position = target * capacity + slot_rank
    empty_rows = jnp.zeros((experts * capacity, quarter), jnp.bfloat16)
    token_buf = (
        empty_rows.at[position]
        .set(jnp.repeat(tokens, top_count, axis=0))
        .reshape(experts, capacity, quarter)
    )
    scaled_buf = empty_rows.at[position].set(scaled).reshape(experts, capacity, quarter)
    token_in, scaled_in = (
        lax.all_to_all(
            jnp.repeat(token_buf, 2, axis=0), "expert", split_axis=0, concat_axis=0, tiled=True
        ),
        lax.all_to_all(
            jnp.repeat(scaled_buf, 2, axis=0), "expert", split_axis=0, concat_axis=0, tiled=True
        ),
    )
    routed_rows = token_in.reshape(-1, quarter)
    scaled_rows = scaled_in.reshape(-1, quarter)
    up_block, down_block = resident
    up_part = jnp.dot(routed_rows, up_block, preferred_element_type=jnp.float32)
    grad_part = jnp.dot(scaled_rows, down_block, preferred_element_type=jnp.float32)
    up_pre, grad_hidden = (
        lax.psum(up_part.astype(jnp.bfloat16), "dp").astype(jnp.float32),
        lax.psum(grad_part.astype(jnp.bfloat16), "dp").astype(jnp.float32),
    )
    hidden, pairing_part, grad_pre = activate(up_pre, grad_hidden)
    pairing_half = pairing_part.astype(jnp.bfloat16)
    route_half = jnp.einsum(
        "nf,df->nd", grad_pre, up_block, preferred_element_type=jnp.float32
    ).astype(jnp.bfloat16)
    grad_up = jnp.einsum(
        "nd,nf->df", routed_rows, grad_pre, preferred_element_type=jnp.float32
    ).astype(jnp.bfloat16)
    grad_down = jnp.einsum(
        "nd,nf->df", scaled_rows, hidden, preferred_element_type=jnp.float32
    ).astype(jnp.bfloat16)
    back_rows, back_pairing = (
        lax.all_to_all(
            route_half.reshape(devices_ex, capacity, quarter),
            "expert",
            split_axis=0,
            concat_axis=0,
            tiled=True,
        ),
        lax.all_to_all(
            pairing_half.reshape(devices_ex, capacity),
            "expert",
            split_axis=0,
            concat_axis=0,
            tiled=True,
        ),
    )
    back_grid = back_rows.reshape(experts, 2, capacity, quarter)
    picked = back_grid[target, :, slot_rank]
    grad_tokens = jnp.sum(
        picked.astype(jnp.float32).reshape(tok_rows, top_count * 2, quarter), 1
    ).astype(jnp.bfloat16)
    pair_grid = back_pairing.reshape(experts, 2, capacity)
    pair_picked = pair_grid[target, :, slot_rank]
    pairing_mine = jnp.sum(pair_picked.astype(jnp.float32), 1).reshape(tok_rows, top_count)
    grad_logits = (1.0 - affinity) * (
        pairing_mine - weights * jnp.sum(pairing_mine, -1, keepdims=True)
    )
    return (grad_tokens, grad_logits, grad_up, grad_down)


def solution(mesh):
    in_specs = (
        P("expert", "dp"),
        P("expert", None),
        P("expert", None),
        P("expert", "dp"),
        P(),
        P("dp", "expert"),
        P("dp", "expert"),
    )
    out_specs = (P("expert", "dp"), P("expert", None), P("dp", "expert"), P("dp", "expert"))
    return jax.shard_map(local, mesh=mesh, in_specs=in_specs, out_specs=out_specs, check_vma=False)
```

profile of v0, /device:TPU:1, one launch (start us, length us, event | category | flops | bytes accessed | tf_op | source)
XLA Modules:
  0.0 437.8 jit_solution(4129395316092720993)
XLA Ops:
  10.2 1.2 broadcast_in_dim.10
  11.5 1.9 gather_fusion
  13.4 1.9 scatter_custom_fusion.1
  15.5 1.4 broadcast_in_dim.11
  16.9 20.5 %all-to-all-start.1 = ((bf16[128,6,896]{2,1,0:T(8,128)(2,1)}), bf16[128,6,896]{2,1,0:T(8,128)(2,1)S(1)}, u32[]{:S(2)}, u32[]{:S(2)}) async-start(bf16[128,6,896]{2,1,0:T(8,128)(2,1)} %bitcast.36), calls=%async_computation.1 | async-start | bytes 3670016 | tf_op jit(solution)/shard_map/all_to_all | solution.py:63
  37.9 1.2 mul.61
  39.1 1.8 mul.62
  40.9 1.9 scatter_custom_fusion
  43.1 82.2 %all-to-all-done.1 = bf16[128,6,896]{2,1,0:T(8,128)(2,1)S(1)} async-done(((bf16[128,6,896]{2,1,0:T(8,128)(2,1)}), bf16[128,6,896]{2,1,0:T(8,128)(2,1)S(1)}, u32[]{:S(2)}, u32[]{:S(2)}) %all-to-all-start.1) | async-done | bytes 1376288 | tf_op jit(solution)/shard_map/all_to_all | solution.py:63
  125.3 1.4 broadcast_in_dim.9
  126.7 9.1 %all-to-all-start = ((bf16[128,6,896]{2,1,0:T(8,128)(2,1)}), bf16[128,6,896]{2,1,0:T(8,128)(2,1)}, u32[]{:S(2)}, u32[]{:S(2)}) async-start(bf16[128,6,896]{2,1,0:T(8,128)(2,1)} %bitcast.35), calls=%async_computation | async-start | bytes 3670016 | tf_op jit(solution)/shard_map/all_to_all | solution.py:66
  135.8 5.1 %collective-permute-start = (bf16[896,512]{1,0:T(8,128)(2,1)}, bf16[896,512]{1,0:T(8,128)(2,1)}, u32[]{:S(2)}, u32[]{:S(2)}) collective-permute-start(bf16[896,512]{1,0:T(8,128)(2,1)} %param.13), channel_id=1, source_target_pairs={{0,256},{4,260},{8,264},{12,268},{16,272},{20,276},{24,280},{28,28... | collective-permute-start | bytes 2752520 | tf_op jit(solution)/shard_map/ppermute | solution.py:10
  140.9 2.1 collective-permute-start.1
  144.2 79.2 %all-to-all-done = bf16[128,6,896]{2,1,0:T(8,128)(2,1)} async-done(((bf16[128,6,896]{2,1,0:T(8,128)(2,1)}), bf16[128,6,896]{2,1,0:T(8,128)(2,1)}, u32[]{:S(2)}, u32[]{:S(2)}) %all-to-all-start) | async-done | bytes 1376288 | tf_op jit(solution)/shard_map/all_to_all | solution.py:66
  223.4 2.5 reshape.177
  225.9 3.8 convolution_convert_fusion.4
  229.6 3.7 convolution_convert_fusion.3
  233.4 59.6 %all-reduce.3.cloned.1.call-done = (bf16[768,512]{1,0:T(8,128)(2,1)}, bf16[768,512]{1,0:T(8,128)(2,1)}) async-done(((bf16[768,512]{1,0:T(8,128)(2,1)}, bf16[768,512]{1,0:T(8,128)(2,1)}), (bf16[768,512]{1,0:T(8,128)(2,1)}, bf16[768,512]{1,0:T(8,128)(2,1)})) %all-reduce.3.cloned.1.call-update) | async-done | bytes 1572880 | tf_op jit(solution)/shard_map/psum | solution.py:77
  293.0 1.9 fusion.2
  295.7 16.7 %all-to-all-start.3 = ((bf16[128,1,6]{2,1,0:T(2,128)(2,1)}), bf16[128,1,6]{2,1,0:T(2,128)(2,1)S(1)}, u32[]{:S(2)}, u32[]{:S(2)}) async-start(bf16[128,1,6]{2,1,0:T(2,128)(2,1)} %convert_element_type.86), calls=%async_computation.3 | async-start | bytes 131072 | tf_op jit(solution)/shard_map/all_to_all | solution.py:98
  312.4 3.6 convolution_convert_fusion
  316.1 1.5 reshape.182
  317.6 9.8 %all-to-all-done.3 = bf16[128,1,6]{2,1,0:T(2,128)(2,1)S(1)} async-done(((bf16[128,1,6]{2,1,0:T(2,128)(2,1)}), bf16[128,1,6]{2,1,0:T(2,128)(2,1)S(1)}, u32[]{:S(2)}, u32[]{:S(2)}) %all-to-all-start.3) | async-done | bytes 1568 | tf_op jit(solution)/shard_map/all_to_all | solution.py:98
  327.4 6.6 %all-to-all-start.2 = ((bf16[128,6,896]{2,1,0:T(8,128)(2,1)}), bf16[128,6,896]{2,1,0:T(8,128)(2,1)S(1)}, u32[]{:S(2)}, u32[]{:S(2)}) async-start(bf16[128,6,896]{2,1,0:T(8,128)(2,1)} %reshape.182), calls=%async_computation.2 | async-start | bytes 3670016 | tf_op jit(solution)/shard_map/all_to_all | solution.py:91
  334.1 3.6 convolution_convert_fusion.1
  337.7 2.0 convolution_convert_fusion.2
  340.3 1.6 gather_fusion.2
  343.0 79.0 %all-to-all-done.2 = bf16[128,6,896]{2,1,0:T(8,128)(2,1)S(1)} async-done(((bf16[128,6,896]{2,1,0:T(8,128)(2,1)}), bf16[128,6,896]{2,1,0:T(8,128)(2,1)S(1)}, u32[]{:S(2)}, u32[]{:S(2)}) %all-to-all-start.2) | async-done | bytes 1376288 | tf_op jit(solution)/shard_map/all_to_all | solution.py:91
  422.0 1.1 copy.53
  423.1 2.8 gather_fusion.1
  425.9 2.6 convert_reduce_fusion
  429.1 1.9 reduce_sum.65
  (47 shorter events, 8.3 us)
Async XLA Ops:
  16.9 20.5 %copy-start.4 = (f32[128,2]{0,1:T(2,128)S(1)}, f32[128,2]{0,1:T(2,128)}, u32[]{:S(2)}) copy-start(f32[128,2]{0,1:T(2,128)} %param.9) | copy-start | bytes 3076
  16.9 21.0 %copy-start.3 = (bf16[128,896]{1,0:T(8,128)(2,1)S(1)}, bf16[128,896]{1,0:T(8,128)(2,1)}, u32[]{:S(2)}) copy-start(bf16[128,896]{1,0:T(8,128)(2,1)} %param.10) | copy-start | bytes 688132
  16.9 108.4 %all-to-all-start.1 = ((bf16[128,6,896]{2,1,0:T(8,128)(2,1)}), bf16[128,6,896]{2,1,0:T(8,128)(2,1)S(1)}, u32[]{:S(2)}, u32[]{:S(2)}) async-start(bf16[128,6,896]{2,1,0:T(8,128)(2,1)} %bitcast.36), calls=%async_computation.1 | async-start | bytes 3670016 | tf_op jit(solution)/shard_map/all_to_all | solution.py:63
  126.7 96.7 %all-to-all-start = ((bf16[128,6,896]{2,1,0:T(8,128)(2,1)}), bf16[128,6,896]{2,1,0:T(8,128)(2,1)}, u32[]{:S(2)}, u32[]{:S(2)}) async-start(bf16[128,6,896]{2,1,0:T(8,128)(2,1)} %bitcast.35), calls=%async_computation | async-start | bytes 3670016 | tf_op jit(solution)/shard_map/all_to_all | solution.py:66
  135.8 157.2 %all-reduce.3.cloned.1.call-start = ((), (), s32[]{:S(2)}) async-start(), calls=%async_computation.4 | async-start | bytes 3145728 | tf_op jit(solution)/shard_map/psum | solution.py:77
  135.8 90.0 %collective-permute-start = (bf16[896,512]{1,0:T(8,128)(2,1)}, bf16[896,512]{1,0:T(8,128)(2,1)}, u32[]{:S(2)}, u32[]{:S(2)}) collective-permute-start(bf16[896,512]{1,0:T(8,128)(2,1)} %param.13), channel_id=1, source_target_pairs={{0,256},{4,260},{8,264},{12,268},{16,272},{20,276},{24,280},{28,28... | collective-permute-start | bytes 2752520 | tf_op jit(solution)/shard_map/ppermute | solution.py:10
  140.9 88.7 %collective-permute-start.1 = (bf16[896,512]{1,0:T(8,128)(2,1)}, bf16[896,512]{1,0:T(8,128)(2,1)}, u32[]{:S(2)}, u32[]{:S(2)}) collective-permute-start(bf16[896,512]{1,0:T(8,128)(2,1)} %param.12), channel_id=1, source_target_pairs={{0,256},{4,260},{8,264},{12,268},{16,272},{20,276},{24,280},{28,28... | collective-permute-start | bytes 2752520 | tf_op jit(solution)/shard_map/ppermute | solution.py:10
  225.8 3.8 copy-start
  295.7 31.7 %all-to-all-start.3 = ((bf16[128,1,6]{2,1,0:T(2,128)(2,1)}), bf16[128,1,6]{2,1,0:T(2,128)(2,1)S(1)}, u32[]{:S(2)}, u32[]{:S(2)}) async-start(bf16[128,1,6]{2,1,0:T(2,128)(2,1)} %convert_element_type.86), calls=%async_computation.3 | async-start | bytes 131072 | tf_op jit(solution)/shard_map/all_to_all | solution.py:98
  327.4 94.6 %all-to-all-start.2 = ((bf16[128,6,896]{2,1,0:T(8,128)(2,1)}), bf16[128,6,896]{2,1,0:T(8,128)(2,1)S(1)}, u32[]{:S(2)}, u32[]{:S(2)}) async-start(bf16[128,6,896]{2,1,0:T(8,128)(2,1)} %reshape.182), calls=%async_computation.2 | async-start | bytes 3670016 | tf_op jit(solution)/shard_map/all_to_all | solution.py:91
  334.0 3.6 copy-start.1
  334.0 3.6 copy-start.2
Sparse Core Ops, SparseCore 0:
  233.5 59.4 all-reduce.2
where the time goes:
time: 439 us; the launch traced here: 438 us
  waiting for transfers between devices  310 us (71%)
  starting transfers between devices  60.2 us (14%)
  local copies, waits for them, and re-layouts  26.2 us (6%)
  matrix products  16.8 us (4%)
  between operations  14.3 us (3%)
  other arithmetic  10.5 us (2%)
    all_to_all x1, waiting for transfers between devices, local(): lax.all_to_all(jnp.repeat(token_buf, 2, axis=0), 'expert', split_axis=0,...  82.2 us
    all_to_all x1, waiting for transfers between devices, local(): lax.all_to_all(jnp.repeat(scaled_buf, 2, axis=0), 'expert', split_axis=0,...  79.2 us
    all_to_all x1, waiting for transfers between devices, local(): lax.all_to_all(route_half.reshape(devices_ex, capacity, quarter), 'expert...  79 us
    psum x1, waiting for transfers between devices, local(): lax.psum(grad_part.astype(jnp.bfloat16), 'dp').astype(jnp.float32)  59.6 us
    all_to_all x1, starting transfers between devices, local(): lax.all_to_all(jnp.repeat(token_buf, 2, axis=0), 'expert', split_axis=0,...  20.5 us
    all_to_all x1, starting transfers between devices, local(): lax.all_to_all(pairing_half.reshape(devices_ex, capacity), 'expert', spli...  16.7 us
    all_to_all x1, waiting for transfers between devices, local(): lax.all_to_all(pairing_half.reshape(devices_ex, capacity), 'expert', spli...  9.83 us
    all_to_all x1, starting transfers between devices, local(): lax.all_to_all(jnp.repeat(scaled_buf, 2, axis=0), 'expert', split_axis=0,...  9.12 us
  transfers between devices with their start and end apart: 7, of which 5 were waited for; matrix products, arithmetic and copies ran while one was open for 6% of the time, Pallas kernels for 0%

commit v1 on v0

--- a/solution.py
+++ b/solution.py
@@ -7,6 +7,12 @@
 def passed_along(value, axis, steps):
     count = lax.axis_size(axis)
     pairs = [(source, (source + steps) % count) for source in range(count)]
+    return lax.ppermute(value, axis, pairs)
+
+
+def core_swap(value, axis):
+    count = lax.axis_size(axis)
+    pairs = [(source, source ^ 1) for source in range(count)]
     return lax.ppermute(value, axis, pairs)
 
 
@@ -33,9 +39,12 @@
     half_way = experts // 2
     here_index = lax.axis_index("expert")
     slot_here = here_index // 2
+    first_core = (here_index % 2) == 0
     tok_rows, top_count = routes.shape
     quarter = tokens.shape[1]
     capacity = max(2, 2 * (3 * tok_rows * top_count // (4 * experts)))
+    share = capacity // 2
+    lanes = 128
     expert_ids = jnp.arange(experts, dtype=jnp.int32)
     paired = jnp.concatenate([pair_flags, pair_flags]) > 0
     owner_slot = jnp.where(paired, (expert_ids + half_way) % experts, expert_ids)
@@ -59,16 +68,11 @@
         .reshape(experts, capacity, quarter)
     )
     scaled_buf = empty_rows.at[position].set(scaled).reshape(experts, capacity, quarter)
-    token_in, scaled_in = (
-        lax.all_to_all(
-            jnp.repeat(token_buf, 2, axis=0), "expert", split_axis=0, concat_axis=0, tiled=True
-        ),
-        lax.all_to_all(
-            jnp.repeat(scaled_buf, 2, axis=0), "expert", split_axis=0, concat_axis=0, tiled=True
-        ),
-    )
-    routed_rows = token_in.reshape(-1, quarter)
-    scaled_rows = scaled_in.reshape(-1, quarter)
+    dispatch = jnp.stack([token_buf, scaled_buf], axis=1).reshape(devices_ex, capacity, quarter)
+    got = lax.all_to_all(dispatch, "expert", split_axis=0, concat_axis=0, tiled=True)
+    partner_got = core_swap(got, "expert")
+    routed_rows = jnp.where(first_core, got, partner_got).reshape(-1, quarter)
+    scaled_rows = jnp.where(first_core, partner_got, got).reshape(-1, quarter)
     up_block, down_block = resident
     up_part = jnp.dot(routed_rows, up_block, preferred_element_type=jnp.float32)
     grad_part = jnp.dot(scaled_rows, down_block, preferred_element_type=jnp.float32)
@@ -87,30 +91,30 @@
     grad_down = jnp.einsum(
         "nd,nf->df", scaled_rows, hidden, preferred_element_type=jnp.float32
     ).astype(jnp.bfloat16)
-    back_rows, back_pairing = (
-        lax.all_to_all(
-            route_half.reshape(devices_ex, capacity, quarter),
-            "expert",
-            split_axis=0,
-            concat_axis=0,
-            tiled=True,
-        ),
-        lax.all_to_all(
-            pairing_half.reshape(devices_ex, capacity),
-            "expert",
-            split_axis=0,
-            concat_axis=0,
-            tiled=True,
-        ),
+    lane_ids = jnp.arange(lanes, dtype=jnp.int32)
+    my_lane = jnp.where(first_core, 0, 1)
+    pair_cols = jnp.where(
+        lane_ids[None, None, :] == my_lane,
+        pairing_half.reshape(devices_ex, capacity, 1),
+        jnp.zeros((), jnp.bfloat16),
     )
-    back_grid = back_rows.reshape(experts, 2, capacity, quarter)
-    picked = back_grid[target, :, slot_rank]
+    packed = jnp.concatenate(
+        [route_half.reshape(devices_ex, capacity, quarter), pair_cols], axis=-1
+    )
+    low, high = packed[:, :share], packed[:, share:]
+    keep = jnp.where(first_core, low, high)
+    give = jnp.where(first_core, high, low)
+    taken = core_swap(give, "expert")
+    combined = (keep.astype(jnp.float32) + taken.astype(jnp.float32)).astype(jnp.bfloat16)
+    back = lax.all_to_all(combined, "expert", split_axis=0, concat_axis=0, tiled=True)
+    back_grid = back.reshape(experts, capacity, quarter + lanes)
+    picked = back_grid[target, slot_rank]
     grad_tokens = jnp.sum(
-        picked.astype(jnp.float32).reshape(tok_rows, top_count * 2, quarter), 1
+        picked[:, :quarter].astype(jnp.float32).reshape(tok_rows, top_count, quarter), 1
     ).astype(jnp.bfloat16)
-    pair_grid = back_pairing.reshape(experts, 2, capacity)
-    pair_picked = pair_grid[target, :, slot_rank]
-    pairing_mine = jnp.sum(pair_picked.astype(jnp.float32), 1).reshape(tok_rows, top_count)
+    pairing_mine = (
+        picked[:, quarter].astype(jnp.float32) + picked[:, quarter + 1].astype(jnp.float32)
+    ).reshape(tok_rows, top_count)
     grad_logits = (1.0 - affinity) * (
         pairing_mine - weights * jnp.sum(pairing_mine, -1, keepdims=True)
     )

time: 439 us -> 340 us (0.77)
  waiting for transfers between devices: 310 us -> 139 us
  blocking collectives: 0 us -> 108 us
  starting transfers between devices: 60.2 us -> 28.7 us
    all_to_all x4 -> x1, waiting for transfers between devices: 250 us -> 50.4 us  [local(): lax.all_to_all(combined, 'expert', split_axis=0, concat_axis=0, tiled=True)]
    all_to_all x0 -> x1, blocking collectives: none -> 108 us  [local(): lax.all_to_all(dispatch, 'expert', split_axis=0, concat_axis=0, tiled=True)]
    all_to_all x4 -> x1, starting transfers between devices: 52.9 us -> 16.3 us  [local(): lax.all_to_all(combined, 'expert', split_axis=0, concat_axis=0, tiled=True)]
    ppermute x2, waiting for transfers between devices: 0.01 us -> 26.9 us  [passed_along(): return lax.ppermute(value, axis, pairs)]
    ppermute x0 -> x2, starting transfers between devices: none -> 5.35 us  [core_swap(): return lax.ppermute(value, axis, pairs)]
  transfers between devices with their start and end apart: 7 -> 6, of which waited for: 5 -> 5; matrix products, arithmetic and copies ran while one was open for 6% -> 5% of each run, Pallas kernels for 0% -> 0%
where the time goes in v1:
time: 340 us; the launch traced here: 339 us
  waiting for transfers between devices  139 us (41%)
  blocking collectives  108 us (32%)
  starting transfers between devices  28.7 us (8%)
  local copies, waits for them, and re-layouts  22.3 us (7%)
  matrix products  14.7 us (4%)
  between operations  14.5 us (4%)
  other arithmetic  12.1 us (4%)
    all_to_all x1, blocking collectives, local(): lax.all_to_all(dispatch, 'expert', split_axis=0, concat_axis=0, tiled=True)  108 us
    psum x1, waiting for transfers between devices, local(): lax.psum(grad_part.astype(jnp.bfloat16), 'dp').astype(jnp.float32)  59.7 us
    all_to_all x1, waiting for transfers between devices, local(): lax.all_to_all(combined, 'expert', split_axis=0, concat_axis=0, tiled=True)  50.4 us
    ppermute x2, waiting for transfers between devices, passed_along(): return lax.ppermute(value, axis, pairs)  26.9 us
    all_to_all x1, starting transfers between devices, local(): lax.all_to_all(combined, 'expert', split_axis=0, concat_axis=0, tiled=True)  16.3 us
    ppermute x2, starting transfers between devices, passed_along(): return lax.ppermute(value, axis, pairs)  6.97 us
  transfers between devices with their start and end apart: 6, of which 5 were waited for; matrix products, arithmetic and copies ran while one was open for 5% of the time, Pallas kernels for 0%

profile of v1, /device:TPU:1, one launch (start us, length us, event | category | flops | bytes accessed | tf_op | source)
XLA Modules:
  0.0 339.1 jit_solution(4798310997403195365)
XLA Ops:
  7.2 0.8 copy.69
  9.4 0.8 fusion.25
  10.2 0.8 copy.73
  11.4 1.2 mul.61
  13.2 1.9 gather_fusion
  15.1 1.9 scatter_custom_fusion.1
  17.7 1.9 scatter_custom_fusion
  20.5 108.0 %all_to_all.10 = bf16[128,6,896]{2,1,0:T(8,128)(2,1)S(1)} all-to-all(bf16[128,6,896]{2,1,0:T(8,128)(2,1)S(1)} %bitcast.28), channel_id=1, replica_groups=mesh['expert'=128,'dp'=4] {'expert'}, dimensions={0} | all-to-all | bytes 2752512 | tf_op jit(solution)/shard_map/all_to_all | solution.py:72
  128.5 1.3 copy.76
  129.8 2.7 collective-permute-start
  132.5 4.7 %collective-permute-start.2 = (bf16[896,512]{1,0:T(8,128)(2,1)}, bf16[896,512]{1,0:T(8,128)(2,1)}, u32[]{:S(2)}, u32[]{:S(2)}) collective-permute-start(bf16[896,512]{1,0:T(8,128)(2,1)} %param.12), channel_id=1, source_target_pairs={{0,256},{4,260},{8,264},{12,268},{16,272},{20,276},{24,280},{28,28... | collective-permute-start | bytes 2752520 | tf_op jit(solution)/shard_map/ppermute | solution.py:10
  137.2 2.2 collective-permute-start.1
  140.1 2.8 copy_select_fusion
  142.9 2.6 reshape.168
  145.5 1.5 reshape.167
  147.0 11.1 %collective-permute-done.2 = bf16[896,512]{1,0:T(8,128)(2,1)} collective-permute-done((bf16[896,512]{1,0:T(8,128)(2,1)}, bf16[896,512]{1,0:T(8,128)(2,1)}, u32[]{:S(2)}, u32[]{:S(2)}) %collective-permute-start.2) | collective-permute-done | bytes 917536 | tf_op jit(solution)/shard_map/ppermute | solution.py:10
  158.1 3.8 %convolution_convert_fusion.3 = bf16[768,512]{1,0:T(8,128)(2,1)} fusion(bf16[768,896]{1,0:T(8,128)(2,1)S(1)} %reshape.168, bf16[896,512]{1,0:T(8,128)(2,1)} %collective-permute-done.2, bf16[896,512]{1,0:T(8,128)(2,1)} %param.12, pred[]{:T(512)} %bitcast.6), kind=kOutput, calls=%fused_computation.26 | convolution fusion | flops 705495040 | bytes 3997697 | tf_op jit(solution)/shard_map/dot_general | solution.py:77
  161.9 15.8 %collective-permute-done.1 = bf16[896,512]{1,0:T(8,128)(2,1)} collective-permute-done((bf16[896,512]{1,0:T(8,128)(2,1)}, bf16[896,512]{1,0:T(8,128)(2,1)}, u32[]{:S(2)}, u32[]{:S(2)}) %collective-permute-start.1) | collective-permute-done | bytes 917536 | tf_op jit(solution)/shard_map/ppermute | solution.py:10
  177.8 3.7 %convolution_convert_fusion.4 = bf16[768,512]{1,0:T(8,128)(2,1)} fusion(bf16[768,896]{1,0:T(8,128)(2,1)S(1)} %copy-done.3, bf16[896,512]{1,0:T(8,128)(2,1)} %collective-permute-done.1, bf16[896,512]{1,0:T(8,128)(2,1)} %param.13, pred[]{:T(512)} %bitcast.6), kind=kOutput, calls=%fused_computation.27 | convolution fusion | flops 705495040 | bytes 3997697 | tf_op jit(solution)/shard_map/dot_general | solution.py:78
  181.5 59.7 %all-reduce.3.cloned.1.call-done = (bf16[768,512]{1,0:T(8,128)(2,1)}, bf16[768,512]{1,0:T(8,128)(2,1)}) async-done(((bf16[768,512]{1,0:T(8,128)(2,1)}, bf16[768,512]{1,0:T(8,128)(2,1)}), (bf16[768,512]{1,0:T(8,128)(2,1)}, bf16[768,512]{1,0:T(8,128)(2,1)})) %all-reduce.3.cloned.1.call-update) | async-done | bytes 1572880 | tf_op jit(solution)/shard_map/psum | solution.py:81
  241.2 2.0 fusion.2
  243.3 3.2 convolution_convert_fusion
  247.8 2.7 collective-permute-start.3
  250.5 1.9 collective-permute-done.3
  252.7 1.7 copy.81
  254.4 16.3 %all-to-all-start.1 = ((bf16[128,3,1024]{2,1,0:T(4,128)(2,1)}), bf16[128,3,1024]{2,1,0:T(4,128)(2,1)S(1)}, u32[]{:S(2)}, u32[]{:S(2)}) async-start(bf16[128,3,1024]{2,1,0:T(4,128)(2,1)} %copy.81), calls=%async_computation.1 | async-start | bytes 2097152 | tf_op jit(solution)/shard_map/all_to_all | solution.py:109
  270.7 1.9 convolution_convert_fusion.1
  272.7 2.0 convolution_convert_fusion.2
  274.7 50.4 %all-to-all-done.1 = bf16[128,3,1024]{2,1,0:T(4,128)(2,1)S(1)} async-done(((bf16[128,3,1024]{2,1,0:T(4,128)(2,1)}), bf16[128,3,1024]{2,1,0:T(4,128)(2,1)S(1)}, u32[]{:S(2)}, u32[]{:S(2)}) %all-to-all-start.1) | async-done | bytes 786464 | tf_op jit(solution)/shard_map/all_to_all | solution.py:109
  325.1 0.6 reshape.170
  326.2 2.7 gather_fusion.1
  330.3 1.9 reduce
  (63 shorter events, 8.0 us)
Async XLA Ops:
  7.2 234.0 %all-reduce.3.cloned.1.call-start = ((), (), s32[]{:S(2)}) async-start(), calls=%async_computation.2 | async-start | bytes 3145728 | tf_op jit(solution)/shard_map/psum | solution.py:81
  15.1 2.2 copy-start.9
  129.8 10.3 %collective-permute-start = (bf16[128,6,896]{2,0,1:T(8,128)(2,1)}, bf16[128,6,896]{2,0,1:T(8,128)(2,1)S(1)}, u32[]{:S(2)}, u32[]{:S(2)}) collective-permute-start(bf16[128,6,896]{2,0,1:T(8,128)(2,1)} %copy.76), channel_id=1, source_target_pairs={{0,4},{4,0},{8,12},{12,8},{16,20},{20,16},{24,28},{28,24},{32,36},... | collective-permute-start | bytes 4128776 | tf_op jit(solution)/shard_map/ppermute | solution.py:16
  132.5 25.6 %collective-permute-start.2 = (bf16[896,512]{1,0:T(8,128)(2,1)}, bf16[896,512]{1,0:T(8,128)(2,1)}, u32[]{:S(2)}, u32[]{:S(2)}) collective-permute-start(bf16[896,512]{1,0:T(8,128)(2,1)} %param.12), channel_id=1, source_target_pairs={{0,256},{4,260},{8,264},{12,268},{16,272},{20,276},{24,280},{28,28... | collective-permute-start | bytes 2752520 | tf_op jit(solution)/shard_map/ppermute | solution.py:10
  137.2 40.5 %collective-permute-start.1 = (bf16[896,512]{1,0:T(8,128)(2,1)}, bf16[896,512]{1,0:T(8,128)(2,1)}, u32[]{:S(2)}, u32[]{:S(2)}) collective-permute-start(bf16[896,512]{1,0:T(8,128)(2,1)} %param.13), channel_id=1, source_target_pairs={{0,256},{4,260},{8,264},{12,268},{16,272},{20,276},{24,280},{28,28... | collective-permute-start | bytes 2752520 | tf_op jit(solution)/shard_map/ppermute | solution.py:10
  142.9 2.6 copy-start
  145.5 12.6 %copy-start.1 = (bf16[768,896]{1,0:T(8,128)(2,1)}, bf16[768,896]{1,0:T(8,128)(2,1)S(1)}, u32[]{:S(2)}) copy-start(bf16[768,896]{1,0:T(8,128)(2,1)S(1)} %reshape.168) | copy-start | bytes 4128772
  158.1 19.7 %copy-start.3 = (bf16[768,896]{1,0:T(8,128)(2,1)S(1)}, bf16[768,896]{1,0:T(8,128)(2,1)}, u32[]{:S(2)}) copy-start(bf16[768,896]{1,0:T(8,128)(2,1)} %reshape.167) | copy-start | bytes 4128772
  241.2 2.0 copy-start.5
  241.2 2.0 copy-start.7
  247.8 4.6 %collective-permute-start.3 = (bf16[128,3,1024]{2,0,1:T(8,128)(2,1)S(1)}, bf16[128,3,1024]{2,0,1:T(8,128)(2,1)S(1)}, u32[]{:S(2)}, u32[]{:S(2)}) collective-permute-start(bf16[128,3,1024]{2,0,1:T(8,128)(2,1)S(1)} %broadcast_select_fusion.1), channel_id=1, source_target_pairs={{0,4},{4,0},{8,12},{12,8},{16,20},{20,16},{24,28},{28,24},{32,36},... | collective-permute-start | bytes 2359304 | tf_op jit(solution)/shard_map/ppermute | solution.py:16
  252.7 18.0 %copy-start.4 = (bf16[768,896]{1,0:T(8,128)(2,1)S(1)}, bf16[768,896]{1,0:T(8,128)(2,1)}, u32[]{:S(2)}) copy-start(bf16[768,896]{1,0:T(8,128)(2,1)} %reshape.167) | copy-start | bytes 4128772
  252.7 18.0 %copy-start.8 = (bf16[768,512]{1,0:T(8,128)(2,1)S(1)}, bf16[768,512]{1,0:T(8,128)(2,1)}, u32[]{:S(2)}) copy-start(bf16[768,512]{1,0:T(8,128)(2,1)} %get-tuple-element.29) | copy-start | bytes 2359300
  254.4 70.7 %all-to-all-start.1 = ((bf16[128,3,1024]{2,1,0:T(4,128)(2,1)}), bf16[128,3,1024]{2,1,0:T(4,128)(2,1)S(1)}, u32[]{:S(2)}, u32[]{:S(2)}) async-start(bf16[128,3,1024]{2,1,0:T(4,128)(2,1)} %copy.81), calls=%async_computation.1 | async-start | bytes 2097152 | tf_op jit(solution)/shard_map/all_to_all | solution.py:109
  270.7 2.0 copy-start.2
  270.7 2.0 copy-start.6
Sparse Core Ops, SparseCore 0:
  181.6 59.5 all-reduce.2

commit v2 on v1

--- a/solution.py
+++ b/solution.py
@@ -14,6 +14,27 @@
     count = lax.axis_size(axis)
     pairs = [(source, source ^ 1) for source in range(count)]
     return lax.ppermute(value, axis, pairs)
+
+
+def dp_sum(part, axis):
+    count = lax.axis_size(axis)
+    here = lax.axis_index(axis)
+    rows = part.shape[0] // count
+    blocks = part.reshape(count, rows, part.shape[1])
+    total = blocks[here].astype(jnp.float32)
+    for step in range(1, count):
+        pairs = [(source, (source + step) % count) for source in range(count)]
+        total = total + lax.ppermute(blocks[(here + step) % count], axis, pairs).astype(
+            jnp.float32
+        )
+    reduced = total.astype(jnp.bfloat16)
+    gathered = [reduced]
+    for step in range(1, count):
+        pairs = [(source, (source + step) % count) for source in range(count)]
+        gathered.append(lax.ppermute(reduced, axis, pairs))
+    stacked = jnp.stack(gathered)
+    order = (here - jnp.arange(count)) % count
+    return stacked[order].reshape(part.shape)
 
 
 def pick_pair(swapped_here, theirs, ours):
@@ -33,7 +54,7 @@
     return (hidden, pairing_part, grad_pre)
 
 
-def local(tokens, routes, logits, cotangent, pair_flags, w_up, w_down):
+def layer(tokens, routes, logits, cotangent, pair_flags, w_up, w_down):
     devices_ex = lax.axis_size("expert")
     experts = devices_ex // 2
     half_way = experts // 2
@@ -76,10 +97,12 @@
     up_block, down_block = resident
     up_part = jnp.dot(routed_rows, up_block, preferred_element_type=jnp.float32)
     grad_part = jnp.dot(scaled_rows, down_block, preferred_element_type=jnp.float32)
-    up_pre, grad_hidden = (
-        lax.psum(up_part.astype(jnp.bfloat16), "dp").astype(jnp.float32),
-        lax.psum(grad_part.astype(jnp.bfloat16), "dp").astype(jnp.float32),
+    width = up_part.shape[1]
+    both = jnp.concatenate(
+        [up_part.astype(jnp.bfloat16), grad_part.astype(jnp.bfloat16)], axis=1
     )
+    summed = dp_sum(both, "dp").astype(jnp.float32)
+    up_pre, grad_hidden = summed[:, :width], summed[:, width:]
     hidden, pairing_part, grad_pre = activate(up_pre, grad_hidden)
     pairing_half = pairing_part.astype(jnp.bfloat16)
     route_half = jnp.einsum(
@@ -132,4 +155,4 @@
         P("dp", "expert"),
     )
     out_specs = (P("expert", "dp"), P("expert", None), P("dp", "expert"), P("dp", "expert"))
-    return jax.shard_map(local, mesh=mesh, in_specs=in_specs, out_specs=out_specs, check_vma=False)
+    return jax.shard_map(layer, mesh=mesh, in_specs=in_specs, out_specs=out_specs, check_vma=False)

time: 340 us -> 313 us (0.921)
  waiting for transfers between devices: 139 us -> 106 us
  starting transfers between devices: 28.7 us -> 43.6 us
  between operations: 14.5 us -> 1.22 us
  local copies, waits for them, and re-layouts: 22.3 us -> 26.3 us
    psum x1 -> x0, waiting for transfers between devices: 59.7 us -> none  [local(): lax.psum(grad_part.astype(jnp.bfloat16), 'dp').astype(jnp.float32)]
    ppermute x0 -> x6, waiting for transfers between devices: none -> 26.7 us  [the longest x3 13.4 us: dp_sum(): lax.ppermute(blocks[(here + step) % count], axis, pairs).astype(jnp.float32)]
    ppermute x0 -> x6, starting transfers between devices: none -> 22.2 us  [the longest x3 11.5 us: dp_sum(): gathered.append(lax.ppermute(reduced, axis, pairs))]
    all_to_all x1, starting transfers between devices: 16.3 us -> 8.33 us  [layer(): lax.all_to_all(combined, 'expert', split_axis=0, concat_axis=0, tiled=True)]
  transfers between devices with their start and end apart: 6 -> 11, of which waited for: 5 -> 10; matrix products, arithmetic and copies ran while one was open for 5% -> 5% of each run, Pallas kernels for 0% -> 0%
where the time goes in v2:
time: 313 us; the launch traced here: 311 us
  blocking collectives  108 us (35%)
  waiting for transfers between devices  106 us (34%)
  starting transfers between devices  43.6 us (14%)
  local copies, waits for them, and re-layouts  26.3 us (8%)
  other arithmetic  13.1 us (4%)
  matrix products  12.6 us (4%)
    all_to_all x1, blocking collectives, layer(): lax.all_to_all(dispatch, 'expert', split_axis=0, concat_axis=0, tiled=True)  108 us
    all_to_all x1, waiting for transfers between devices, layer(): lax.all_to_all(combined, 'expert', split_axis=0, concat_axis=0, tiled=True)  49.8 us
    ppermute x2, waiting for transfers between devices, passed_along(): return lax.ppermute(value, axis, pairs)  27.6 us
    ppermute x3, waiting for transfers between devices, dp_sum(): lax.ppermute(blocks[(here + step) % count], axis, pairs).astype(jnp.float32)  13.4 us
    ppermute x3, waiting for transfers between devices, dp_sum(): gathered.append(lax.ppermute(reduced, axis, pairs))  13.3 us
    ppermute x3, starting transfers between devices, dp_sum(): gathered.append(lax.ppermute(reduced, axis, pairs))  11.5 us
    ppermute x3, starting transfers between devices, dp_sum(): lax.ppermute(blocks[(here + step) % count], axis, pairs).astype(jnp.float32)  10.7 us
    all_to_all x1, starting transfers between devices, layer(): lax.all_to_all(combined, 'expert', split_axis=0, concat_axis=0, tiled=True)  8.33 us
  transfers between devices with their start and end apart: 11, of which 10 were waited for; matrix products, arithmetic and copies ran while one was open for 5% of the time, Pallas kernels for 0%

profile of v2, /device:TPU:1, one launch (start us, length us, event | category | flops | bytes accessed | tf_op | source)
XLA Modules:
  0.0 311.0 jit_solution(17967290661213537272)
XLA Ops:
  6.6 1.9 gather_fusion
  8.5 1.9 scatter_custom_fusion.1
  11.1 1.9 scatter_custom_fusion
  13.9 108.0 %all_to_all.10 = bf16[128,6,896]{2,1,0:T(8,128)(2,1)S(1)} all-to-all(bf16[128,6,896]{2,1,0:T(8,128)(2,1)S(1)} %bitcast.49), channel_id=1, replica_groups=mesh['expert'=128,'dp'=4] {'expert'}, dimensions={0} | all-to-all | bytes 2752512 | tf_op jit(solution)/shard_map/all_to_all | solution.py:93
  123.2 2.7 collective-permute-start
  125.9 4.7 %collective-permute-start.1 = (bf16[896,512]{1,0:T(8,128)(2,1)}, bf16[896,512]{1,0:T(8,128)(2,1)}, u32[]{:S(2)}, u32[]{:S(2)}) collective-permute-start(bf16[896,512]{1,0:T(8,128)(2,1)} %param.12), channel_id=1, source_target_pairs={{0,256},{4,260},{8,264},{12,268},{16,272},{20,276},{24,280},{28,28... | collective-permute-start | bytes 2752520 | tf_op jit(solution)/shard_map/ppermute | solution.py:10
  130.7 2.2 collective-permute-start.2
  133.5 2.8 copy_select_fusion.1
  136.3 2.6 reshape.224
  140.5 11.0 %collective-permute-done.1 = bf16[896,512]{1,0:T(8,128)(2,1)} collective-permute-done((bf16[896,512]{1,0:T(8,128)(2,1)}, bf16[896,512]{1,0:T(8,128)(2,1)}, u32[]{:S(2)}, u32[]{:S(2)}) %collective-permute-start.1) | collective-permute-done | bytes 917536 | tf_op jit(solution)/shard_map/ppermute | solution.py:10
  151.5 3.1 convolution_convert_fusion.4
  154.6 16.6 %collective-permute-done.2 = bf16[896,512]{1,0:T(8,128)(2,1)} collective-permute-done((bf16[896,512]{1,0:T(8,128)(2,1)}, bf16[896,512]{1,0:T(8,128)(2,1)}, u32[]{:S(2)}, u32[]{:S(2)}) %collective-permute-start.2) | collective-permute-done | bytes 917536 | tf_op jit(solution)/shard_map/ppermute | solution.py:10
  171.2 3.0 convolution_convert_fusion.3
  175.1 3.2 %collective-permute-start.3 = (bf16[192,1024]{1,0:T(8,128)(2,1)S(1)}, bf16[192,1024]{1,0:T(8,128)(2,1)S(1)}, u32[]{:S(2)}, u32[]{:S(2)}) collective-permute-start(bf16[192,1024]{1,0:T(8,128)(2,1)S(1)} %get-tuple-element.34), channel_id=1, source_target_pairs={{0,1},{1,2},{2,3},{3,0},{4,5},{5,6},{6,7},{7,4},{8,9},{9,10},{10,1... | collective-permute-start | bytes 1179656 | tf_op jit(solution)/shard_map/ppermute | solution.py:27
  178.3 4.5 %collective-permute-start.4 = (bf16[192,1024]{1,0:T(8,128)(2,1)S(1)}, bf16[192,1024]{1,0:T(8,128)(2,1)}, u32[]{:S(2)}, u32[]{:S(2)}) collective-permute-start(bf16[192,1024]{1,0:T(8,128)(2,1)S(1)} %get-tuple-element.36), channel_id=1, source_target_pairs={{0,2},{1,3},{2,0},{3,1},{4,6},{5,7},{6,4},{7,5},{8,10},{9,11},{10,... | collective-permute-start | bytes 1179656 | tf_op jit(solution)/shard_map/ppermute | solution.py:27
  182.9 3.0 collective-permute-start.5
  185.9 2.3 collective-permute-done.3
  188.2 9.6 %collective-permute-done.4 = bf16[192,1024]{1,0:T(8,128)(2,1)} collective-permute-done((bf16[192,1024]{1,0:T(8,128)(2,1)S(1)}, bf16[192,1024]{1,0:T(8,128)(2,1)}, u32[]{:S(2)}, u32[]{:S(2)}) %collective-permute-start.4) | collective-permute-done | bytes 393248 | tf_op jit(solution)/shard_map/ppermute | solution.py:27
  200.6 5.3 %collective-permute-start.6 = (bf16[192,1024]{1,0:T(8,128)(2,1)S(1)}, bf16[192,1024]{1,0:T(8,128)(2,1)S(1)}, u32[]{:S(2)}, u32[]{:S(2)}) collective-permute-start(bf16[192,1024]{1,0:T(8,128)(2,1)S(1)} %fusion.5), channel_id=1, source_target_pairs={{0,1},{1,2},{2,3},{3,0},{4,5},{5,6},{6,7},{7,4},{8,9},{9,10},{10,1... | collective-permute-start | bytes 1179656 | tf_op jit(solution)/shard_map/ppermute | solution.py:34
  205.9 3.2 %collective-permute-start.7 = (bf16[192,1024]{1,0:T(8,128)(2,1)S(1)}, bf16[192,1024]{1,0:T(8,128)(2,1)S(1)}, u32[]{:S(2)}, u32[]{:S(2)}) collective-permute-start(bf16[192,1024]{1,0:T(8,128)(2,1)S(1)} %fusion.5), channel_id=1, source_target_pairs={{0,2},{1,3},{2,0},{3,1},{4,6},{5,7},{6,4},{7,5},{8,10},{9,11},{10,... | collective-permute-start | bytes 1179656 | tf_op jit(solution)/shard_map/ppermute | solution.py:34
  209.2 3.0 collective-permute-start.8
  212.2 2.2 collective-permute-done.6
  214.5 9.9 %collective-permute-done.7 = bf16[192,1024]{1,0:T(8,128)(2,1)S(1)} collective-permute-done((bf16[192,1024]{1,0:T(8,128)(2,1)S(1)}, bf16[192,1024]{1,0:T(8,128)(2,1)S(1)}, u32[]{:S(2)}, u32[]{:S(2)}) %collective-permute-start.7) | collective-permute-done | bytes 393248 | tf_op jit(solution)/shard_map/ppermute | solution.py:34
  229.4 2.9 convolution_convert_fusion
  233.7 3.5 %collective-permute-start.9 = (bf16[128,3,1024]{2,0,1:T(8,128)(2,1)S(1)}, bf16[128,3,1024]{2,0,1:T(8,128)(2,1)S(1)}, u32[]{:S(2)}, u32[]{:S(2)}) collective-permute-start(bf16[128,3,1024]{2,0,1:T(8,128)(2,1)S(1)} %broadcast_select_fusion.1), channel_id=1, source_target_pairs={{0,4},{4,0},{8,12},{12,8},{16,20},{20,16},{24,28},{28,24},{32,36},... | collective-permute-start | bytes 2359304 | tf_op jit(solution)/shard_map/ppermute | solution.py:16
  237.1 1.9 collective-permute-done.9
  241.0 8.3 %all-to-all-start.1 = ((bf16[128,3,1024]{2,1,0:T(4,128)(2,1)}), bf16[128,3,1024]{2,1,0:T(4,128)(2,1)S(1)}, u32[]{:S(2)}, u32[]{:S(2)}) async-start(bf16[128,3,1024]{2,1,0:T(4,128)(2,1)} %copy.87), calls=%async_computation.1 | async-start | bytes 2097152 | tf_op jit(solution)/shard_map/all_to_all | solution.py:132
  249.4 1.8 convolution_convert_fusion.2
  252.0 1.9 convolution_convert_fusion.1
  253.9 49.8 %all-to-all-done.1 = bf16[128,3,1024]{2,1,0:T(4,128)(2,1)S(1)} async-done(((bf16[128,3,1024]{2,1,0:T(4,128)(2,1)}), bf16[128,3,1024]{2,1,0:T(4,128)(2,1)S(1)}, u32[]{:S(2)}, u32[]{:S(2)}) %all-to-all-start.1) | async-done | bytes 786464 | tf_op jit(solution)/shard_map/all_to_all | solution.py:132
  304.9 2.7 gather_fusion.2
  309.0 1.9 reduce
  (81 shorter events, 26.3 us)
Async XLA Ops:
  8.5 2.2 copy-start.9
  123.2 10.3 %collective-permute-start = (bf16[128,6,896]{2,0,1:T(8,128)(2,1)}, bf16[128,6,896]{2,0,1:T(8,128)(2,1)S(1)}, u32[]{:S(2)}, u32[]{:S(2)}) collective-permute-start(bf16[128,6,896]{2,0,1:T(8,128)(2,1)} %copy.81), channel_id=1, source_target_pairs={{0,4},{4,0},{8,12},{12,8},{16,20},{20,16},{24,28},{28,24},{32,36},... | collective-permute-start | bytes 4128776 | tf_op jit(solution)/shard_map/ppermute | solution.py:16
  125.9 25.6 %collective-permute-start.1 = (bf16[896,512]{1,0:T(8,128)(2,1)}, bf16[896,512]{1,0:T(8,128)(2,1)}, u32[]{:S(2)}, u32[]{:S(2)}) collective-permute-start(bf16[896,512]{1,0:T(8,128)(2,1)} %param.12), channel_id=1, source_target_pairs={{0,256},{4,260},{8,264},{12,268},{16,272},{20,276},{24,280},{28,28... | collective-permute-start | bytes 2752520 | tf_op jit(solution)/shard_map/ppermute | solution.py:10
  130.7 40.5 %collective-permute-start.2 = (bf16[896,512]{1,0:T(8,128)(2,1)}, bf16[896,512]{1,0:T(8,128)(2,1)}, u32[]{:S(2)}, u32[]{:S(2)}) collective-permute-start(bf16[896,512]{1,0:T(8,128)(2,1)} %param.13), channel_id=1, source_target_pairs={{0,256},{4,260},{8,264},{12,268},{16,272},{20,276},{24,280},{28,28... | collective-permute-start | bytes 2752520 | tf_op jit(solution)/shard_map/ppermute | solution.py:10
  136.3 2.6 copy-start.2
  138.9 12.6 %copy-start.3 = (bf16[768,896]{1,0:T(8,128)(2,1)}, bf16[768,896]{1,0:T(8,128)(2,1)S(1)}, u32[]{:S(2)}) copy-start(bf16[768,896]{1,0:T(8,128)(2,1)S(1)} %reshape.224) | copy-start | bytes 4128772
  151.5 19.7 %copy-start.5 = (bf16[768,896]{1,0:T(8,128)(2,1)S(1)}, bf16[768,896]{1,0:T(8,128)(2,1)}, u32[]{:S(2)}) copy-start(bf16[768,896]{1,0:T(8,128)(2,1)} %reshape.225) | copy-start | bytes 4128772
  175.1 13.0 %collective-permute-start.3 = (bf16[192,1024]{1,0:T(8,128)(2,1)S(1)}, bf16[192,1024]{1,0:T(8,128)(2,1)S(1)}, u32[]{:S(2)}, u32[]{:S(2)}) collective-permute-start(bf16[192,1024]{1,0:T(8,128)(2,1)S(1)} %get-tuple-element.34), channel_id=1, source_target_pairs={{0,1},{1,2},{2,3},{3,0},{4,5},{5,6},{6,7},{7,4},{8,9},{9,10},{10,1... | collective-permute-start | bytes 1179656 | tf_op jit(solution)/shard_map/ppermute | solution.py:27
  178.3 19.5 %collective-permute-start.4 = (bf16[192,1024]{1,0:T(8,128)(2,1)S(1)}, bf16[192,1024]{1,0:T(8,128)(2,1)}, u32[]{:S(2)}, u32[]{:S(2)}) collective-permute-start(bf16[192,1024]{1,0:T(8,128)(2,1)S(1)} %get-tuple-element.36), channel_id=1, source_target_pairs={{0,2},{1,3},{2,0},{3,1},{4,6},{5,7},{6,4},{7,5},{8,10},{9,11},{10,... | collective-permute-start | bytes 1179656 | tf_op jit(solution)/shard_map/ppermute | solution.py:27
  182.9 16.4 %collective-permute-start.5 = (bf16[192,1024]{1,0:T(8,128)(2,1)S(1)}, bf16[192,1024]{1,0:T(8,128)(2,1)}, u32[]{:S(2)}, u32[]{:S(2)}) collective-permute-start(bf16[192,1024]{1,0:T(8,128)(2,1)S(1)} %get-tuple-element.35), channel_id=1, source_target_pairs={{0,3},{1,0},{2,1},{3,2},{4,7},{5,4},{6,5},{7,6},{8,11},{9,8},{10,9... | collective-permute-start | bytes 1179656 | tf_op jit(solution)/shard_map/ppermute | solution.py:27
  200.6 13.8 %collective-permute-start.6 = (bf16[192,1024]{1,0:T(8,128)(2,1)S(1)}, bf16[192,1024]{1,0:T(8,128)(2,1)S(1)}, u32[]{:S(2)}, u32[]{:S(2)}) collective-permute-start(bf16[192,1024]{1,0:T(8,128)(2,1)S(1)} %fusion.5), channel_id=1, source_target_pairs={{0,1},{1,2},{2,3},{3,0},{4,5},{5,6},{6,7},{7,4},{8,9},{9,10},{10,1... | collective-permute-start | bytes 1179656 | tf_op jit(solution)/shard_map/ppermute | solution.py:34
  205.9 18.5 %collective-permute-start.7 = (bf16[192,1024]{1,0:T(8,128)(2,1)S(1)}, bf16[192,1024]{1,0:T(8,128)(2,1)S(1)}, u32[]{:S(2)}, u32[]{:S(2)}) collective-permute-start(bf16[192,1024]{1,0:T(8,128)(2,1)S(1)} %fusion.5), channel_id=1, source_target_pairs={{0,2},{1,3},{2,0},{3,1},{4,6},{5,7},{6,4},{7,5},{8,10},{9,11},{10,... | collective-permute-start | bytes 1179656 | tf_op jit(solution)/shard_map/ppermute | solution.py:34
  209.2 16.4 %collective-permute-start.8 = (bf16[192,1024]{1,0:T(8,128)(2,1)S(1)}, bf16[192,1024]{1,0:T(8,128)(2,1)S(1)}, u32[]{:S(2)}, u32[]{:S(2)}) collective-permute-start(bf16[192,1024]{1,0:T(8,128)(2,1)S(1)} %fusion.5), channel_id=1, source_target_pairs={{0,3},{1,0},{2,1},{3,2},{4,7},{5,4},{6,5},{7,6},{8,11},{9,8},{10,9... | collective-permute-start | bytes 1179656 | tf_op jit(solution)/shard_map/ppermute | solution.py:34
  226.9 1.7 copy-start
  228.6 0.9 copy-start.7
  233.7 5.4 %collective-permute-start.9 = (bf16[128,3,1024]{2,0,1:T(8,128)(2,1)S(1)}, bf16[128,3,1024]{2,0,1:T(8,128)(2,1)S(1)}, u32[]{:S(2)}, u32[]{:S(2)}) collective-permute-start(bf16[128,3,1024]{2,0,1:T(8,128)(2,1)S(1)} %broadcast_select_fusion.1), channel_id=1, source_target_pairs={{0,4},{4,0},{8,12},{12,8},{16,20},{20,16},{24,28},{28,24},{32,36},... | collective-permute-start | bytes 2359304 | tf_op jit(solution)/shard_map/ppermute | solution.py:16
  239.3 10.0 %copy-start.4 = (bf16[768,896]{1,0:T(8,128)(2,1)S(1)}, bf16[768,896]{1,0:T(8,128)(2,1)}, u32[]{:S(2)}) copy-start(bf16[768,896]{1,0:T(8,128)(2,1)} %copy-done.3) | copy-start | bytes 4128772
  239.3 10.0 %copy-start.8 = (bf16[768,512]{1,0:T(8,128)(2,1)S(1)}, bf16[768,512]{1,0:T(8,128)(2,1)}, u32[]{:S(2)}) copy-start(bf16[768,512]{1,0:T(8,128)(2,1)} %copy-done.7) | copy-start | bytes 2359300
  241.0 62.7 %all-to-all-start.1 = ((bf16[128,3,1024]{2,1,0:T(4,128)(2,1)}), bf16[128,3,1024]{2,1,0:T(4,128)(2,1)S(1)}, u32[]{:S(2)}, u32[]{:S(2)}) async-start(bf16[128,3,1024]{2,1,0:T(4,128)(2,1)} %copy.87), calls=%async_computation.1 | async-start | bytes 2097152 | tf_op jit(solution)/shard_map/all_to_all | solution.py:132
  249.4 1.9 copy-start.1
  249.4 2.6 copy-start.6

commit v3 on v2

--- a/solution.py
+++ b/solution.py
@@ -35,6 +35,11 @@
     stacked = jnp.stack(gathered)
     order = (here - jnp.arange(count)) % count
     return stacked[order].reshape(part.shape)
+
+
+def lane_rows(value):
+    count = value.shape[0]
+    return value.reshape(count, -1, 128)
 
 
 def pick_pair(swapped_here, theirs, ours):
@@ -90,7 +95,9 @@
     )
     scaled_buf = empty_rows.at[position].set(scaled).reshape(experts, capacity, quarter)
     dispatch = jnp.stack([token_buf, scaled_buf], axis=1).reshape(devices_ex, capacity, quarter)
-    got = lax.all_to_all(dispatch, "expert", split_axis=0, concat_axis=0, tiled=True)
+    got = lax.all_to_all(
+        lane_rows(dispatch), "expert", split_axis=0, concat_axis=0, tiled=True
+    ).reshape(devices_ex, capacity, quarter)
     partner_got = core_swap(got, "expert")
     routed_rows = jnp.where(first_core, got, partner_got).reshape(-1, quarter)
     scaled_rows = jnp.where(first_core, partner_got, got).reshape(-1, quarter)
@@ -129,7 +136,9 @@
     give = jnp.where(first_core, high, low)
     taken = core_swap(give, "expert")
     combined = (keep.astype(jnp.float32) + taken.astype(jnp.float32)).astype(jnp.bfloat16)
-    back = lax.all_to_all(combined, "expert", split_axis=0, concat_axis=0, tiled=True)
+    back = lax.all_to_all(
+        lane_rows(combined), "expert", split_axis=0, concat_axis=0, tiled=True
+    )
     back_grid = back.reshape(experts, capacity, quarter + lanes)
     picked = back_grid[target, slot_rank]
     grad_tokens = jnp.sum(

time: 313 us -> 293 us (0.936)
  waiting for transfers between devices: 106 us -> 92.1 us
  blocking collectives: 108 us -> 96.8 us
  local copies, waits for them, and re-layouts: 26.3 us -> 32 us
    all_to_all x1, blocking collectives: 108 us -> 96.8 us  [layer(): lax.all_to_all(lane_rows(dispatch), 'expert', split_axis=0, concat_axis=0...]
    all_to_all x1, waiting for transfers between devices: 49.8 us -> 38.9 us  [layer(): lax.all_to_all(lane_rows(combined), 'expert', split_axis=0, concat_axis=0...]
    select_n x0 -> x2, local copies, waits for them, and re-layouts: none -> 5.09 us  [the longest x1 3.08 us: layer(): routed_rows = jnp.where(first_core, got, partner_got).reshape(-1, quarter)]
  transfers between devices with their start and end apart: 11 -> 11, of which waited for: 10 -> 10; matrix products, arithmetic and copies ran while one was open for 5% -> 6% of each run, Pallas kernels for 0% -> 0%
where the time goes in v3:
time: 293 us; the launch traced here: 291 us
  blocking collectives  96.8 us (33%)
  waiting for transfers between devices  92.1 us (31%)
  starting transfers between devices  43.6 us (15%)
  local copies, waits for them, and re-layouts  32 us (11%)
  matrix products  12.7 us (4%)
  other arithmetic  12.1 us (4%)
    all_to_all x1, blocking collectives, layer(): lax.all_to_all(lane_rows(dispatch), 'expert', split_axis=0, concat_axis=0...  96.8 us
    all_to_all x1, waiting for transfers between devices, layer(): lax.all_to_all(lane_rows(combined), 'expert', split_axis=0, concat_axis=0...  38.9 us
    ppermute x2, waiting for transfers between devices, passed_along(): return lax.ppermute(value, axis, pairs)  24.6 us
    ppermute x3, waiting for transfers between devices, dp_sum(): lax.ppermute(blocks[(here + step) % count], axis, pairs).astype(jnp.float32)  13.4 us
    ppermute x3, waiting for transfers between devices, dp_sum(): gathered.append(lax.ppermute(reduced, axis, pairs))  13.3 us
    ppermute x3, starting transfers between devices, dp_sum(): gathered.append(lax.ppermute(reduced, axis, pairs))  11.5 us
    ppermute x3, starting transfers between devices, dp_sum(): lax.ppermute(blocks[(here + step) % count], axis, pairs).astype(jnp.float32)  10.7 us
    all_to_all x1, starting transfers between devices, layer(): lax.all_to_all(lane_rows(combined), 'expert', split_axis=0, concat_axis=0...  7.94 us
  transfers between devices with their start and end apart: 11, of which 10 were waited for; matrix products, arithmetic and copies ran while one was open for 6% of the time, Pallas kernels for 0%

profile of v3, /device:TPU:1, one launch (start us, length us, event | category | flops | bytes accessed | tf_op | source)
XLA Modules:
  0.0 290.6 jit_solution(6191484248709401539)
XLA Ops:
  6.6 1.9 gather_fusion
  8.5 1.9 scatter_custom_fusion.1
  11.1 1.9 scatter_custom_fusion
  15.3 96.8 %all_to_all.10 = bf16[128,42,128]{2,1,0:T(8,128)(2,1)S(1)} all-to-all(bf16[128,42,128]{2,1,0:T(8,128)(2,1)S(1)} %reshape_reshape.3), channel_id=1, replica_groups=mesh['expert'=128,'dp'=4] {'expert'}, dimensions={0} | all-to-all | bytes 2752512 | tf_op jit(solution)/shard_map/all_to_all | solution.py:98
  113.6 3.0 %collective-permute-start = (bf16[128,6,896]{0,2,1:T(8,128)(2,1)S(1)}, bf16[128,6,896]{0,2,1:T(8,128)(2,1)S(1)}, u32[]{:S(2)}, u32[]{:S(2)}) collective-permute-start(bf16[128,6,896]{0,2,1:T(8,128)(2,1)S(1)} %bitcast.55), channel_id=1, source_target_pairs={{0,4},{4,0},{8,12},{12,8},{16,20},{20,16},{24,28},{28,24},{32,36},... | collective-permute-start | bytes 4128776 | tf_op jit(solution)/shard_map/ppermute | solution.py:16
  116.6 4.7 %collective-permute-start.1 = (bf16[896,512]{1,0:T(8,128)(2,1)}, bf16[896,512]{1,0:T(8,128)(2,1)}, u32[]{:S(2)}, u32[]{:S(2)}) collective-permute-start(bf16[896,512]{1,0:T(8,128)(2,1)} %param.12), channel_id=1, source_target_pairs={{0,256},{4,260},{8,264},{12,268},{16,272},{20,276},{24,280},{28,28... | collective-permute-start | bytes 2752520 | tf_op jit(solution)/shard_map/ppermute | solution.py:10
  121.4 2.2 collective-permute-start.2
  126.0 3.1 %copy.49 = bf16[128,6,896]{2,1,0:T(8,128)(2,1)S(1)} copy(bf16[128,6,896]{0,2,1:T(8,128)(2,1)} %get-tuple-element.20) | data formatting | bytes 2752512 | tf_op jit(solution)/shard_map/jit(_where)/select_n | solution.py:102
  130.7 2.0 copy.50
  134.1 8.1 %collective-permute-done.1 = bf16[896,512]{1,0:T(8,128)(2,1)} collective-permute-done((bf16[896,512]{1,0:T(8,128)(2,1)}, bf16[896,512]{1,0:T(8,128)(2,1)}, u32[]{:S(2)}, u32[]{:S(2)}) %collective-permute-start.1) | collective-permute-done | bytes 917536 | tf_op jit(solution)/shard_map/ppermute | solution.py:10
  142.2 3.1 %convolution_convert_fusion.4 = bf16[768,512]{0,1:T(8,128)(2,1)S(1)} fusion(bf16[768,896]{1,0:T(8,128)(2,1)S(1)} %copy-done.3, bf16[896,512]{1,0:T(8,128)(2,1)} %collective-permute-done.1, bf16[896,512]{1,0:T(8,128)(2,1)} %param.12, pred[]{:T(512)} %bitcast.6), kind=kOutput, calls=%fused_computation.20 | convolution fusion | flops 705495040 | bytes 3997697 | tf_op jit(solution)/shard_map/dot_general | solution.py:105
  145.3 16.5 %collective-permute-done.2 = bf16[896,512]{1,0:T(8,128)(2,1)} collective-permute-done((bf16[896,512]{1,0:T(8,128)(2,1)}, bf16[896,512]{1,0:T(8,128)(2,1)}, u32[]{:S(2)}, u32[]{:S(2)}) %collective-permute-start.2) | collective-permute-done | bytes 917536 | tf_op jit(solution)/shard_map/ppermute | solution.py:10
  161.9 2.9 %convolution_convert_fusion.3 = bf16[768,512]{0,1:T(8,128)(2,1)S(1)} fusion(bf16[768,896]{1,0:T(8,128)(2,1)S(1)} %copy-done.5, bf16[896,512]{1,0:T(8,128)(2,1)} %collective-permute-done.2, bf16[896,512]{1,0:T(8,128)(2,1)S(1)} %copy-done.10, pred[]{:T(512)} %bitcast.6), kind=kOutput, calls=%fused_computation.19 | convolution fusion | flops 705495040 | bytes 3997697 | tf_op jit(solution)/shard_map/dot_general | solution.py:106
  165.8 3.2 %collective-permute-start.3 = (bf16[192,1024]{1,0:T(8,128)(2,1)S(1)}, bf16[192,1024]{1,0:T(8,128)(2,1)S(1)}, u32[]{:S(2)}, u32[]{:S(2)}) collective-permute-start(bf16[192,1024]{1,0:T(8,128)(2,1)S(1)} %get-tuple-element.22), channel_id=1, source_target_pairs={{0,1},{1,2},{2,3},{3,0},{4,5},{5,6},{6,7},{7,4},{8,9},{9,10},{10,1... | collective-permute-start | bytes 1179656 | tf_op jit(solution)/shard_map/ppermute | solution.py:27
  169.1 4.5 %collective-permute-start.4 = (bf16[192,1024]{1,0:T(8,128)(2,1)S(1)}, bf16[192,1024]{1,0:T(8,128)(2,1)}, u32[]{:S(2)}, u32[]{:S(2)}) collective-permute-start(bf16[192,1024]{1,0:T(8,128)(2,1)S(1)} %get-tuple-element.24), channel_id=1, source_target_pairs={{0,2},{1,3},{2,0},{3,1},{4,6},{5,7},{6,4},{7,5},{8,10},{9,11},{10,... | collective-permute-start | bytes 1179656 | tf_op jit(solution)/shard_map/ppermute | solution.py:27
  173.6 3.0 %collective-permute-start.5 = (bf16[192,1024]{1,0:T(8,128)(2,1)S(1)}, bf16[192,1024]{1,0:T(8,128)(2,1)}, u32[]{:S(2)}, u32[]{:S(2)}) collective-permute-start(bf16[192,1024]{1,0:T(8,128)(2,1)S(1)} %get-tuple-element.23), channel_id=1, source_target_pairs={{0,3},{1,0},{2,1},{3,2},{4,7},{5,4},{6,5},{7,6},{8,11},{9,8},{10,9... | collective-permute-start | bytes 1179656 | tf_op jit(solution)/shard_map/ppermute | solution.py:27
  176.6 2.3 collective-permute-done.3
  178.9 9.6 %collective-permute-done.4 = bf16[192,1024]{1,0:T(8,128)(2,1)} collective-permute-done((bf16[192,1024]{1,0:T(8,128)(2,1)S(1)}, bf16[192,1024]{1,0:T(8,128)(2,1)}, u32[]{:S(2)}, u32[]{:S(2)}) %collective-permute-start.4) | collective-permute-done | bytes 393248 | tf_op jit(solution)/shard_map/ppermute | solution.py:27
  191.4 5.3 %collective-permute-start.6 = (bf16[192,1024]{1,0:T(8,128)(2,1)S(1)}, bf16[192,1024]{1,0:T(8,128)(2,1)S(1)}, u32[]{:S(2)}, u32[]{:S(2)}) collective-permute-start(bf16[192,1024]{1,0:T(8,128)(2,1)S(1)} %fusion.5), channel_id=1, source_target_pairs={{0,1},{1,2},{2,3},{3,0},{4,5},{5,6},{6,7},{7,4},{8,9},{9,10},{10,1... | collective-permute-start | bytes 1179656 | tf_op jit(solution)/shard_map/ppermute | solution.py:34
  196.6 3.2 %collective-permute-start.7 = (bf16[192,1024]{1,0:T(8,128)(2,1)S(1)}, bf16[192,1024]{1,0:T(8,128)(2,1)S(1)}, u32[]{:S(2)}, u32[]{:S(2)}) collective-permute-start(bf16[192,1024]{1,0:T(8,128)(2,1)S(1)} %fusion.5), channel_id=1, source_target_pairs={{0,2},{1,3},{2,0},{3,1},{4,6},{5,7},{6,4},{7,5},{8,10},{9,11},{10,... | collective-permute-start | bytes 1179656 | tf_op jit(solution)/shard_map/ppermute | solution.py:34
  199.9 3.0 %collective-permute-start.8 = (bf16[192,1024]{1,0:T(8,128)(2,1)S(1)}, bf16[192,1024]{1,0:T(8,128)(2,1)S(1)}, u32[]{:S(2)}, u32[]{:S(2)}) collective-permute-start(bf16[192,1024]{1,0:T(8,128)(2,1)S(1)} %fusion.5), channel_id=1, source_target_pairs={{0,3},{1,0},{2,1},{3,2},{4,7},{5,4},{6,5},{7,6},{8,11},{9,8},{10,9... | collective-permute-start | bytes 1179656 | tf_op jit(solution)/shard_map/ppermute | solution.py:34
  202.9 2.2 collective-permute-done.6
  205.2 9.9 %collective-permute-done.7 = bf16[192,1024]{1,0:T(8,128)(2,1)S(1)} collective-permute-done((bf16[192,1024]{1,0:T(8,128)(2,1)S(1)}, bf16[192,1024]{1,0:T(8,128)(2,1)S(1)}, u32[]{:S(2)}, u32[]{:S(2)}) %collective-permute-start.7) | collective-permute-done | bytes 393248 | tf_op jit(solution)/shard_map/ppermute | solution.py:34
  220.2 2.9 convolution_convert_fusion
  224.4 3.5 %collective-permute-start.9 = (bf16[128,3,1024]{2,0,1:T(8,128)(2,1)S(1)}, bf16[128,3,1024]{2,0,1:T(8,128)(2,1)S(1)}, u32[]{:S(2)}, u32[]{:S(2)}) collective-permute-start(bf16[128,3,1024]{2,0,1:T(8,128)(2,1)S(1)} %broadcast_select_fusion.3), channel_id=1, source_target_pairs={{0,4},{4,0},{8,12},{12,8},{16,20},{20,16},{24,28},{28,24},{32,36},... | collective-permute-start | bytes 2359304 | tf_op jit(solution)/shard_map/ppermute | solution.py:16
  227.9 1.9 collective-permute-done.9
  231.8 7.9 %all-to-all-start.1 = ((bf16[128,24,128]{2,1,0:T(8,128)(2,1)}), bf16[128,24,128]{2,1,0:T(8,128)(2,1)S(1)}, u32[]{:S(2)}, u32[]{:S(2)}) async-start(bf16[128,24,128]{2,1,0:T(8,128)(2,1)} %copy.55), calls=%async_computation.1 | async-start | bytes 1572864 | tf_op jit(solution)/shard_map/all_to_all | solution.py:139
  239.8 1.8 convolution_convert_fusion.2
  242.4 1.9 convolution_convert_fusion.1
  244.3 38.9 %all-to-all-done.1 = bf16[128,24,128]{2,1,0:T(8,128)(2,1)S(1)} async-done(((bf16[128,24,128]{2,1,0:T(8,128)(2,1)}), bf16[128,24,128]{2,1,0:T(8,128)(2,1)S(1)}, u32[]{:S(2)}, u32[]{:S(2)}) %all-to-all-start.1) | async-done | bytes 786464 | tf_op jit(solution)/shard_map/all_to_all | solution.py:139
  284.5 2.7 gather_fusion.2
  288.7 1.9 reduce
  (89 shorter events, 31.3 us)
Async XLA Ops:
  8.5 2.2 copy-start.9
  113.6 10.7 %collective-permute-start = (bf16[128,6,896]{0,2,1:T(8,128)(2,1)S(1)}, bf16[128,6,896]{0,2,1:T(8,128)(2,1)S(1)}, u32[]{:S(2)}, u32[]{:S(2)}) collective-permute-start(bf16[128,6,896]{0,2,1:T(8,128)(2,1)S(1)} %bitcast.55), channel_id=1, source_target_pairs={{0,4},{4,0},{8,12},{12,8},{16,20},{20,16},{24,28},{28,24},{32,36},... | collective-permute-start | bytes 4128776 | tf_op jit(solution)/shard_map/ppermute | solution.py:16
  116.6 25.6 %collective-permute-start.1 = (bf16[896,512]{1,0:T(8,128)(2,1)}, bf16[896,512]{1,0:T(8,128)(2,1)}, u32[]{:S(2)}, u32[]{:S(2)}) collective-permute-start(bf16[896,512]{1,0:T(8,128)(2,1)} %param.12), channel_id=1, source_target_pairs={{0,256},{4,260},{8,264},{12,268},{16,272},{20,276},{24,280},{28,28... | collective-permute-start | bytes 2752520 | tf_op jit(solution)/shard_map/ppermute | solution.py:10
  121.4 40.5 %collective-permute-start.2 = (bf16[896,512]{1,0:T(8,128)(2,1)}, bf16[896,512]{1,0:T(8,128)(2,1)}, u32[]{:S(2)}, u32[]{:S(2)}) collective-permute-start(bf16[896,512]{1,0:T(8,128)(2,1)} %param.13), channel_id=1, source_target_pairs={{0,256},{4,260},{8,264},{12,268},{16,272},{20,276},{24,280},{28,28... | collective-permute-start | bytes 2752520 | tf_op jit(solution)/shard_map/ppermute | solution.py:10
  129.1 1.7 copy-start.2
  132.8 9.5 %copy-start.3 = (bf16[768,896]{1,0:T(8,128)(2,1)S(1)}, bf16[768,896]{1,0:T(8,128)(2,1)}, u32[]{:S(2)}) copy-start(bf16[768,896]{1,0:T(8,128)(2,1)} %reshape.227) | copy-start | bytes 4128772
  142.2 19.7 %copy-start.5 = (bf16[768,896]{1,0:T(8,128)(2,1)S(1)}, bf16[768,896]{1,0:T(8,128)(2,1)}, u32[]{:S(2)}) copy-start(bf16[768,896]{1,0:T(8,128)(2,1)} %reshape.228) | copy-start | bytes 4128772
  142.2 19.7 %copy-start.10 = (bf16[896,512]{1,0:T(8,128)(2,1)S(1)}, bf16[896,512]{1,0:T(8,128)(2,1)}, u32[]{:S(2)}) copy-start(bf16[896,512]{1,0:T(8,128)(2,1)} %param.13) | copy-start | bytes 2752516
  165.8 13.0 %collective-permute-start.3 = (bf16[192,1024]{1,0:T(8,128)(2,1)S(1)}, bf16[192,1024]{1,0:T(8,128)(2,1)S(1)}, u32[]{:S(2)}, u32[]{:S(2)}) collective-permute-start(bf16[192,1024]{1,0:T(8,128)(2,1)S(1)} %get-tuple-element.22), channel_id=1, source_target_pairs={{0,1},{1,2},{2,3},{3,0},{4,5},{5,6},{6,7},{7,4},{8,9},{9,10},{10,1... | collective-permute-start | bytes 1179656 | tf_op jit(solution)/shard_map/ppermute | solution.py:27
  169.1 19.5 %collective-permute-start.4 = (bf16[192,1024]{1,0:T(8,128)(2,1)S(1)}, bf16[192,1024]{1,0:T(8,128)(2,1)}, u32[]{:S(2)}, u32[]{:S(2)}) collective-permute-start(bf16[192,1024]{1,0:T(8,128)(2,1)S(1)} %get-tuple-element.24), channel_id=1, source_target_pairs={{0,2},{1,3},{2,0},{3,1},{4,6},{5,7},{6,4},{7,5},{8,10},{9,11},{10,... | collective-permute-start | bytes 1179656 | tf_op jit(solution)/shard_map/ppermute | solution.py:27
  173.6 16.4 %collective-permute-start.5 = (bf16[192,1024]{1,0:T(8,128)(2,1)S(1)}, bf16[192,1024]{1,0:T(8,128)(2,1)}, u32[]{:S(2)}, u32[]{:S(2)}) collective-permute-start(bf16[192,1024]{1,0:T(8,128)(2,1)S(1)} %get-tuple-element.23), channel_id=1, source_target_pairs={{0,3},{1,0},{2,1},{3,2},{4,7},{5,4},{6,5},{7,6},{8,11},{9,8},{10,9... | collective-permute-start | bytes 1179656 | tf_op jit(solution)/shard_map/ppermute | solution.py:27
  191.4 13.8 %collective-permute-start.6 = (bf16[192,1024]{1,0:T(8,128)(2,1)S(1)}, bf16[192,1024]{1,0:T(8,128)(2,1)S(1)}, u32[]{:S(2)}, u32[]{:S(2)}) collective-permute-start(bf16[192,1024]{1,0:T(8,128)(2,1)S(1)} %fusion.5), channel_id=1, source_target_pairs={{0,1},{1,2},{2,3},{3,0},{4,5},{5,6},{6,7},{7,4},{8,9},{9,10},{10,1... | collective-permute-start | bytes 1179656 | tf_op jit(solution)/shard_map/ppermute | solution.py:34
  196.6 18.5 %collective-permute-start.7 = (bf16[192,1024]{1,0:T(8,128)(2,1)S(1)}, bf16[192,1024]{1,0:T(8,128)(2,1)S(1)}, u32[]{:S(2)}, u32[]{:S(2)}) collective-permute-start(bf16[192,1024]{1,0:T(8,128)(2,1)S(1)} %fusion.5), channel_id=1, source_target_pairs={{0,2},{1,3},{2,0},{3,1},{4,6},{5,7},{6,4},{7,5},{8,10},{9,11},{10,... | collective-permute-start | bytes 1179656 | tf_op jit(solution)/shard_map/ppermute | solution.py:34
  199.9 16.4 %collective-permute-start.8 = (bf16[192,1024]{1,0:T(8,128)(2,1)S(1)}, bf16[192,1024]{1,0:T(8,128)(2,1)S(1)}, u32[]{:S(2)}, u32[]{:S(2)}) collective-permute-start(bf16[192,1024]{1,0:T(8,128)(2,1)S(1)} %fusion.5), channel_id=1, source_target_pairs={{0,3},{1,0},{2,1},{3,2},{4,7},{5,4},{6,5},{7,6},{8,11},{9,8},{10,9... | collective-permute-start | bytes 1179656 | tf_op jit(solution)/shard_map/ppermute | solution.py:34
  217.6 1.7 copy-start
  217.6 2.6 copy-start.11
  219.3 0.9 copy-start.7
  224.4 5.4 %collective-permute-start.9 = (bf16[128,3,1024]{2,0,1:T(8,128)(2,1)S(1)}, bf16[128,3,1024]{2,0,1:T(8,128)(2,1)S(1)}, u32[]{:S(2)}, u32[]{:S(2)}) collective-permute-start(bf16[128,3,1024]{2,0,1:T(8,128)(2,1)S(1)} %broadcast_select_fusion.3), channel_id=1, source_target_pairs={{0,4},{4,0},{8,12},{12,8},{16,20},{20,16},{24,28},{28,24},{32,36},... | collective-permute-start | bytes 2359304 | tf_op jit(solution)/shard_map/ppermute | solution.py:16
  230.5 9.2 %copy-start.4 = (bf16[768,896]{1,0:T(8,128)(2,1)S(1)}, bf16[768,896]{1,0:T(8,128)(2,1)}, u32[]{:S(2)}) copy-start(bf16[768,896]{1,0:T(8,128)(2,1)} %reshape.227) | copy-start | bytes 4128772
  230.5 9.2 %copy-start.8 = (bf16[768,512]{1,0:T(8,128)(2,1)S(1)}, bf16[768,512]{1,0:T(8,128)(2,1)}, u32[]{:S(2)}) copy-start(bf16[768,512]{1,0:T(8,128)(2,1)} %copy-done.7) | copy-start | bytes 2359300
  231.8 51.4 %all-to-all-start.1 = ((bf16[128,24,128]{2,1,0:T(8,128)(2,1)}), bf16[128,24,128]{2,1,0:T(8,128)(2,1)S(1)}, u32[]{:S(2)}, u32[]{:S(2)}) async-start(bf16[128,24,128]{2,1,0:T(8,128)(2,1)} %copy.55), calls=%async_computation.1 | async-start | bytes 1572864 | tf_op jit(solution)/shard_map/all_to_all | solution.py:139
  239.7 1.9 copy-start.1
  239.8 2.6 copy-start.6

commit v4 on v3

--- a/solution.py
+++ b/solution.py
@@ -18,23 +18,13 @@
 
 def dp_sum(part, axis):
     count = lax.axis_size(axis)
-    here = lax.axis_index(axis)
     rows = part.shape[0] // count
-    blocks = part.reshape(count, rows, part.shape[1])
-    total = blocks[here].astype(jnp.float32)
-    for step in range(1, count):
-        pairs = [(source, (source + step) % count) for source in range(count)]
-        total = total + lax.ppermute(blocks[(here + step) % count], axis, pairs).astype(
-            jnp.float32
-        )
-    reduced = total.astype(jnp.bfloat16)
-    gathered = [reduced]
-    for step in range(1, count):
-        pairs = [(source, (source + step) % count) for source in range(count)]
-        gathered.append(lax.ppermute(reduced, axis, pairs))
-    stacked = jnp.stack(gathered)
-    order = (here - jnp.arange(count)) % count
-    return stacked[order].reshape(part.shape)
+    blocks = lane_rows(part.reshape(count, rows, part.shape[1]))
+    pieces = lax.all_to_all(blocks, axis, split_axis=0, concat_axis=0, tiled=True)
+    reduced = jnp.sum(pieces.astype(jnp.float32), 0).astype(jnp.bfloat16)
+    copies = jnp.broadcast_to(reduced[None], (count,) + reduced.shape)
+    gathered = lax.all_to_all(copies, axis, split_axis=0, concat_axis=0, tiled=True)
+    return gathered.reshape(part.shape)
 
 
 def lane_rows(value):

time: 293 us -> 306 us (1.044)
  blocking collectives: 96.8 us -> 120 us
  starting transfers between devices: 43.6 us -> 27.4 us
  local copies, waits for them, and re-layouts: 32 us -> 44 us
  waiting for transfers between devices: 92.1 us -> 83.1 us
    ppermute x6 -> x0, waiting for transfers between devices: 26.7 us -> none  [the longest x3 13.4 us: dp_sum(): lax.ppermute(blocks[(here + step) % count], axis, pairs).astype(jnp.float32)]
    all_to_all x0 -> x1, blocking collectives: none -> 23.6 us  [dp_sum(): lax.all_to_all(blocks, axis, split_axis=0, concat_axis=0, tiled=True)]
    ppermute x6 -> x0, starting transfers between devices: 22.2 us -> none  [the longest x3 11.5 us: dp_sum(): gathered.append(lax.ppermute(reduced, axis, pairs))]
    all_to_all x0 -> x1, waiting for transfers between devices: none -> 18.8 us  [dp_sum(): lax.all_to_all(copies, axis, split_axis=0, concat_axis=0, tiled=True)]
    reshape x2, local copies, waits for them, and re-layouts: 0.69 us -> 6.29 us  [layer(): route_half.reshape(devices_ex, capacity, quarter)]
    all_to_all x0 -> x1, starting transfers between devices: none -> 4.34 us  [dp_sum(): lax.all_to_all(copies, axis, split_axis=0, concat_axis=0, tiled=True)]
  transfers between devices with their start and end apart: 11 -> 6, of which waited for: 10 -> 5; matrix products, arithmetic and copies ran while one was open for 6% -> 6% of each run, Pallas kernels for 0% -> 0%
where the time goes in v4:
time: 306 us; the launch traced here: 304 us
  blocking collectives  120 us (39%)
  waiting for transfers between devices  83.1 us (27%)
  local copies, waits for them, and re-layouts  44 us (14%)
  starting transfers between devices  27.4 us (9%)
  matrix products  15.4 us (5%)
  other arithmetic  12.7 us (4%)
    all_to_all x1, blocking collectives, layer(): lax.all_to_all(lane_rows(dispatch), 'expert', split_axis=0, concat_axis=0...  96.8 us
    all_to_all x1, waiting for transfers between devices, layer(): lax.all_to_all(lane_rows(combined), 'expert', split_axis=0, concat_axis=0...  37.7 us
    ppermute x2, waiting for transfers between devices, passed_along(): return lax.ppermute(value, axis, pairs)  24.7 us
    all_to_all x1, blocking collectives, dp_sum(): lax.all_to_all(blocks, axis, split_axis=0, concat_axis=0, tiled=True)  23.6 us
    all_to_all x1, waiting for transfers between devices, dp_sum(): lax.all_to_all(copies, axis, split_axis=0, concat_axis=0, tiled=True)  18.8 us
    all_to_all x1, starting transfers between devices, layer(): lax.all_to_all(lane_rows(combined), 'expert', split_axis=0, concat_axis=0...  8.36 us
    ppermute x2, starting transfers between devices, core_swap(): return lax.ppermute(value, axis, pairs)  7.78 us
    ppermute x2, starting transfers between devices, passed_along(): return lax.ppermute(value, axis, pairs)  6.97 us
  transfers between devices with their start and end apart: 6, of which 5 were waited for; matrix products, arithmetic and copies ran while one was open for 6% of the time, Pallas kernels for 0%

profile of v4, /device:TPU:1, one launch (start us, length us, event | category | flops | bytes accessed | tf_op | source)
XLA Modules:
  0.0 304.3 jit_solution(8592294162671115454)
XLA Ops:
  6.6 1.9 gather_fusion
  8.5 1.9 scatter_custom_fusion.1
  11.1 1.9 scatter_custom_fusion
  15.3 96.8 %all_to_all.20 = bf16[128,42,128]{2,1,0:T(8,128)(2,1)S(1)} all-to-all(bf16[128,42,128]{2,1,0:T(8,128)(2,1)S(1)} %reshape_reshape.6), channel_id=1, replica_groups=mesh['expert'=128,'dp'=4] {'expert'}, dimensions={0} | all-to-all | bytes 2752512 | tf_op jit(solution)/shard_map/all_to_all | solution.py:88
  113.6 3.0 collective-permute-start
  116.6 4.7 %collective-permute-start.1 = (bf16[896,512]{1,0:T(8,128)(2,1)}, bf16[896,512]{1,0:T(8,128)(2,1)}, u32[]{:S(2)}, u32[]{:S(2)}) collective-permute-start(bf16[896,512]{1,0:T(8,128)(2,1)} %param.12), channel_id=1, source_target_pairs={{0,256},{4,260},{8,264},{12,268},{16,272},{20,276},{24,280},{28,28... | collective-permute-start | bytes 2752520 | tf_op jit(solution)/shard_map/ppermute | solution.py:10
  121.4 2.2 collective-permute-start.2
  124.2 1.7 broadcast_select_fusion.1
  126.0 3.1 %copy.65 = bf16[128,6,896]{2,1,0:T(8,128)(2,1)S(1)} copy(bf16[128,6,896]{0,2,1:T(8,128)(2,1)} %get-tuple-element.24) | data formatting | bytes 2752512 | tf_op jit(solution)/shard_map/jit(_where)/select_n | solution.py:92
  130.7 2.0 copy.66
  134.1 8.1 %collective-permute-done.1 = bf16[896,512]{1,0:T(8,128)(2,1)} collective-permute-done((bf16[896,512]{1,0:T(8,128)(2,1)}, bf16[896,512]{1,0:T(8,128)(2,1)}, u32[]{:S(2)}, u32[]{:S(2)}) %collective-permute-start.1) | collective-permute-done | bytes 917536 | tf_op jit(solution)/shard_map/ppermute | solution.py:10
  142.2 3.1 %convolution_convert_fusion.4 = bf16[768,512]{0,1:T(8,128)(2,1)S(1)} fusion(bf16[768,896]{1,0:T(8,128)(2,1)S(1)} %copy-done.2, bf16[896,512]{1,0:T(8,128)(2,1)} %collective-permute-done.1, bf16[896,512]{1,0:T(8,128)(2,1)} %param.12, pred[]{:T(512)} %bitcast.6), kind=kOutput, calls=%fused_computation.17 | convolution fusion | flops 705495040 | bytes 3997697 | tf_op jit(solution)/shard_map/dot_general | solution.py:95
  145.3 16.5 %collective-permute-done.2 = bf16[896,512]{1,0:T(8,128)(2,1)} collective-permute-done((bf16[896,512]{1,0:T(8,128)(2,1)}, bf16[896,512]{1,0:T(8,128)(2,1)}, u32[]{:S(2)}, u32[]{:S(2)}) %collective-permute-start.2) | collective-permute-done | bytes 917536 | tf_op jit(solution)/shard_map/ppermute | solution.py:10
  161.9 2.9 convolution_convert_fusion.3
  166.5 23.6 %all_to_all.21 = bf16[4,1536,128]{2,1,0:T(8,128)(2,1)S(1)} all-to-all(bf16[4,1536,128]{2,1,0:T(8,128)(2,1)S(1)} %reshape_reshape.7), channel_id=1, replica_groups=mesh['expert'=128,'dp'=4] {'dp'}, dimensions={0} | all-to-all | bytes 3145728 | tf_op jit(solution)/shard_map/all_to_all | solution.py:23
  192.0 4.3 %all-to-all-start.2 = ((bf16[4,1536,128]{2,1,0:T(8,128)(2,1)}), bf16[4,1536,128]{2,1,0:T(8,128)(2,1)}, u32[]{:S(2)}, u32[]{:S(2)}) async-start(bf16[4,1536,128]{2,1,0:T(8,128)(2,1)} %broadcast_in_dim.28), calls=%async_computation.2 | async-start | bytes 3145728 | tf_op jit(solution)/shard_map/all_to_all | solution.py:26
  196.3 18.8 %all-to-all-done.2 = bf16[4,1536,128]{2,1,0:T(8,128)(2,1)} async-done(((bf16[4,1536,128]{2,1,0:T(8,128)(2,1)}), bf16[4,1536,128]{2,1,0:T(8,128)(2,1)}, u32[]{:S(2)}, u32[]{:S(2)}) %all-to-all-start.2) | async-done | bytes 1572896 | tf_op jit(solution)/shard_map/all_to_all | solution.py:26
  215.2 2.5 reshape.181
  219.4 4.0 %convolution_convert_fusion = bf16[768,896]{1,0:T(8,128)(2,1)} fusion(bf16[768,512]{1,0:T(8,128)(2,1)S(1)} %get-tuple-element.22, bf16[896,512]{1,0:T(8,128)(2,1)} %collective-permute-done.1, bf16[896,512]{1,0:T(8,128)(2,1)S(1)} %copy-done.8, pred[]{:T(512)} %bitcast.6), kind=kOutput, calls=%fused_computation.5 | convolution fusion | flops 705789952 | bytes 3997697 | tf_op jit(solution)/shard_map/nf,df->nd/dot_general | solution.py:105
  223.4 3.5 %reshape.176 = bf16[128,6,896]{2,1,0:T(8,128)(2,1)} reshape(bf16[768,896]{1,0:T(8,128)(2,1)} %convolution_convert_fusion) | data formatting | bytes 2752512 | tf_op jit(solution)/shard_map/reshape | solution.py:122
  226.9 2.8 copy.69
  231.7 4.8 %collective-permute-start.3 = (bf16[128,3,1024]{2,0,1:T(8,128)(2,1)S(1)}, bf16[128,3,1024]{2,0,1:T(8,128)(2,1)S(1)}, u32[]{:S(2)}, u32[]{:S(2)}) collective-permute-start(bf16[128,3,1024]{2,0,1:T(8,128)(2,1)S(1)} %broadcast_select_fusion.3), channel_id=1, source_target_pairs={{0,4},{4,0},{8,12},{12,8},{16,20},{20,16},{24,28},{28,24},{32,36},... | collective-permute-start | bytes 2359304 | tf_op jit(solution)/shard_map/ppermute | solution.py:16
  236.5 1.9 collective-permute-done.3
  239.6 2.3 copy.70
  241.9 2.4 copy.71
  244.3 8.4 %all-to-all-start.3 = ((bf16[128,24,128]{2,1,0:T(8,128)(2,1)}), bf16[128,24,128]{2,1,0:T(8,128)(2,1)}, u32[]{:S(2)}, u32[]{:S(2)}) async-start(bf16[128,24,128]{2,1,0:T(8,128)(2,1)} %copy.71), calls=%async_computation.3 | async-start | bytes 1572864 | tf_op jit(solution)/shard_map/all_to_all | solution.py:129
  252.6 3.5 %convolution_convert_fusion.2 = bf16[896,512]{1,0:T(8,128)(2,1)} fusion(bf16[768,896]{1,0:T(8,128)(2,1)} %reshape.174, bf16[768,512]{1,0:T(8,128)(2,1)} %copy-done.5), kind=kOutput, calls=%fused_computation.15 | convolution fusion | flops 705101824 | bytes 3080192 | tf_op jit(solution)/shard_map/nd,nf->df/dot_general | solution.py:108
  256.1 1.9 convolution_convert_fusion.1
  258.1 37.7 %all-to-all-done.3 = bf16[128,24,128]{2,1,0:T(8,128)(2,1)} async-done(((bf16[128,24,128]{2,1,0:T(8,128)(2,1)}), bf16[128,24,128]{2,1,0:T(8,128)(2,1)}, u32[]{:S(2)}, u32[]{:S(2)}) %all-to-all-start.3) | async-done | bytes 786464 | tf_op jit(solution)/shard_map/all_to_all | solution.py:129
  295.8 2.0 reshape.178
  298.2 2.7 gather_fusion.1
  302.3 1.9 reduce.1
  (71 shorter events, 24.1 us)
Async XLA Ops:
  8.5 2.2 copy-start.6
  113.6 10.6 %collective-permute-start = (bf16[128,6,896]{0,2,1:T(8,128)(2,1)S(1)}, bf16[128,6,896]{0,2,1:T(8,128)(2,1)S(1)}, u32[]{:S(2)}, u32[]{:S(2)}) collective-permute-start(bf16[128,6,896]{0,2,1:T(8,128)(2,1)S(1)} %bitcast.34), channel_id=1, source_target_pairs={{0,4},{4,0},{8,12},{12,8},{16,20},{20,16},{24,28},{28,24},{32,36},... | collective-permute-start | bytes 4128776 | tf_op jit(solution)/shard_map/ppermute | solution.py:16
  116.6 25.6 %collective-permute-start.1 = (bf16[896,512]{1,0:T(8,128)(2,1)}, bf16[896,512]{1,0:T(8,128)(2,1)}, u32[]{:S(2)}, u32[]{:S(2)}) collective-permute-start(bf16[896,512]{1,0:T(8,128)(2,1)} %param.12), channel_id=1, source_target_pairs={{0,256},{4,260},{8,264},{12,268},{16,272},{20,276},{24,280},{28,28... | collective-permute-start | bytes 2752520 | tf_op jit(solution)/shard_map/ppermute | solution.py:10
  121.4 40.5 %collective-permute-start.2 = (bf16[896,512]{1,0:T(8,128)(2,1)}, bf16[896,512]{1,0:T(8,128)(2,1)}, u32[]{:S(2)}, u32[]{:S(2)}) collective-permute-start(bf16[896,512]{1,0:T(8,128)(2,1)} %param.13), channel_id=1, source_target_pairs={{0,256},{4,260},{8,264},{12,268},{16,272},{20,276},{24,280},{28,28... | collective-permute-start | bytes 2752520 | tf_op jit(solution)/shard_map/ppermute | solution.py:10
  129.0 1.7 copy-start.1
  132.8 9.5 %copy-start.2 = (bf16[768,896]{1,0:T(8,128)(2,1)S(1)}, bf16[768,896]{1,0:T(8,128)(2,1)}, u32[]{:S(2)}) copy-start(bf16[768,896]{1,0:T(8,128)(2,1)} %reshape.174) | copy-start | bytes 4128772
  142.2 19.7 %copy-start.3 = (bf16[768,896]{1,0:T(8,128)(2,1)S(1)}, bf16[768,896]{1,0:T(8,128)(2,1)}, u32[]{:S(2)}) copy-start(bf16[768,896]{1,0:T(8,128)(2,1)} %reshape.175) | copy-start | bytes 4128772
  142.2 19.7 %copy-start.7 = (bf16[896,512]{1,0:T(8,128)(2,1)S(1)}, bf16[896,512]{1,0:T(8,128)(2,1)}, u32[]{:S(2)}) copy-start(bf16[896,512]{1,0:T(8,128)(2,1)} %param.13) | copy-start | bytes 2752516
  192.0 23.2 %all-to-all-start.2 = ((bf16[4,1536,128]{2,1,0:T(8,128)(2,1)}), bf16[4,1536,128]{2,1,0:T(8,128)(2,1)}, u32[]{:S(2)}, u32[]{:S(2)}) async-start(bf16[4,1536,128]{2,1,0:T(8,128)(2,1)} %broadcast_in_dim.28), calls=%async_computation.2 | async-start | bytes 3145728 | tf_op jit(solution)/shard_map/all_to_all | solution.py:26
  217.7 1.7 copy-start.8
  218.6 0.9 copy-start.5
  229.9 8.5 %copy-start = (bf16[128,6,896]{2,0,1:T(8,128)(2,1)S(1)}, bf16[128,6,896]{2,0,1:T(8,128)(2,1)}, u32[]{:S(2)}) copy-start(bf16[128,6,896]{2,0,1:T(8,128)(2,1)} %copy.69) | copy-start | bytes 4128772
  231.7 6.7 %collective-permute-start.3 = (bf16[128,3,1024]{2,0,1:T(8,128)(2,1)S(1)}, bf16[128,3,1024]{2,0,1:T(8,128)(2,1)S(1)}, u32[]{:S(2)}, u32[]{:S(2)}) collective-permute-start(bf16[128,3,1024]{2,0,1:T(8,128)(2,1)S(1)} %broadcast_select_fusion.3), channel_id=1, source_target_pairs={{0,4},{4,0},{8,12},{12,8},{16,20},{20,16},{24,28},{28,24},{32,36},... | collective-permute-start | bytes 2359304 | tf_op jit(solution)/shard_map/ppermute | solution.py:16
  244.3 51.5 %all-to-all-start.3 = ((bf16[128,24,128]{2,1,0:T(8,128)(2,1)}), bf16[128,24,128]{2,1,0:T(8,128)(2,1)}, u32[]{:S(2)}, u32[]{:S(2)}) async-start(bf16[128,24,128]{2,1,0:T(8,128)(2,1)} %copy.71), calls=%async_computation.3 | async-start | bytes 1572864 | tf_op jit(solution)/shard_map/all_to_all | solution.py:129
  252.6 3.5 %copy-start.4 = (bf16[768,896]{1,0:T(8,128)(2,1)S(1)}, bf16[768,896]{1,0:T(8,128)(2,1)}, u32[]{:S(2)}) copy-start(bf16[768,896]{1,0:T(8,128)(2,1)} %reshape.175) | copy-start | bytes 4128772

commit v5 on v3

--- a/solution.py
+++ b/solution.py
@@ -86,15 +86,18 @@
     shifted = passed_along((w_up, w_down), "expert", devices_ex // 2)
     resident = pick_pair(swapped_here, shifted, own_weights)
     target = owner_slot[flat_routes]
-    position = target * capacity + slot_rank
-    empty_rows = jnp.zeros((experts * capacity, quarter), jnp.bfloat16)
-    token_buf = (
-        empty_rows.at[position]
-        .set(jnp.repeat(tokens, top_count, axis=0))
-        .reshape(experts, capacity, quarter)
+    token_pos = (2 * target * capacity + slot_rank).reshape(tok_rows, top_count)
+    scaled_pos = (2 * target + 1) * capacity + slot_rank
+    row_ids = jnp.arange(devices_ex * capacity, dtype=jnp.int32)[:, None]
+    pick_token = jnp.any(row_ids[:, :, None] == token_pos[None, :, :], -1)
+    pick_scaled = row_ids == scaled_pos[None, :]
+    picker = jnp.concatenate([pick_token, pick_scaled], axis=1).astype(jnp.bfloat16)
+    sources = jnp.concatenate([tokens, scaled], axis=0)
+    dispatch = (
+        jnp.dot(picker, sources, preferred_element_type=jnp.float32)
+        .astype(jnp.bfloat16)
+        .reshape(devices_ex, capacity, quarter)
     )
-    scaled_buf = empty_rows.at[position].set(scaled).reshape(experts, capacity, quarter)
-    dispatch = jnp.stack([token_buf, scaled_buf], axis=1).reshape(devices_ex, capacity, quarter)
     got = lax.all_to_all(
         lane_rows(dispatch), "expert", split_axis=0, concat_axis=0, tiled=True
     ).reshape(devices_ex, capacity, quarter)
@@ -139,14 +142,18 @@
     back = lax.all_to_all(
         lane_rows(combined), "expert", split_axis=0, concat_axis=0, tiled=True
     )
-    back_grid = back.reshape(experts, capacity, quarter + lanes)
-    picked = back_grid[target, slot_rank]
-    grad_tokens = jnp.sum(
-        picked[:, :quarter].astype(jnp.float32).reshape(tok_rows, top_count, quarter), 1
+    back_rows = back.reshape(experts * capacity, quarter + lanes)
+    route_pos = target * capacity + slot_rank
+    slot_ids = jnp.arange(experts * capacity, dtype=jnp.int32)[None, :]
+    of_route = route_pos[:, None] == slot_ids
+    of_token = jnp.any(of_route.reshape(tok_rows, top_count, -1), 1).astype(jnp.bfloat16)
+    grad_tokens = jnp.dot(
+        of_token, back_rows[:, :quarter], preferred_element_type=jnp.float32
     ).astype(jnp.bfloat16)
-    pairing_mine = (
-        picked[:, quarter].astype(jnp.float32) + picked[:, quarter + 1].astype(jnp.float32)
-    ).reshape(tok_rows, top_count)
+    pair_lanes = jnp.dot(
+        of_route.astype(jnp.bfloat16), back_rows[:, quarter:], preferred_element_type=jnp.float32
+    )
+    pairing_mine = (pair_lanes[:, 0] + pair_lanes[:, 1]).reshape(tok_rows, top_count)
     grad_logits = (1.0 - affinity) * (
         pairing_mine - weights * jnp.sum(pairing_mine, -1, keepdims=True)
     )

time: 293 us -> 299 us (1.020)
  matrix products: 12.7 us -> 18.6 us
  waiting for transfers between devices: 92.1 us -> 89 us
    reshape x2, local copies, waits for them, and re-layouts: 0.69 us -> 6.32 us  [layer(): route_half.reshape(devices_ex, capacity, quarter)]
    dot_general x0 -> x3, matrix products: none -> 3.14 us  [the longest x1 1.84 us: layer(): jnp.dot(picker, sources, preferred_element_type=jnp.float32)]
  transfers between devices with their start and end apart: 11 -> 11, of which waited for: 10 -> 10; matrix products, arithmetic and copies ran while one was open for 6% -> 7% of each run, Pallas kernels for 0% -> 0%
where the time goes in v5:
time: 299 us; the launch traced here: 296 us
  blocking collectives  96.8 us (32%)
  waiting for transfers between devices  89 us (30%)
  starting transfers between devices  44 us (15%)
  local copies, waits for them, and re-layouts  34.1 us (11%)
  matrix products  18.6 us (6%)
  other arithmetic  12.5 us (4%)
    all_to_all x1, blocking collectives, layer(): lax.all_to_all(lane_rows(dispatch), 'expert', split_axis=0, concat_axis=0...  96.8 us
    all_to_all x1, waiting for transfers between devices, layer(): lax.all_to_all(lane_rows(combined), 'expert', split_axis=0, concat_axis=0...  37.4 us
    ppermute x2, waiting for transfers between devices, passed_along(): return lax.ppermute(value, axis, pairs)  23 us
    ppermute x3, waiting for transfers between devices, dp_sum(): lax.ppermute(blocks[(here + step) % count], axis, pairs).astype(jnp.float32)  13.4 us
    ppermute x3, waiting for transfers between devices, dp_sum(): gathered.append(lax.ppermute(reduced, axis, pairs))  13.3 us
    ppermute x3, starting transfers between devices, dp_sum(): gathered.append(lax.ppermute(reduced, axis, pairs))  11.5 us
    ppermute x3, starting transfers between devices, dp_sum(): lax.ppermute(blocks[(here + step) % count], axis, pairs).astype(jnp.float32)  10.7 us
    all_to_all x1, starting transfers between devices, layer(): lax.all_to_all(lane_rows(combined), 'expert', split_axis=0, concat_axis=0...  8.36 us
  transfers between devices with their start and end apart: 11, of which 10 were waited for; matrix products, arithmetic and copies ran while one was open for 7% of the time, Pallas kernels for 0%

profile of v5, /device:TPU:1, one launch (start us, length us, event | category | flops | bytes accessed | tf_op | source)
XLA Modules:
  0.0 296.1 jit_solution(3280832490378688428)
XLA Ops:
  10.8 96.8 %all_to_all.10 = bf16[128,42,128]{2,1,0:T(8,128)(2,1)S(1)} all-to-all(bf16[128,42,128]{2,1,0:T(8,128)(2,1)S(1)} %reshape_reshape.3), channel_id=1, replica_groups=mesh['expert'=128,'dp'=4] {'expert'}, dimensions={0} | all-to-all | bytes 2752512 | tf_op jit(solution)/shard_map/all_to_all | solution.py:101
  109.1 3.0 %collective-permute-start = (bf16[128,6,896]{0,2,1:T(8,128)(2,1)S(1)}, bf16[128,6,896]{0,2,1:T(8,128)(2,1)S(1)}, u32[]{:S(2)}, u32[]{:S(2)}) collective-permute-start(bf16[128,6,896]{0,2,1:T(8,128)(2,1)S(1)} %bitcast.50), channel_id=1, source_target_pairs={{0,4},{4,0},{8,12},{12,8},{16,20},{20,16},{24,28},{28,24},{32,36},... | collective-permute-start | bytes 4128776 | tf_op jit(solution)/shard_map/ppermute | solution.py:16
  112.1 4.7 %collective-permute-start.1 = (bf16[896,512]{1,0:T(8,128)(2,1)}, bf16[896,512]{1,0:T(8,128)(2,1)}, u32[]{:S(2)}, u32[]{:S(2)}) collective-permute-start(bf16[896,512]{1,0:T(8,128)(2,1)} %param.12), channel_id=1, source_target_pairs={{0,256},{4,260},{8,264},{12,268},{16,272},{20,276},{24,280},{28,28... | collective-permute-start | bytes 2752520 | tf_op jit(solution)/shard_map/ppermute | solution.py:10
  116.9 2.2 collective-permute-start.2
  120.8 2.6 broadcast_select_fusion.1
  123.5 3.1 %copy.73 = bf16[128,6,896]{2,1,0:T(8,128)(2,1)S(1)} copy(bf16[128,6,896]{0,2,1:T(8,128)(2,1)} %get-tuple-element.28) | data formatting | bytes 2752512 | tf_op jit(solution)/shard_map/jit(_where)/select_n | solution.py:105
  127.9 2.0 copy.74
  131.3 6.5 %collective-permute-done.1 = bf16[896,512]{1,0:T(8,128)(2,1)} collective-permute-done((bf16[896,512]{1,0:T(8,128)(2,1)}, bf16[896,512]{1,0:T(8,128)(2,1)}, u32[]{:S(2)}, u32[]{:S(2)}) %collective-permute-start.1) | collective-permute-done | bytes 917536 | tf_op jit(solution)/shard_map/ppermute | solution.py:10
  137.7 3.1 %convolution_convert_fusion.5 = bf16[768,512]{0,1:T(8,128)(2,1)S(1)} fusion(bf16[768,896]{1,0:T(8,128)(2,1)S(1)} %copy-done.2, bf16[896,512]{1,0:T(8,128)(2,1)} %collective-permute-done.1, bf16[896,512]{1,0:T(8,128)(2,1)} %param.12, pred[]{:T(512)} %bitcast.3), kind=kOutput, calls=%fused_computation.17 | convolution fusion | flops 705495040 | bytes 3997697 | tf_op jit(solution)/shard_map/dot_general | solution.py:108
  140.8 16.6 %collective-permute-done.2 = bf16[896,512]{1,0:T(8,128)(2,1)} collective-permute-done((bf16[896,512]{1,0:T(8,128)(2,1)}, bf16[896,512]{1,0:T(8,128)(2,1)}, u32[]{:S(2)}, u32[]{:S(2)}) %collective-permute-start.2) | collective-permute-done | bytes 917536 | tf_op jit(solution)/shard_map/ppermute | solution.py:10
  157.4 3.0 %convolution_convert_fusion.4 = bf16[768,512]{0,1:T(8,128)(2,1)S(1)} fusion(bf16[768,896]{1,0:T(8,128)(2,1)S(1)} %copy-done.3, bf16[896,512]{1,0:T(8,128)(2,1)} %collective-permute-done.2, bf16[896,512]{1,0:T(8,128)(2,1)S(1)} %copy-done.8, pred[]{:T(512)} %bitcast.3), kind=kOutput, calls=%fused_computation.16 | convolution fusion | flops 705495040 | bytes 3997697 | tf_op jit(solution)/shard_map/dot_general | solution.py:109
  161.4 3.2 %collective-permute-start.3 = (bf16[192,1024]{1,0:T(8,128)(2,1)S(1)}, bf16[192,1024]{1,0:T(8,128)(2,1)S(1)}, u32[]{:S(2)}, u32[]{:S(2)}) collective-permute-start(bf16[192,1024]{1,0:T(8,128)(2,1)S(1)} %get-tuple-element.30), channel_id=1, source_target_pairs={{0,1},{1,2},{2,3},{3,0},{4,5},{5,6},{6,7},{7,4},{8,9},{9,10},{10,1... | collective-permute-start | bytes 1179656 | tf_op jit(solution)/shard_map/ppermute | solution.py:27
  164.6 4.5 %collective-permute-start.4 = (bf16[192,1024]{1,0:T(8,128)(2,1)S(1)}, bf16[192,1024]{1,0:T(8,128)(2,1)}, u32[]{:S(2)}, u32[]{:S(2)}) collective-permute-start(bf16[192,1024]{1,0:T(8,128)(2,1)S(1)} %get-tuple-element.32), channel_id=1, source_target_pairs={{0,2},{1,3},{2,0},{3,1},{4,6},{5,7},{6,4},{7,5},{8,10},{9,11},{10,... | collective-permute-start | bytes 1179656 | tf_op jit(solution)/shard_map/ppermute | solution.py:27
  169.1 3.0 %collective-permute-start.5 = (bf16[192,1024]{1,0:T(8,128)(2,1)S(1)}, bf16[192,1024]{1,0:T(8,128)(2,1)}, u32[]{:S(2)}, u32[]{:S(2)}) collective-permute-start(bf16[192,1024]{1,0:T(8,128)(2,1)S(1)} %get-tuple-element.31), channel_id=1, source_target_pairs={{0,3},{1,0},{2,1},{3,2},{4,7},{5,4},{6,5},{7,6},{8,11},{9,8},{10,9... | collective-permute-start | bytes 1179656 | tf_op jit(solution)/shard_map/ppermute | solution.py:27
  172.1 2.3 collective-permute-done.3
  174.4 9.6 %collective-permute-done.4 = bf16[192,1024]{1,0:T(8,128)(2,1)} collective-permute-done((bf16[192,1024]{1,0:T(8,128)(2,1)S(1)}, bf16[192,1024]{1,0:T(8,128)(2,1)}, u32[]{:S(2)}, u32[]{:S(2)}) %collective-permute-start.4) | collective-permute-done | bytes 393248 | tf_op jit(solution)/shard_map/ppermute | solution.py:27
  186.8 5.3 %collective-permute-start.6 = (bf16[192,1024]{1,0:T(8,128)(2,1)S(1)}, bf16[192,1024]{1,0:T(8,128)(2,1)S(1)}, u32[]{:S(2)}, u32[]{:S(2)}) collective-permute-start(bf16[192,1024]{1,0:T(8,128)(2,1)S(1)} %fusion.8), channel_id=1, source_target_pairs={{0,1},{1,2},{2,3},{3,0},{4,5},{5,6},{6,7},{7,4},{8,9},{9,10},{10,1... | collective-permute-start | bytes 1179656 | tf_op jit(solution)/shard_map/ppermute | solution.py:34
  192.1 3.2 %collective-permute-start.7 = (bf16[192,1024]{1,0:T(8,128)(2,1)S(1)}, bf16[192,1024]{1,0:T(8,128)(2,1)S(1)}, u32[]{:S(2)}, u32[]{:S(2)}) collective-permute-start(bf16[192,1024]{1,0:T(8,128)(2,1)S(1)} %fusion.8), channel_id=1, source_target_pairs={{0,2},{1,3},{2,0},{3,1},{4,6},{5,7},{6,4},{7,5},{8,10},{9,11},{10,... | collective-permute-start | bytes 1179656 | tf_op jit(solution)/shard_map/ppermute | solution.py:34
  195.4 3.0 %collective-permute-start.8 = (bf16[192,1024]{1,0:T(8,128)(2,1)S(1)}, bf16[192,1024]{1,0:T(8,128)(2,1)S(1)}, u32[]{:S(2)}, u32[]{:S(2)}) collective-permute-start(bf16[192,1024]{1,0:T(8,128)(2,1)S(1)} %fusion.8), channel_id=1, source_target_pairs={{0,3},{1,0},{2,1},{3,2},{4,7},{5,4},{6,5},{7,6},{8,11},{9,8},{10,9... | collective-permute-start | bytes 1179656 | tf_op jit(solution)/shard_map/ppermute | solution.py:34
  198.4 2.2 collective-permute-done.6
  200.7 9.9 %collective-permute-done.7 = bf16[192,1024]{1,0:T(8,128)(2,1)S(1)} collective-permute-done((bf16[192,1024]{1,0:T(8,128)(2,1)S(1)}, bf16[192,1024]{1,0:T(8,128)(2,1)S(1)}, u32[]{:S(2)}, u32[]{:S(2)}) %collective-permute-start.7) | collective-permute-done | bytes 393248 | tf_op jit(solution)/shard_map/ppermute | solution.py:34
  217.3 4.0 %convolution_convert_fusion.1 = bf16[768,896]{1,0:T(8,128)(2,1)} fusion(bf16[768,512]{1,0:T(8,128)(2,1)S(1)} %get-tuple-element.26, bf16[896,512]{1,0:T(8,128)(2,1)} %collective-permute-done.1, bf16[896,512]{1,0:T(8,128)(2,1)S(1)} %copy-done.9, pred[]{:T(512)} %bitcast.3), kind=kOutput, calls=%fused_computation.3 | convolution fusion | flops 705789952 | bytes 3997697 | tf_op jit(solution)/shard_map/nf,df->nd/dot_general | solution.py:118
  221.2 3.5 %reshape.208 = bf16[128,6,896]{2,1,0:T(8,128)(2,1)} reshape(bf16[768,896]{1,0:T(8,128)(2,1)} %convolution_convert_fusion.1) | data formatting | bytes 2752512 | tf_op jit(solution)/shard_map/reshape | solution.py:135
  224.8 2.8 copy.77
  229.6 3.5 %collective-permute-start.9 = (bf16[128,3,1024]{2,0,1:T(8,128)(2,1)S(1)}, bf16[128,3,1024]{2,0,1:T(8,128)(2,1)S(1)}, u32[]{:S(2)}, u32[]{:S(2)}) collective-permute-start(bf16[128,3,1024]{2,0,1:T(8,128)(2,1)S(1)} %broadcast_select_fusion.3), channel_id=1, source_target_pairs={{0,4},{4,0},{8,12},{12,8},{16,20},{20,16},{24,28},{28,24},{32,36},... | collective-permute-start | bytes 2359304 | tf_op jit(solution)/shard_map/ppermute | solution.py:16
  233.1 1.9 collective-permute-done.9
  236.2 2.3 copy.78
  238.4 2.4 copy.79
  240.8 8.4 %all-to-all-start.1 = ((bf16[128,24,128]{2,1,0:T(8,128)(2,1)}), bf16[128,24,128]{2,1,0:T(8,128)(2,1)}, u32[]{:S(2)}, u32[]{:S(2)}) async-start(bf16[128,24,128]{2,1,0:T(8,128)(2,1)} %copy.79), calls=%async_computation.1 | async-start | bytes 1572864 | tf_op jit(solution)/shard_map/all_to_all | solution.py:142
  249.6 3.5 %convolution_convert_fusion.3 = bf16[896,512]{1,0:T(8,128)(2,1)} fusion(bf16[768,896]{1,0:T(8,128)(2,1)} %reshape.205, bf16[768,512]{1,0:T(8,128)(2,1)} %copy-done.5), kind=kOutput, calls=%fused_computation.15 | convolution fusion | flops 705101824 | bytes 3080192 | tf_op jit(solution)/shard_map/nd,nf->df/dot_general | solution.py:121
  253.0 1.9 convolution_convert_fusion.2
  255.0 37.4 %all-to-all-done.1 = bf16[128,24,128]{2,1,0:T(8,128)(2,1)} async-done(((bf16[128,24,128]{2,1,0:T(8,128)(2,1)}), bf16[128,24,128]{2,1,0:T(8,128)(2,1)}, u32[]{:S(2)}, u32[]{:S(2)}) %all-to-all-start.1) | async-done | bytes 786464 | tf_op jit(solution)/shard_map/all_to_all | solution.py:142
  (82 shorter events, 33.6 us)
Async XLA Ops:
  0.6 5.4 %copy-start.7 = (f32[128,2]{0,1:T(2,128)S(1)}, f32[128,2]{0,1:T(2,128)}, u32[]{:S(2)}) copy-start(f32[128,2]{0,1:T(2,128)} %param.9) | copy-start | bytes 3076
  0.6 5.9 %copy-start.6 = (bf16[128,896]{1,0:T(8,128)(2,1)S(1)}, bf16[128,896]{1,0:T(8,128)(2,1)}, u32[]{:S(2)}) copy-start(bf16[128,896]{1,0:T(8,128)(2,1)} %param.10) | copy-start | bytes 688132
  109.1 10.7 %collective-permute-start = (bf16[128,6,896]{0,2,1:T(8,128)(2,1)S(1)}, bf16[128,6,896]{0,2,1:T(8,128)(2,1)S(1)}, u32[]{:S(2)}, u32[]{:S(2)}) collective-permute-start(bf16[128,6,896]{0,2,1:T(8,128)(2,1)S(1)} %bitcast.50), channel_id=1, source_target_pairs={{0,4},{4,0},{8,12},{12,8},{16,20},{20,16},{24,28},{28,24},{32,36},... | collective-permute-start | bytes 4128776 | tf_op jit(solution)/shard_map/ppermute | solution.py:16
  112.1 25.6 %collective-permute-start.1 = (bf16[896,512]{1,0:T(8,128)(2,1)}, bf16[896,512]{1,0:T(8,128)(2,1)}, u32[]{:S(2)}, u32[]{:S(2)}) collective-permute-start(bf16[896,512]{1,0:T(8,128)(2,1)} %param.12), channel_id=1, source_target_pairs={{0,256},{4,260},{8,264},{12,268},{16,272},{20,276},{24,280},{28,28... | collective-permute-start | bytes 2752520 | tf_op jit(solution)/shard_map/ppermute | solution.py:10
  116.9 40.5 %collective-permute-start.2 = (bf16[896,512]{1,0:T(8,128)(2,1)}, bf16[896,512]{1,0:T(8,128)(2,1)}, u32[]{:S(2)}, u32[]{:S(2)}) collective-permute-start(bf16[896,512]{1,0:T(8,128)(2,1)} %param.13), channel_id=1, source_target_pairs={{0,256},{4,260},{8,264},{12,268},{16,272},{20,276},{24,280},{28,28... | collective-permute-start | bytes 2752520 | tf_op jit(solution)/shard_map/ppermute | solution.py:10
  119.8 1.1 copy-start.1
  129.9 7.8 %copy-start.2 = (bf16[768,896]{1,0:T(8,128)(2,1)S(1)}, bf16[768,896]{1,0:T(8,128)(2,1)}, u32[]{:S(2)}) copy-start(bf16[768,896]{1,0:T(8,128)(2,1)} %reshape.205) | copy-start | bytes 4128772
  137.7 19.7 %copy-start.3 = (bf16[768,896]{1,0:T(8,128)(2,1)S(1)}, bf16[768,896]{1,0:T(8,128)(2,1)}, u32[]{:S(2)}) copy-start(bf16[768,896]{1,0:T(8,128)(2,1)} %reshape.206) | copy-start | bytes 4128772
  137.7 19.7 %copy-start.8 = (bf16[896,512]{1,0:T(8,128)(2,1)S(1)}, bf16[896,512]{1,0:T(8,128)(2,1)}, u32[]{:S(2)}) copy-start(bf16[896,512]{1,0:T(8,128)(2,1)} %param.13) | copy-start | bytes 2752516
  161.4 13.0 %collective-permute-start.3 = (bf16[192,1024]{1,0:T(8,128)(2,1)S(1)}, bf16[192,1024]{1,0:T(8,128)(2,1)S(1)}, u32[]{:S(2)}, u32[]{:S(2)}) collective-permute-start(bf16[192,1024]{1,0:T(8,128)(2,1)S(1)} %get-tuple-element.30), channel_id=1, source_target_pairs={{0,1},{1,2},{2,3},{3,0},{4,5},{5,6},{6,7},{7,4},{8,9},{9,10},{10,1... | collective-permute-start | bytes 1179656 | tf_op jit(solution)/shard_map/ppermute | solution.py:27
  164.6 19.5 %collective-permute-start.4 = (bf16[192,1024]{1,0:T(8,128)(2,1)S(1)}, bf16[192,1024]{1,0:T(8,128)(2,1)}, u32[]{:S(2)}, u32[]{:S(2)}) collective-permute-start(bf16[192,1024]{1,0:T(8,128)(2,1)S(1)} %get-tuple-element.32), channel_id=1, source_target_pairs={{0,2},{1,3},{2,0},{3,1},{4,6},{5,7},{6,4},{7,5},{8,10},{9,11},{10,... | collective-permute-start | bytes 1179656 | tf_op jit(solution)/shard_map/ppermute | solution.py:27
  169.1 16.4 %collective-permute-start.5 = (bf16[192,1024]{1,0:T(8,128)(2,1)S(1)}, bf16[192,1024]{1,0:T(8,128)(2,1)}, u32[]{:S(2)}, u32[]{:S(2)}) collective-permute-start(bf16[192,1024]{1,0:T(8,128)(2,1)S(1)} %get-tuple-element.31), channel_id=1, source_target_pairs={{0,3},{1,0},{2,1},{3,2},{4,7},{5,4},{6,5},{7,6},{8,11},{9,8},{10,9... | collective-permute-start | bytes 1179656 | tf_op jit(solution)/shard_map/ppermute | solution.py:27
  186.8 13.8 %collective-permute-start.6 = (bf16[192,1024]{1,0:T(8,128)(2,1)S(1)}, bf16[192,1024]{1,0:T(8,128)(2,1)S(1)}, u32[]{:S(2)}, u32[]{:S(2)}) collective-permute-start(bf16[192,1024]{1,0:T(8,128)(2,1)S(1)} %fusion.8), channel_id=1, source_target_pairs={{0,1},{1,2},{2,3},{3,0},{4,5},{5,6},{6,7},{7,4},{8,9},{9,10},{10,1... | collective-permute-start | bytes 1179656 | tf_op jit(solution)/shard_map/ppermute | solution.py:34
  192.1 18.5 %collective-permute-start.7 = (bf16[192,1024]{1,0:T(8,128)(2,1)S(1)}, bf16[192,1024]{1,0:T(8,128)(2,1)S(1)}, u32[]{:S(2)}, u32[]{:S(2)}) collective-permute-start(bf16[192,1024]{1,0:T(8,128)(2,1)S(1)} %fusion.8), channel_id=1, source_target_pairs={{0,2},{1,3},{2,0},{3,1},{4,6},{5,7},{6,4},{7,5},{8,10},{9,11},{10,... | collective-permute-start | bytes 1179656 | tf_op jit(solution)/shard_map/ppermute | solution.py:34
  195.4 16.4 %collective-permute-start.8 = (bf16[192,1024]{1,0:T(8,128)(2,1)S(1)}, bf16[192,1024]{1,0:T(8,128)(2,1)S(1)}, u32[]{:S(2)}, u32[]{:S(2)}) collective-permute-start(bf16[192,1024]{1,0:T(8,128)(2,1)S(1)} %fusion.8), channel_id=1, source_target_pairs={{0,3},{1,0},{2,1},{3,2},{4,7},{5,4},{6,5},{7,6},{8,11},{9,8},{10,9... | collective-permute-start | bytes 1179656 | tf_op jit(solution)/shard_map/ppermute | solution.py:34
  215.5 1.7 copy-start.9
  216.4 0.9 copy-start.5
  227.8 7.2 %copy-start = (bf16[128,6,896]{2,0,1:T(8,128)(2,1)S(1)}, bf16[128,6,896]{2,0,1:T(8,128)(2,1)}, u32[]{:S(2)}) copy-start(bf16[128,6,896]{2,0,1:T(8,128)(2,1)} %copy.77) | copy-start | bytes 4128772
  229.6 5.4 %collective-permute-start.9 = (bf16[128,3,1024]{2,0,1:T(8,128)(2,1)S(1)}, bf16[128,3,1024]{2,0,1:T(8,128)(2,1)S(1)}, u32[]{:S(2)}, u32[]{:S(2)}) collective-permute-start(bf16[128,3,1024]{2,0,1:T(8,128)(2,1)S(1)} %broadcast_select_fusion.3), channel_id=1, source_target_pairs={{0,4},{4,0},{8,12},{12,8},{16,20},{20,16},{24,28},{28,24},{32,36},... | collective-permute-start | bytes 2359304 | tf_op jit(solution)/shard_map/ppermute | solution.py:16
  240.8 51.5 %all-to-all-start.1 = ((bf16[128,24,128]{2,1,0:T(8,128)(2,1)}), bf16[128,24,128]{2,1,0:T(8,128)(2,1)}, u32[]{:S(2)}, u32[]{:S(2)}) async-start(bf16[128,24,128]{2,1,0:T(8,128)(2,1)} %copy.79), calls=%async_computation.1 | async-start | bytes 1572864 | tf_op jit(solution)/shard_map/all_to_all | solution.py:142
  249.5 3.5 %copy-start.4 = (bf16[768,896]{1,0:T(8,128)(2,1)S(1)}, bf16[768,896]{1,0:T(8,128)(2,1)}, u32[]{:S(2)}) copy-start(bf16[768,896]{1,0:T(8,128)(2,1)} %reshape.206) | copy-start | bytes 4128772

commit v6 on v5

--- a/solution.py
+++ b/solution.py
@@ -142,18 +142,14 @@
     back = lax.all_to_all(
         lane_rows(combined), "expert", split_axis=0, concat_axis=0, tiled=True
     )
-    back_rows = back.reshape(experts * capacity, quarter + lanes)
-    route_pos = target * capacity + slot_rank
-    slot_ids = jnp.arange(experts * capacity, dtype=jnp.int32)[None, :]
-    of_route = route_pos[:, None] == slot_ids
-    of_token = jnp.any(of_route.reshape(tok_rows, top_count, -1), 1).astype(jnp.bfloat16)
-    grad_tokens = jnp.dot(
-        of_token, back_rows[:, :quarter], preferred_element_type=jnp.float32
+    back_grid = back.reshape(experts, capacity, quarter + lanes)
+    picked = back_grid[target, slot_rank]
+    grad_tokens = jnp.sum(
+        picked[:, :quarter].astype(jnp.float32).reshape(tok_rows, top_count, quarter), 1
     ).astype(jnp.bfloat16)
-    pair_lanes = jnp.dot(
-        of_route.astype(jnp.bfloat16), back_rows[:, quarter:], preferred_element_type=jnp.float32
-    )
-    pairing_mine = (pair_lanes[:, 0] + pair_lanes[:, 1]).reshape(tok_rows, top_count)
+    pairing_mine = (
+        picked[:, quarter].astype(jnp.float32) + picked[:, quarter + 1].astype(jnp.float32)
+    ).reshape(tok_rows, top_count)
     grad_logits = (1.0 - affinity) * (
         pairing_mine - weights * jnp.sum(pairing_mine, -1, keepdims=True)
     )

time: 299 us -> 287 us (0.960)
  local copies, waits for them, and re-layouts: 34.1 us -> 27.2 us
  waiting for transfers between devices: 89 us -> 95.1 us
  matrix products: 18.6 us -> 14.5 us
  starting transfers between devices: 44 us -> 40.4 us
    reshape x2, local copies, waits for them, and re-layouts: 6.32 us -> 0.69 us  [layer(): route_half.reshape(devices_ex, capacity, quarter)]
    ppermute x3, waiting for transfers between devices: 13.3 us -> 17.5 us  [dp_sum(): gathered.append(lax.ppermute(reduced, axis, pairs))]
  transfers between devices with their start and end apart: 11 -> 11, of which waited for: 10 -> 10; matrix products, arithmetic and copies ran while one was open for 7% -> 6% of each run, Pallas kernels for 0% -> 0%
where the time goes in v6:
time: 287 us; the launch traced here: 286 us
  blocking collectives  96.8 us (34%)
  waiting for transfers between devices  95.1 us (33%)
  starting transfers between devices  40.4 us (14%)
  local copies, waits for them, and re-layouts  27.2 us (9%)
  matrix products  14.5 us (5%)
  other arithmetic  10.7 us (4%)
    all_to_all x1, blocking collectives, layer(): lax.all_to_all(lane_rows(dispatch), 'expert', split_axis=0, concat_axis=0...  96.8 us
    all_to_all x1, waiting for transfers between devices, layer(): lax.all_to_all(lane_rows(combined), 'expert', split_axis=0, concat_axis=0...  38.9 us
    ppermute x2, waiting for transfers between devices, passed_along(): return lax.ppermute(value, axis, pairs)  24.3 us
    ppermute x3, waiting for transfers between devices, dp_sum(): gathered.append(lax.ppermute(reduced, axis, pairs))  17.5 us
    ppermute x3, waiting for transfers between devices, dp_sum(): lax.ppermute(blocks[(here + step) % count], axis, pairs).astype(jnp.float32)  12.5 us
    ppermute x3, starting transfers between devices, dp_sum(): lax.ppermute(blocks[(here + step) % count], axis, pairs).astype(jnp.float32)  10.1 us
    ppermute x3, starting transfers between devices, dp_sum(): gathered.append(lax.ppermute(reduced, axis, pairs))  10 us
    all_to_all x1, starting transfers between devices, layer(): lax.all_to_all(lane_rows(combined), 'expert', split_axis=0, concat_axis=0...  7.95 us
  transfers between devices with their start and end apart: 11, of which 10 were waited for; matrix products, arithmetic and copies ran while one was open for 6% of the time, Pallas kernels for 0%

profile of v6, /device:TPU:1, one launch (start us, length us, event | category | flops | bytes accessed | tf_op | source)
XLA Modules:
  0.0 286.1 jit_solution(8033340746400388198)
XLA Ops:
  3.6 1.9 gather_fusion
  7.5 1.8 convolution_convert_fusion
  10.8 96.8 %all_to_all.10 = bf16[128,42,128]{2,1,0:T(8,128)(2,1)S(1)} all-to-all(bf16[128,42,128]{2,1,0:T(8,128)(2,1)S(1)} %reshape_reshape.3), channel_id=1, replica_groups=mesh['expert'=128,'dp'=4] {'expert'}, dimensions={0} | all-to-all | bytes 2752512 | tf_op jit(solution)/shard_map/all_to_all | solution.py:101
  109.1 3.0 %collective-permute-start = (bf16[128,6,896]{0,2,1:T(8,128)(2,1)S(1)}, bf16[128,6,896]{0,2,1:T(8,128)(2,1)}, u32[]{:S(2)}, u32[]{:S(2)}) collective-permute-start(bf16[128,6,896]{0,2,1:T(8,128)(2,1)S(1)} %bitcast.54), channel_id=1, source_target_pairs={{0,4},{4,0},{8,12},{12,8},{16,20},{20,16},{24,28},{28,24},{32,36},... | collective-permute-start | bytes 4128776 | tf_op jit(solution)/shard_map/ppermute | solution.py:16
  112.1 4.7 %collective-permute-start.1 = (bf16[896,512]{1,0:T(8,128)(2,1)}, bf16[896,512]{1,0:T(8,128)(2,1)}, u32[]{:S(2)}, u32[]{:S(2)}) collective-permute-start(bf16[896,512]{1,0:T(8,128)(2,1)} %param.12), channel_id=1, source_target_pairs={{0,256},{4,260},{8,264},{12,268},{16,272},{20,276},{24,280},{28,28... | collective-permute-start | bytes 2752520 | tf_op jit(solution)/shard_map/ppermute | solution.py:10
  116.9 2.1 collective-permute-start.2
  119.6 2.6 broadcast_select_fusion.1
  122.2 3.1 %copy.63 = bf16[128,6,896]{2,1,0:T(8,128)(2,1)S(1)} copy(bf16[128,6,896]{0,2,1:T(8,128)(2,1)} %get-tuple-element.24) | data formatting | bytes 2752512 | tf_op jit(solution)/shard_map/jit(_where)/select_n | solution.py:105
  126.6 2.0 copy.64
  130.0 7.7 %collective-permute-done.1 = bf16[896,512]{1,0:T(8,128)(2,1)} collective-permute-done((bf16[896,512]{1,0:T(8,128)(2,1)}, bf16[896,512]{1,0:T(8,128)(2,1)}, u32[]{:S(2)}, u32[]{:S(2)}) %collective-permute-start.1) | collective-permute-done | bytes 917536 | tf_op jit(solution)/shard_map/ppermute | solution.py:10
  137.7 3.1 %convolution_convert_fusion.5 = bf16[768,512]{0,1:T(8,128)(2,1)S(1)} fusion(bf16[768,896]{1,0:T(8,128)(2,1)S(1)} %copy-done.2, bf16[896,512]{1,0:T(8,128)(2,1)} %collective-permute-done.1, bf16[896,512]{1,0:T(8,128)(2,1)} %param.12, pred[]{:T(512)} %bitcast.3), kind=kOutput, calls=%fused_computation.18 | convolution fusion | flops 705495040 | bytes 3997697 | tf_op jit(solution)/shard_map/dot_general | solution.py:108
  140.8 16.6 %collective-permute-done.2 = bf16[896,512]{1,0:T(8,128)(2,1)} collective-permute-done((bf16[896,512]{1,0:T(8,128)(2,1)}, bf16[896,512]{1,0:T(8,128)(2,1)}, u32[]{:S(2)}, u32[]{:S(2)}) %collective-permute-start.2) | collective-permute-done | bytes 917536 | tf_op jit(solution)/shard_map/ppermute | solution.py:10
  157.4 3.0 %convolution_convert_fusion.4 = bf16[768,512]{0,1:T(8,128)(2,1)S(1)} fusion(bf16[768,896]{1,0:T(8,128)(2,1)S(1)} %copy-done.4, bf16[896,512]{1,0:T(8,128)(2,1)} %collective-permute-done.2, bf16[896,512]{1,0:T(8,128)(2,1)S(1)} %copy-done.10, pred[]{:T(512)} %bitcast.3), kind=kOutput, calls=%fused_computation.17 | convolution fusion | flops 705495040 | bytes 3997697 | tf_op jit(solution)/shard_map/dot_general | solution.py:109
  161.4 3.2 %collective-permute-start.3 = (bf16[192,1024]{1,0:T(8,128)(2,1)S(1)}, bf16[192,1024]{1,0:T(8,128)(2,1)S(1)}, u32[]{:S(2)}, u32[]{:S(2)}) collective-permute-start(bf16[192,1024]{1,0:T(8,128)(2,1)S(1)} %get-tuple-element.26), channel_id=1, source_target_pairs={{0,1},{1,2},{2,3},{3,0},{4,5},{5,6},{6,7},{7,4},{8,9},{9,10},{10,1... | collective-permute-start | bytes 1179656 | tf_op jit(solution)/shard_map/ppermute | solution.py:27
  164.6 3.4 %collective-permute-start.5 = (bf16[192,1024]{1,0:T(8,128)(2,1)S(1)}, bf16[192,1024]{1,0:T(8,128)(2,1)}, u32[]{:S(2)}, u32[]{:S(2)}) collective-permute-start(bf16[192,1024]{1,0:T(8,128)(2,1)S(1)} %get-tuple-element.27), channel_id=1, source_target_pairs={{0,3},{1,0},{2,1},{3,2},{4,7},{5,4},{6,5},{7,6},{8,11},{9,8},{10,9... | collective-permute-start | bytes 1179656 | tf_op jit(solution)/shard_map/ppermute | solution.py:27
  167.9 3.5 %collective-permute-start.4 = (bf16[192,1024]{1,0:T(8,128)(2,1)S(1)}, bf16[192,1024]{1,0:T(8,128)(2,1)}, u32[]{:S(2)}, u32[]{:S(2)}) collective-permute-start(bf16[192,1024]{1,0:T(8,128)(2,1)S(1)} %get-tuple-element.28), channel_id=1, source_target_pairs={{0,2},{1,3},{2,0},{3,1},{4,6},{5,7},{6,4},{7,5},{8,10},{9,11},{10,... | collective-permute-start | bytes 1179656 | tf_op jit(solution)/shard_map/ppermute | solution.py:27
  171.5 2.9 %collective-permute-done.3 = bf16[192,1024]{1,0:T(8,128)(2,1)S(1)} collective-permute-done((bf16[192,1024]{1,0:T(8,128)(2,1)S(1)}, bf16[192,1024]{1,0:T(8,128)(2,1)S(1)}, u32[]{:S(2)}, u32[]{:S(2)}) %collective-permute-start.3) | collective-permute-done | bytes 393248 | tf_op jit(solution)/shard_map/ppermute | solution.py:27
  176.1 7.9 %collective-permute-done.4 = bf16[192,1024]{1,0:T(8,128)(2,1)} collective-permute-done((bf16[192,1024]{1,0:T(8,128)(2,1)S(1)}, bf16[192,1024]{1,0:T(8,128)(2,1)}, u32[]{:S(2)}, u32[]{:S(2)}) %collective-permute-start.4) | collective-permute-done | bytes 393248 | tf_op jit(solution)/shard_map/ppermute | solution.py:27
  185.4 4.9 %collective-permute-start.8 = (bf16[192,1024]{1,0:T(8,128)(2,1)S(1)}, bf16[192,1024]{1,0:T(8,128)(2,1)S(1)}, u32[]{:S(2)}, u32[]{:S(2)}) collective-permute-start(bf16[192,1024]{1,0:T(8,128)(2,1)S(1)} %fusion.8), channel_id=1, source_target_pairs={{0,3},{1,0},{2,1},{3,2},{4,7},{5,4},{6,5},{7,6},{8,11},{9,8},{10,9... | collective-permute-start | bytes 1179656 | tf_op jit(solution)/shard_map/ppermute | solution.py:34
  190.3 3.2 %collective-permute-start.7 = (bf16[192,1024]{1,0:T(8,128)(2,1)S(1)}, bf16[192,1024]{1,0:T(8,128)(2,1)S(1)}, u32[]{:S(2)}, u32[]{:S(2)}) collective-permute-start(bf16[192,1024]{1,0:T(8,128)(2,1)S(1)} %fusion.8), channel_id=1, source_target_pairs={{0,2},{1,3},{2,0},{3,1},{4,6},{5,7},{6,4},{7,5},{8,10},{9,11},{10,... | collective-permute-start | bytes 1179656 | tf_op jit(solution)/shard_map/ppermute | solution.py:34
  193.5 1.9 collective-permute-start.6
  197.3 4.7 %collective-permute-done.7 = bf16[192,1024]{1,0:T(8,128)(2,1)S(1)} collective-permute-done((bf16[192,1024]{1,0:T(8,128)(2,1)S(1)}, bf16[192,1024]{1,0:T(8,128)(2,1)S(1)}, u32[]{:S(2)}, u32[]{:S(2)}) %collective-permute-start.7) | collective-permute-done | bytes 393248 | tf_op jit(solution)/shard_map/ppermute | solution.py:34
  201.9 11.1 %collective-permute-done.6 = bf16[192,1024]{1,0:T(8,128)(2,1)S(1)} collective-permute-done((bf16[192,1024]{1,0:T(8,128)(2,1)S(1)}, bf16[192,1024]{1,0:T(8,128)(2,1)S(1)}, u32[]{:S(2)}, u32[]{:S(2)}) %collective-permute-start.6) | collective-permute-done | bytes 393248 | tf_op jit(solution)/shard_map/ppermute | solution.py:34
  216.9 2.8 convolution_convert_fusion.1
  220.9 2.6 collective-permute-start.9
  223.4 1.9 collective-permute-done.9
  227.3 7.9 %all-to-all-start.1 = ((bf16[128,24,128]{2,1,0:T(8,128)(2,1)}), bf16[128,24,128]{2,1,0:T(8,128)(2,1)S(1)}, u32[]{:S(2)}, u32[]{:S(2)}) async-start(bf16[128,24,128]{2,1,0:T(8,128)(2,1)} %copy.69), calls=%async_computation.1 | async-start | bytes 1572864 | tf_op jit(solution)/shard_map/all_to_all | solution.py:142
  235.3 1.8 convolution_convert_fusion.3
  237.9 1.9 convolution_convert_fusion.2
  239.8 38.9 %all-to-all-done.1 = bf16[128,24,128]{2,1,0:T(8,128)(2,1)S(1)} async-done(((bf16[128,24,128]{2,1,0:T(8,128)(2,1)}), bf16[128,24,128]{2,1,0:T(8,128)(2,1)S(1)}, u32[]{:S(2)}, u32[]{:S(2)}) %all-to-all-start.1) | async-done | bytes 786464 | tf_op jit(solution)/shard_map/all_to_all | solution.py:142
  280.0 2.7 gather_fusion.2
  284.2 1.9 reduce
  (87 shorter events, 27.3 us)
Async XLA Ops:
  0.6 5.2 %copy-start.9 = (f32[128,2]{0,1:T(2,128)S(1)}, f32[128,2]{0,1:T(2,128)}, u32[]{:S(2)}) copy-start(f32[128,2]{0,1:T(2,128)} %param.9) | copy-start | bytes 3076
  0.6 5.9 %copy-start.8 = (bf16[128,896]{1,0:T(8,128)(2,1)S(1)}, bf16[128,896]{1,0:T(8,128)(2,1)}, u32[]{:S(2)}) copy-start(bf16[128,896]{1,0:T(8,128)(2,1)} %param.10) | copy-start | bytes 688132
  109.1 10.5 %collective-permute-start = (bf16[128,6,896]{0,2,1:T(8,128)(2,1)S(1)}, bf16[128,6,896]{0,2,1:T(8,128)(2,1)}, u32[]{:S(2)}, u32[]{:S(2)}) collective-permute-start(bf16[128,6,896]{0,2,1:T(8,128)(2,1)S(1)} %bitcast.54), channel_id=1, source_target_pairs={{0,4},{4,0},{8,12},{12,8},{16,20},{20,16},{24,28},{28,24},{32,36},... | collective-permute-start | bytes 4128776 | tf_op jit(solution)/shard_map/ppermute | solution.py:16
  112.1 25.6 %collective-permute-start.1 = (bf16[896,512]{1,0:T(8,128)(2,1)}, bf16[896,512]{1,0:T(8,128)(2,1)}, u32[]{:S(2)}, u32[]{:S(2)}) collective-permute-start(bf16[896,512]{1,0:T(8,128)(2,1)} %param.12), channel_id=1, source_target_pairs={{0,256},{4,260},{8,264},{12,268},{16,272},{20,276},{24,280},{28,28... | collective-permute-start | bytes 2752520 | tf_op jit(solution)/shard_map/ppermute | solution.py:10
  116.9 40.5 %collective-permute-start.2 = (bf16[896,512]{1,0:T(8,128)(2,1)}, bf16[896,512]{1,0:T(8,128)(2,1)}, u32[]{:S(2)}, u32[]{:S(2)}) collective-permute-start(bf16[896,512]{1,0:T(8,128)(2,1)} %param.13), channel_id=1, source_target_pairs={{0,256},{4,260},{8,264},{12,268},{16,272},{20,276},{24,280},{28,28... | collective-permute-start | bytes 2752520 | tf_op jit(solution)/shard_map/ppermute | solution.py:10
  128.6 9.1 %copy-start.2 = (bf16[768,896]{1,0:T(8,128)(2,1)S(1)}, bf16[768,896]{1,0:T(8,128)(2,1)}, u32[]{:S(2)}) copy-start(bf16[768,896]{1,0:T(8,128)(2,1)} %reshape.225) | copy-start | bytes 4128772
  137.7 19.7 %copy-start.4 = (bf16[768,896]{1,0:T(8,128)(2,1)S(1)}, bf16[768,896]{1,0:T(8,128)(2,1)}, u32[]{:S(2)}) copy-start(bf16[768,896]{1,0:T(8,128)(2,1)} %reshape.226) | copy-start | bytes 4128772
  137.7 19.7 %copy-start.10 = (bf16[896,512]{1,0:T(8,128)(2,1)S(1)}, bf16[896,512]{1,0:T(8,128)(2,1)}, u32[]{:S(2)}) copy-start(bf16[896,512]{1,0:T(8,128)(2,1)} %param.13) | copy-start | bytes 2752516
  161.4 13.0 %collective-permute-start.3 = (bf16[192,1024]{1,0:T(8,128)(2,1)S(1)}, bf16[192,1024]{1,0:T(8,128)(2,1)S(1)}, u32[]{:S(2)}, u32[]{:S(2)}) collective-permute-start(bf16[192,1024]{1,0:T(8,128)(2,1)S(1)} %get-tuple-element.26), channel_id=1, source_target_pairs={{0,1},{1,2},{2,3},{3,0},{4,5},{5,6},{6,7},{7,4},{8,9},{9,10},{10,1... | collective-permute-start | bytes 1179656 | tf_op jit(solution)/shard_map/ppermute | solution.py:27
  164.6 11.6 %collective-permute-start.5 = (bf16[192,1024]{1,0:T(8,128)(2,1)S(1)}, bf16[192,1024]{1,0:T(8,128)(2,1)}, u32[]{:S(2)}, u32[]{:S(2)}) collective-permute-start(bf16[192,1024]{1,0:T(8,128)(2,1)S(1)} %get-tuple-element.27), channel_id=1, source_target_pairs={{0,3},{1,0},{2,1},{3,2},{4,7},{5,4},{6,5},{7,6},{8,11},{9,8},{10,9... | collective-permute-start | bytes 1179656 | tf_op jit(solution)/shard_map/ppermute | solution.py:27
  167.9 16.1 %collective-permute-start.4 = (bf16[192,1024]{1,0:T(8,128)(2,1)S(1)}, bf16[192,1024]{1,0:T(8,128)(2,1)}, u32[]{:S(2)}, u32[]{:S(2)}) collective-permute-start(bf16[192,1024]{1,0:T(8,128)(2,1)S(1)} %get-tuple-element.28), channel_id=1, source_target_pairs={{0,2},{1,3},{2,0},{3,1},{4,6},{5,7},{6,4},{7,5},{8,10},{9,11},{10,... | collective-permute-start | bytes 1179656 | tf_op jit(solution)/shard_map/ppermute | solution.py:27
  185.4 11.9 %collective-permute-start.8 = (bf16[192,1024]{1,0:T(8,128)(2,1)S(1)}, bf16[192,1024]{1,0:T(8,128)(2,1)S(1)}, u32[]{:S(2)}, u32[]{:S(2)}) collective-permute-start(bf16[192,1024]{1,0:T(8,128)(2,1)S(1)} %fusion.8), channel_id=1, source_target_pairs={{0,3},{1,0},{2,1},{3,2},{4,7},{5,4},{6,5},{7,6},{8,11},{9,8},{10,9... | collective-permute-start | bytes 1179656 | tf_op jit(solution)/shard_map/ppermute | solution.py:34
  190.3 11.6 %collective-permute-start.7 = (bf16[192,1024]{1,0:T(8,128)(2,1)S(1)}, bf16[192,1024]{1,0:T(8,128)(2,1)S(1)}, u32[]{:S(2)}, u32[]{:S(2)}) collective-permute-start(bf16[192,1024]{1,0:T(8,128)(2,1)S(1)} %fusion.8), channel_id=1, source_target_pairs={{0,2},{1,3},{2,0},{3,1},{4,6},{5,7},{6,4},{7,5},{8,10},{9,11},{10,... | collective-permute-start | bytes 1179656 | tf_op jit(solution)/shard_map/ppermute | solution.py:34
  193.5 19.5 %collective-permute-start.6 = (bf16[192,1024]{1,0:T(8,128)(2,1)S(1)}, bf16[192,1024]{1,0:T(8,128)(2,1)S(1)}, u32[]{:S(2)}, u32[]{:S(2)}) collective-permute-start(bf16[192,1024]{1,0:T(8,128)(2,1)S(1)} %fusion.8), channel_id=1, source_target_pairs={{0,1},{1,2},{2,3},{3,0},{4,5},{5,6},{6,7},{7,4},{8,9},{9,10},{10,1... | collective-permute-start | bytes 1179656 | tf_op jit(solution)/shard_map/ppermute | solution.py:34
  214.3 1.7 copy-start
  214.3 2.6 copy-start.11
  216.0 0.9 copy-start.6
  220.9 4.5 %collective-permute-start.9 = (bf16[128,3,1024]{2,0,1:T(8,128)(2,1)S(1)}, bf16[128,3,1024]{2,0,1:T(8,128)(2,1)S(1)}, u32[]{:S(2)}, u32[]{:S(2)}) collective-permute-start(bf16[128,3,1024]{2,0,1:T(8,128)(2,1)S(1)} %broadcast_select_fusion.3), channel_id=1, source_target_pairs={{0,4},{4,0},{8,12},{12,8},{16,20},{20,16},{24,28},{28,24},{32,36},... | collective-permute-start | bytes 2359304 | tf_op jit(solution)/shard_map/ppermute | solution.py:16
  226.0 9.3 %copy-start.3 = (bf16[768,896]{1,0:T(8,128)(2,1)S(1)}, bf16[768,896]{1,0:T(8,128)(2,1)}, u32[]{:S(2)}) copy-start(bf16[768,896]{1,0:T(8,128)(2,1)} %reshape.225) | copy-start | bytes 4128772
  226.0 9.3 %copy-start.7 = (bf16[768,512]{1,0:T(8,128)(2,1)S(1)}, bf16[768,512]{1,0:T(8,128)(2,1)}, u32[]{:S(2)}) copy-start(bf16[768,512]{1,0:T(8,128)(2,1)} %copy-done.6) | copy-start | bytes 2359300
  227.3 51.4 %all-to-all-start.1 = ((bf16[128,24,128]{2,1,0:T(8,128)(2,1)}), bf16[128,24,128]{2,1,0:T(8,128)(2,1)S(1)}, u32[]{:S(2)}, u32[]{:S(2)}) async-start(bf16[128,24,128]{2,1,0:T(8,128)(2,1)} %copy.69), calls=%async_computation.1 | async-start | bytes 1572864 | tf_op jit(solution)/shard_map/all_to_all | solution.py:142
  235.3 1.9 copy-start.1
  235.3 2.6 copy-start.5

commit v7 on v6

--- a/solution.py
+++ b/solution.py
@@ -42,15 +42,6 @@
     return value.reshape(count, -1, 128)
 
 
-def pick_pair(swapped_here, theirs, ours):
-    return tuple(
-        (
-            jnp.where(swapped_here, other_part, mine_part)
-            for other_part, mine_part in zip(theirs, ours)
-        )
-    )
-
-
 def activate(up_pre, grad_hidden):
     up_sig = jax.nn.sigmoid(up_pre)
     hidden = (up_pre * up_sig).astype(jnp.bfloat16)
@@ -82,12 +73,15 @@
     flat_routes = routes.reshape(-1)
     onehot = (flat_routes[:, None] == expert_ids[None, :]).astype(jnp.int32)
     slot_rank = jnp.sum(jnp.cumsum(onehot, 0) * onehot, 1) - 1
-    own_weights = (w_up, w_down)
-    shifted = passed_along((w_up, w_down), "expert", devices_ex // 2)
-    resident = pick_pair(swapped_here, shifted, own_weights)
+    width = w_up.shape[1]
+    own_weights = jnp.concatenate([w_up, w_down], axis=1)
+    shifted = passed_along(own_weights, "expert", devices_ex // 2)
+    resident_both = jnp.where(swapped_here, shifted, own_weights)
+    resident = (resident_both[:, :width], resident_both[:, width:])
     target = owner_slot[flat_routes]
-    token_pos = (2 * target * capacity + slot_rank).reshape(tok_rows, top_count)
-    scaled_pos = (2 * target + 1) * capacity + slot_rank
+    lead = ((2 * target + slot_rank // share) * 2) * share + slot_rank % share
+    token_pos = lead.reshape(tok_rows, top_count)
+    scaled_pos = lead + share
     row_ids = jnp.arange(devices_ex * capacity, dtype=jnp.int32)[:, None]
     pick_token = jnp.any(row_ids[:, :, None] == token_pos[None, :, :], -1)
     pick_scaled = row_ids == scaled_pos[None, :]
@@ -100,10 +94,10 @@
     )
     got = lax.all_to_all(
         lane_rows(dispatch), "expert", split_axis=0, concat_axis=0, tiled=True
-    ).reshape(devices_ex, capacity, quarter)
+    ).reshape(devices_ex, 2, share, quarter)
     partner_got = core_swap(got, "expert")
-    routed_rows = jnp.where(first_core, got, partner_got).reshape(-1, quarter)
-    scaled_rows = jnp.where(first_core, partner_got, got).reshape(-1, quarter)
+    routed_rows = jnp.stack([got[:, 0], partner_got[:, 0]]).reshape(-1, quarter)
+    scaled_rows = jnp.stack([got[:, 1], partner_got[:, 1]]).reshape(-1, quarter)
     up_block, down_block = resident
     up_part = jnp.dot(routed_rows, up_block, preferred_element_type=jnp.float32)
     grad_part = jnp.dot(scaled_rows, down_block, preferred_element_type=jnp.float32)
@@ -127,16 +121,14 @@
     lane_ids = jnp.arange(lanes, dtype=jnp.int32)
     my_lane = jnp.where(first_core, 0, 1)
     pair_cols = jnp.where(
-        lane_ids[None, None, :] == my_lane,
-        pairing_half.reshape(devices_ex, capacity, 1),
+        lane_ids[None, None, None, :] == my_lane,
+        pairing_half.reshape(2, devices_ex, share, 1),
         jnp.zeros((), jnp.bfloat16),
     )
     packed = jnp.concatenate(
-        [route_half.reshape(devices_ex, capacity, quarter), pair_cols], axis=-1
+        [route_half.reshape(2, devices_ex, share, quarter), pair_cols], axis=-1
     )
-    low, high = packed[:, :share], packed[:, share:]
-    keep = jnp.where(first_core, low, high)
-    give = jnp.where(first_core, high, low)
+    keep, give = packed[0], packed[1]
     taken = core_swap(give, "expert")
     combined = (keep.astype(jnp.float32) + taken.astype(jnp.float32)).astype(jnp.bfloat16)
     back = lax.all_to_all(

time: 287 us -> 259 us (0.902)
  blocking collectives: 96.8 us -> 0 us
  waiting for transfers between devices: 95.1 us -> 141 us
  starting transfers between devices: 40.4 us -> 59.2 us
  local copies, waits for them, and re-layouts: 27.2 us -> 33.7 us
  matrix products: 14.5 us -> 9.46 us
    all_to_all x1 -> x0, blocking collectives: 96.8 us -> none  [layer(): lax.all_to_all(lane_rows(dispatch), 'expert', split_axis=0, concat_axis=0...]
    all_to_all x0 -> x1, waiting for transfers between devices: none -> 68.9 us  [layer(): lax.all_to_all(lane_rows(dispatch), 'expert', split_axis=0, concat_axis=0...]
    ppermute x2 -> x1, waiting for transfers between devices: 24.3 us -> 0.01 us  [passed_along(): return lax.ppermute(value, axis, pairs)]
    all_to_all x0 -> x1, starting transfers between devices: none -> 20.5 us  [layer(): lax.all_to_all(lane_rows(dispatch), 'expert', split_axis=0, concat_axis=0...]
    another operation x1 -> x5, local copies, waits for them, and re-layouts: 0.01 us -> 5.99 us  [the longest x3 3.59 us: layer(): routed_rows = jnp.stack([got[:, 0], partner_got[:, 0]]).reshape(-1, quarter)]
    select_n x2 -> x0, local copies, waits for them, and re-layouts: 5.09 us -> none  [the longest x1 3.08 us: layer(): routed_rows = jnp.where(first_core, got, partner_got).reshape(-1, quarter)]
    unnamed x27 -> x34, local copies, waits for them, and re-layouts: 3.88 us -> 5.9 us
    ppermute x2 -> x1, starting transfers between devices: 6.79 us -> 5.08 us  [passed_along(): return lax.ppermute(value, axis, pairs)]
  transfers between devices with their start and end apart: 11 -> 11, of which waited for: 10 -> 9; matrix products, arithmetic and copies ran while one was open for 6% -> 5% of each run, Pallas kernels for 0% -> 0%
where the time goes in v7:
time: 259 us; the launch traced here: 257 us
  waiting for transfers between devices  141 us (54%)
  starting transfers between devices  59.2 us (23%)
  local copies, waits for them, and re-layouts  33.7 us (13%)
  other arithmetic  13 us (5%)
  matrix products  9.46 us (4%)
    all_to_all x1, waiting for transfers between devices, layer(): lax.all_to_all(lane_rows(dispatch), 'expert', split_axis=0, concat_axis=0...  68.9 us
    all_to_all x1, waiting for transfers between devices, layer(): lax.all_to_all(lane_rows(combined), 'expert', split_axis=0, concat_axis=0...  38.9 us
    all_to_all x1, starting transfers between devices, layer(): lax.all_to_all(lane_rows(dispatch), 'expert', split_axis=0, concat_axis=0...  20.5 us
    ppermute x3, waiting for transfers between devices, dp_sum(): gathered.append(lax.ppermute(reduced, axis, pairs))  17.6 us
    ppermute x3, waiting for transfers between devices, dp_sum(): lax.ppermute(blocks[(here + step) % count], axis, pairs).astype(jnp.float32)  13.4 us
    ppermute x3, starting transfers between devices, dp_sum(): lax.ppermute(blocks[(here + step) % count], axis, pairs).astype(jnp.float32)  10.1 us
    ppermute x3, starting transfers between devices, dp_sum(): gathered.append(lax.ppermute(reduced, axis, pairs))  10 us
    all_to_all x1, starting transfers between devices, layer(): lax.all_to_all(lane_rows(combined), 'expert', split_axis=0, concat_axis=0...  7.93 us
  transfers between devices with their start and end apart: 11, of which 9 were waited for; matrix products, arithmetic and copies ran while one was open for 5% of the time, Pallas kernels for 0%

profile of v7, /device:TPU:1, one launch (start us, length us, event | category | flops | bytes accessed | tf_op | source)
XLA Modules:
  0.0 257.5 jit_solution(16400954167446631096)
XLA Ops:
  3.7 1.9 gather_fusion
  9.1 2.3 reshape_reshape.3
  11.4 20.5 %all-to-all-start = ((bf16[128,42,128]{2,1,0:T(8,128)(2,1)}), bf16[128,42,128]{2,1,0:T(8,128)(2,1)S(1)}, u32[]{:S(2)}, u32[]{:S(2)}) async-start(bf16[128,42,128]{2,1,0:T(8,128)(2,1)} %reshape_reshape.3), calls=%async_computation | async-start | bytes 3145728 | tf_op jit(solution)/shard_map/all_to_all | solution.py:95
  34.6 5.1 %collective-permute-start.1 = (bf16[896,1024]{1,0:T(8,128)(2,1)}, bf16[896,1024]{1,0:T(8,128)(2,1)}, u32[]{:S(2)}, u32[]{:S(2)}) collective-permute-start(bf16[896,1024]{1,0:T(8,128)(2,1)} %constant_dynamic-update-slice_fusion), channel_id=1, source_target_pairs={{0,256},{4,260},{8,264},{12,268},{16,272},{20,276},{24,280},{28,28... | collective-permute-start | bytes 5505032 | tf_op jit(solution)/shard_map/ppermute | solution.py:10
  39.7 68.9 %all-to-all-done = bf16[128,42,128]{2,1,0:T(8,128)(2,1)S(1)} async-done(((bf16[128,42,128]{2,1,0:T(8,128)(2,1)}), bf16[128,42,128]{2,1,0:T(8,128)(2,1)S(1)}, u32[]{:S(2)}, u32[]{:S(2)}) %all-to-all-start) | async-done | bytes 1376288 | tf_op jit(solution)/shard_map/all_to_all | solution.py:95
  108.6 1.4 copy.64
  110.1 3.2 %collective-permute-start = (bf16[128,2,3,896]{0,3,2,1:T(8,128)(2,1)S(1)}, bf16[128,2,3,896]{0,3,2,1:T(8,128)(2,1)S(1)}, u32[]{:S(2)}, u32[]{:S(2)}) collective-permute-start(bf16[128,2,3,896]{0,3,2,1:T(8,128)(2,1)S(1)} %bitcast.66), channel_id=1, source_target_pairs={{0,4},{4,0},{8,12},{12,8},{16,20},{20,16},{24,28},{28,24},{32,36},... | collective-permute-start | bytes 4128776 | tf_op jit(solution)/shard_map/ppermute | solution.py:16
  113.9 3.6 %broadcast_select_fusion = bf16[896,1024]{1,0:T(8,128)(2,1)} fusion(bf16[896,1024]{1,0:T(8,128)(2,1)} %collective-permute-done.1, bf16[896,1024]{1,0:T(8,128)(2,1)} %constant_dynamic-update-slice_fusion, pred[]{:T(512)} %bitcast.5), kind=kLoop, calls=%fused_computation.3 | loop fusion | flops 917504 | bytes 5505025 | tf_op jit(solution)/shard_map/jit(_where)/select_n | solution.py:79
  119.0 3.4 %copy.65 = bf16[2,128,3,896]{3,2,1,0:T(4,128)(2,1)S(1)} copy(bf16[2,128,3,896]{1,3,2,0:T(8,128)(2,1)} %get-tuple-element.37) | data formatting | bytes 2752512 | tf_op jit(solution)/shard_map/stack | solution.py:99
  122.5 2.4 reshape.260
  124.8 2.4 copy.66
  128.5 2.7 %convolution_convert_fusion.4 = bf16[768,512]{0,1:T(8,128)(2,1)S(1)} fusion(bf16[768,896]{1,0:T(8,128)(2,1)S(1)} %reshape.261, bf16[896,1024]{1,0:T(8,128)(2,1)} %broadcast_select_fusion), kind=kOutput, calls=%fused_computation.19 | convolution fusion | flops 705036288 | bytes 3080192 | tf_op jit(solution)/shard_map/dot_general | solution.py:103
  133.3 3.2 %collective-permute-start.2 = (bf16[192,1024]{1,0:T(8,128)(2,1)S(1)}, bf16[192,1024]{1,0:T(8,128)(2,1)S(1)}, u32[]{:S(2)}, u32[]{:S(2)}) collective-permute-start(bf16[192,1024]{1,0:T(8,128)(2,1)S(1)} %get-tuple-element.24), channel_id=1, source_target_pairs={{0,1},{1,2},{2,3},{3,0},{4,5},{5,6},{6,7},{7,4},{8,9},{9,10},{10,1... | collective-permute-start | bytes 1179656 | tf_op jit(solution)/shard_map/ppermute | solution.py:27
  136.5 3.4 %collective-permute-start.4 = (bf16[192,1024]{1,0:T(8,128)(2,1)S(1)}, bf16[192,1024]{1,0:T(8,128)(2,1)}, u32[]{:S(2)}, u32[]{:S(2)}) collective-permute-start(bf16[192,1024]{1,0:T(8,128)(2,1)S(1)} %get-tuple-element.25), channel_id=1, source_target_pairs={{0,3},{1,0},{2,1},{3,2},{4,7},{5,4},{6,5},{7,6},{8,11},{9,8},{10,9... | collective-permute-start | bytes 1179656 | tf_op jit(solution)/shard_map/ppermute | solution.py:27
  139.9 3.5 %collective-permute-start.3 = (bf16[192,1024]{1,0:T(8,128)(2,1)S(1)}, bf16[192,1024]{1,0:T(8,128)(2,1)}, u32[]{:S(2)}, u32[]{:S(2)}) collective-permute-start(bf16[192,1024]{1,0:T(8,128)(2,1)S(1)} %get-tuple-element.26), channel_id=1, source_target_pairs={{0,2},{1,3},{2,0},{3,1},{4,6},{5,7},{6,4},{7,5},{8,10},{9,11},{10,... | collective-permute-start | bytes 1179656 | tf_op jit(solution)/shard_map/ppermute | solution.py:27
  143.4 3.8 %collective-permute-done.2 = bf16[192,1024]{1,0:T(8,128)(2,1)S(1)} collective-permute-done((bf16[192,1024]{1,0:T(8,128)(2,1)S(1)}, bf16[192,1024]{1,0:T(8,128)(2,1)S(1)}, u32[]{:S(2)}, u32[]{:S(2)}) %collective-permute-start.2) | collective-permute-done | bytes 393248 | tf_op jit(solution)/shard_map/ppermute | solution.py:27
  147.2 1.7 collective-permute-done.4
  148.9 7.9 %collective-permute-done.3 = bf16[192,1024]{1,0:T(8,128)(2,1)} collective-permute-done((bf16[192,1024]{1,0:T(8,128)(2,1)S(1)}, bf16[192,1024]{1,0:T(8,128)(2,1)}, u32[]{:S(2)}, u32[]{:S(2)}) %collective-permute-start.3) | collective-permute-done | bytes 393248 | tf_op jit(solution)/shard_map/ppermute | solution.py:27
  158.2 4.8 %collective-permute-start.7 = (bf16[192,1024]{1,0:T(8,128)(2,1)S(1)}, bf16[192,1024]{1,0:T(8,128)(2,1)S(1)}, u32[]{:S(2)}, u32[]{:S(2)}) collective-permute-start(bf16[192,1024]{1,0:T(8,128)(2,1)S(1)} %fusion.12), channel_id=1, source_target_pairs={{0,3},{1,0},{2,1},{3,2},{4,7},{5,4},{6,5},{7,6},{8,11},{9,8},{10,9... | collective-permute-start | bytes 1179656 | tf_op jit(solution)/shard_map/ppermute | solution.py:34
  163.0 3.3 %collective-permute-start.6 = (bf16[192,1024]{1,0:T(8,128)(2,1)S(1)}, bf16[192,1024]{1,0:T(8,128)(2,1)S(1)}, u32[]{:S(2)}, u32[]{:S(2)}) collective-permute-start(bf16[192,1024]{1,0:T(8,128)(2,1)S(1)} %fusion.12), channel_id=1, source_target_pairs={{0,2},{1,3},{2,0},{3,1},{4,6},{5,7},{6,4},{7,5},{8,10},{9,11},{10,... | collective-permute-start | bytes 1179656 | tf_op jit(solution)/shard_map/ppermute | solution.py:34
  166.3 1.9 collective-permute-start.5
  168.3 2.6 %collective-permute-done.7 = bf16[192,1024]{1,0:T(8,128)(2,1)S(1)} collective-permute-done((bf16[192,1024]{1,0:T(8,128)(2,1)S(1)}, bf16[192,1024]{1,0:T(8,128)(2,1)S(1)}, u32[]{:S(2)}, u32[]{:S(2)}) %collective-permute-start.7) | collective-permute-done | bytes 393248 | tf_op jit(solution)/shard_map/ppermute | solution.py:34
  171.0 4.5 %collective-permute-done.6 = bf16[192,1024]{1,0:T(8,128)(2,1)S(1)} collective-permute-done((bf16[192,1024]{1,0:T(8,128)(2,1)S(1)}, bf16[192,1024]{1,0:T(8,128)(2,1)S(1)}, u32[]{:S(2)}, u32[]{:S(2)}) %collective-permute-start.6) | collective-permute-done | bytes 393248 | tf_op jit(solution)/shard_map/ppermute | solution.py:34
  175.5 10.4 %collective-permute-done.5 = bf16[192,1024]{1,0:T(8,128)(2,1)S(1)} collective-permute-done((bf16[192,1024]{1,0:T(8,128)(2,1)S(1)}, bf16[192,1024]{1,0:T(8,128)(2,1)S(1)}, u32[]{:S(2)}, u32[]{:S(2)}) %collective-permute-start.5) | collective-permute-done | bytes 393248 | tf_op jit(solution)/shard_map/ppermute | solution.py:34
  192.5 2.4 collective-permute-start.8
  194.9 1.9 collective-permute-done.8
  198.7 7.9 %all-to-all-start.1 = ((bf16[128,24,128]{2,1,0:T(8,128)(2,1)}), bf16[128,24,128]{2,1,0:T(8,128)(2,1)S(1)}, u32[]{:S(2)}, u32[]{:S(2)}) async-start(bf16[128,24,128]{2,1,0:T(8,128)(2,1)} %copy.71), calls=%async_computation.1 | async-start | bytes 1572864 | tf_op jit(solution)/shard_map/all_to_all | solution.py:134
  206.7 1.8 convolution_convert_fusion.3
  209.3 1.9 convolution_convert_fusion.2
  211.2 38.9 %all-to-all-done.1 = bf16[128,24,128]{2,1,0:T(8,128)(2,1)S(1)} async-done(((bf16[128,24,128]{2,1,0:T(8,128)(2,1)}), bf16[128,24,128]{2,1,0:T(8,128)(2,1)S(1)}, u32[]{:S(2)}, u32[]{:S(2)}) %all-to-all-start.1) | async-done | bytes 786464 | tf_op jit(solution)/shard_map/all_to_all | solution.py:134
  251.5 2.7 %gather_fusion.2 = bf16[256,1024]{1,0:T(8,128)(2,1)S(1)} fusion(bf16[64,6,1024]{2,0,1:T(8,128)(2,1)S(1)} %copy.72, s32[256]{0:T(256)S(1)} %bitcast.63), kind=kCustom, calls=%fused_computation.2 | custom fusion | bytes 1050624 | tf_op jit(solution)/shard_map/gather | solution.py:138
  255.6 1.9 reduce
  (102 shorter events, 27.7 us)
Async XLA Ops:
  0.6 5.1 %copy-start.13 = (f32[128,2]{0,1:T(2,128)S(1)}, f32[128,2]{0,1:T(2,128)}, u32[]{:S(2)}) copy-start(f32[128,2]{0,1:T(2,128)} %param.9) | copy-start | bytes 3076
  0.6 6.4 %copy-start.12 = (bf16[128,896]{1,0:T(8,128)(2,1)S(1)}, bf16[128,896]{1,0:T(8,128)(2,1)}, u32[]{:S(2)}) copy-start(bf16[128,896]{1,0:T(8,128)(2,1)} %param.10) | copy-start | bytes 688132
  7.3 0.9 copy-start.14
  11.4 20.5 %copy-start.8 = (bf16[896,512]{1,0:T(8,128)(2,1)S(1)}, bf16[896,512]{1,0:T(8,128)(2,1)}, u32[]{:S(2)}) copy-start(bf16[896,512]{1,0:T(8,128)(2,1)} %param.12) | copy-start | bytes 2752516
  11.4 97.2 %all-to-all-start = ((bf16[128,42,128]{2,1,0:T(8,128)(2,1)}), bf16[128,42,128]{2,1,0:T(8,128)(2,1)S(1)}, u32[]{:S(2)}, u32[]{:S(2)}) async-start(bf16[128,42,128]{2,1,0:T(8,128)(2,1)} %reshape_reshape.3), calls=%async_computation | async-start | bytes 3145728 | tf_op jit(solution)/shard_map/all_to_all | solution.py:95
  32.0 1.5 copy-start.9
  34.6 79.3 %collective-permute-start.1 = (bf16[896,1024]{1,0:T(8,128)(2,1)}, bf16[896,1024]{1,0:T(8,128)(2,1)}, u32[]{:S(2)}, u32[]{:S(2)}) collective-permute-start(bf16[896,1024]{1,0:T(8,128)(2,1)} %constant_dynamic-update-slice_fusion), channel_id=1, source_target_pairs={{0,256},{4,260},{8,264},{12,268},{16,272},{20,276},{24,280},{28,28... | collective-permute-start | bytes 5505032 | tf_op jit(solution)/shard_map/ppermute | solution.py:10
  110.1 7.5 %collective-permute-start = (bf16[128,2,3,896]{0,3,2,1:T(8,128)(2,1)S(1)}, bf16[128,2,3,896]{0,3,2,1:T(8,128)(2,1)S(1)}, u32[]{:S(2)}, u32[]{:S(2)}) collective-permute-start(bf16[128,2,3,896]{0,3,2,1:T(8,128)(2,1)S(1)} %bitcast.66), channel_id=1, source_target_pairs={{0,4},{4,0},{8,12},{12,8},{16,20},{20,16},{24,28},{28,24},{32,36},... | collective-permute-start | bytes 4128776 | tf_op jit(solution)/shard_map/ppermute | solution.py:16
  128.4 2.8 %copy-start.6 = (bf16[768,896]{1,0:T(8,128)(2,1)}, bf16[768,896]{1,0:T(8,128)(2,1)S(1)}, u32[]{:S(2)}) copy-start(bf16[768,896]{1,0:T(8,128)(2,1)S(1)} %reshape.261) | copy-start | bytes 4128772
  128.5 2.8 %copy-start.2 = (bf16[896,1024]{1,0:T(8,128)(2,1)S(1)}, bf16[896,1024]{1,0:T(8,128)(2,1)}, u32[]{:S(2)}) copy-start(bf16[896,1024]{1,0:T(8,128)(2,1)} %broadcast_select_fusion) | copy-start | bytes 5505028
  128.5 2.8 %copy-start.4 = (bf16[768,896]{1,0:T(8,128)(2,1)S(1)}, bf16[768,896]{1,0:T(8,128)(2,1)}, u32[]{:S(2)}) copy-start(bf16[768,896]{1,0:T(8,128)(2,1)} %reshape.260) | copy-start | bytes 4128772
  133.3 13.9 %collective-permute-start.2 = (bf16[192,1024]{1,0:T(8,128)(2,1)S(1)}, bf16[192,1024]{1,0:T(8,128)(2,1)S(1)}, u32[]{:S(2)}, u32[]{:S(2)}) collective-permute-start(bf16[192,1024]{1,0:T(8,128)(2,1)S(1)} %get-tuple-element.24), channel_id=1, source_target_pairs={{0,1},{1,2},{2,3},{3,0},{4,5},{5,6},{6,7},{7,4},{8,9},{9,10},{10,1... | collective-permute-start | bytes 1179656 | tf_op jit(solution)/shard_map/ppermute | solution.py:27
  136.5 12.4 %collective-permute-start.4 = (bf16[192,1024]{1,0:T(8,128)(2,1)S(1)}, bf16[192,1024]{1,0:T(8,128)(2,1)}, u32[]{:S(2)}, u32[]{:S(2)}) collective-permute-start(bf16[192,1024]{1,0:T(8,128)(2,1)S(1)} %get-tuple-element.25), channel_id=1, source_target_pairs={{0,3},{1,0},{2,1},{3,2},{4,7},{5,4},{6,5},{7,6},{8,11},{9,8},{10,9... | collective-permute-start | bytes 1179656 | tf_op jit(solution)/shard_map/ppermute | solution.py:27
  139.9 17.0 %collective-permute-start.3 = (bf16[192,1024]{1,0:T(8,128)(2,1)S(1)}, bf16[192,1024]{1,0:T(8,128)(2,1)}, u32[]{:S(2)}, u32[]{:S(2)}) collective-permute-start(bf16[192,1024]{1,0:T(8,128)(2,1)S(1)} %get-tuple-element.26), channel_id=1, source_target_pairs={{0,2},{1,3},{2,0},{3,1},{4,6},{5,7},{6,4},{7,5},{8,10},{9,11},{10,... | collective-permute-start | bytes 1179656 | tf_op jit(solution)/shard_map/ppermute | solution.py:27
  158.2 12.7 %collective-permute-start.7 = (bf16[192,1024]{1,0:T(8,128)(2,1)S(1)}, bf16[192,1024]{1,0:T(8,128)(2,1)S(1)}, u32[]{:S(2)}, u32[]{:S(2)}) collective-permute-start(bf16[192,1024]{1,0:T(8,128)(2,1)S(1)} %fusion.12), channel_id=1, source_target_pairs={{0,3},{1,0},{2,1},{3,2},{4,7},{5,4},{6,5},{7,6},{8,11},{9,8},{10,9... | collective-permute-start | bytes 1179656 | tf_op jit(solution)/shard_map/ppermute | solution.py:34
  163.0 12.5 %collective-permute-start.6 = (bf16[192,1024]{1,0:T(8,128)(2,1)S(1)}, bf16[192,1024]{1,0:T(8,128)(2,1)S(1)}, u32[]{:S(2)}, u32[]{:S(2)}) collective-permute-start(bf16[192,1024]{1,0:T(8,128)(2,1)S(1)} %fusion.12), channel_id=1, source_target_pairs={{0,2},{1,3},{2,0},{3,1},{4,6},{5,7},{6,4},{7,5},{8,10},{9,11},{10,... | collective-permute-start | bytes 1179656 | tf_op jit(solution)/shard_map/ppermute | solution.py:34
  166.3 19.6 %collective-permute-start.5 = (bf16[192,1024]{1,0:T(8,128)(2,1)S(1)}, bf16[192,1024]{1,0:T(8,128)(2,1)S(1)}, u32[]{:S(2)}, u32[]{:S(2)}) collective-permute-start(bf16[192,1024]{1,0:T(8,128)(2,1)S(1)} %fusion.12), channel_id=1, source_target_pairs={{0,1},{1,2},{2,3},{3,0},{4,5},{5,6},{6,7},{7,4},{8,9},{9,10},{10,1... | collective-permute-start | bytes 1179656 | tf_op jit(solution)/shard_map/ppermute | solution.py:34
  187.3 1.7 copy-start
  187.3 2.7 %copy-start.3 = (bf16[896,1024]{1,0:T(8,128)(2,1)S(1)}, bf16[896,1024]{1,0:T(8,128)(2,1)}, u32[]{:S(2)}) copy-start(bf16[896,1024]{1,0:T(8,128)(2,1)} %broadcast_select_fusion) | copy-start | bytes 5505028
  188.9 2.1 copy-start.10
  192.5 4.3 %collective-permute-start.8 = (bf16[128,3,1024]{2,0,1:T(8,128)(2,1)S(1)}, bf16[128,3,1024]{2,0,1:T(8,128)(2,1)S(1)}, u32[]{:S(2)}, u32[]{:S(2)}) collective-permute-start(bf16[128,3,1024]{2,0,1:T(8,128)(2,1)S(1)} %fusion.9), channel_id=1, source_target_pairs={{0,4},{4,0},{8,12},{12,8},{16,20},{20,16},{24,28},{28,24},{32,36},... | collective-permute-start | bytes 2359304 | tf_op jit(solution)/shard_map/ppermute | solution.py:16
  197.4 9.2 %copy-start.5 = (bf16[768,896]{1,0:T(8,128)(2,1)S(1)}, bf16[768,896]{1,0:T(8,128)(2,1)}, u32[]{:S(2)}) copy-start(bf16[768,896]{1,0:T(8,128)(2,1)} %reshape.260) | copy-start | bytes 4128772
  197.5 9.2 %copy-start.11 = (bf16[768,512]{1,0:T(8,128)(2,1)S(1)}, bf16[768,512]{1,0:T(8,128)(2,1)}, u32[]{:S(2)}) copy-start(bf16[768,512]{1,0:T(8,128)(2,1)} %copy-done.10) | copy-start | bytes 2359300
  198.7 51.4 %all-to-all-start.1 = ((bf16[128,24,128]{2,1,0:T(8,128)(2,1)}), bf16[128,24,128]{2,1,0:T(8,128)(2,1)S(1)}, u32[]{:S(2)}, u32[]{:S(2)}) async-start(bf16[128,24,128]{2,1,0:T(8,128)(2,1)} %copy.71), calls=%async_computation.1 | async-start | bytes 1572864 | tf_op jit(solution)/shard_map/all_to_all | solution.py:134
  206.7 1.9 copy-start.1
  206.7 2.6 %copy-start.7 = (bf16[768,896]{1,0:T(8,128)(2,1)S(1)}, bf16[768,896]{1,0:T(8,128)(2,1)}, u32[]{:S(2)}) copy-start(bf16[768,896]{1,0:T(8,128)(2,1)} %copy-done.6) | copy-start | bytes 4128772

commit v8 on v7

--- a/solution.py
+++ b/solution.py
@@ -76,8 +76,10 @@
     width = w_up.shape[1]
     own_weights = jnp.concatenate([w_up, w_down], axis=1)
     shifted = passed_along(own_weights, "expert", devices_ex // 2)
-    resident_both = jnp.where(swapped_here, shifted, own_weights)
-    resident = (resident_both[:, :width], resident_both[:, width:])
+    resident = (
+        jnp.where(swapped_here, shifted[:, :width], w_up),
+        jnp.where(swapped_here, shifted[:, width:], w_down),
+    )
     target = owner_slot[flat_routes]
     lead = ((2 * target + slot_rank // share) * 2) * share + slot_rank % share
     token_pos = lead.reshape(tok_rows, top_count)

time: 259 us -> 261 us (level)
  matrix products: 9.46 us -> 13.9 us
  local copies, waits for them, and re-layouts: 33.7 us -> 30.6 us
    select_n x1 -> x0, other arithmetic: 3.59 us -> none  [layer(): resident_both = jnp.where(swapped_here, shifted, own_weights)]
    concatenate x0 -> x1, other arithmetic: none -> 2.72 us  [layer(): own_weights = jnp.concatenate([w_up, w_down], axis=1)]
    unnamed x34 -> x31, local copies, waits for them, and re-layouts: 5.9 us -> 3.91 us
  transfers between devices with their start and end apart: 11 -> 11, of which waited for: 9 -> 10; matrix products, arithmetic and copies ran while one was open for 5% -> 7% of each run, Pallas kernels for 0% -> 0%
where the time goes in v8:
time: 261 us; the launch traced here: 259 us
  waiting for transfers between devices  142 us (54%)
  starting transfers between devices  59.3 us (23%)
  local copies, waits for them, and re-layouts  30.6 us (12%)
  matrix products  13.9 us (5%)
  other arithmetic  12.1 us (5%)
    all_to_all x1, waiting for transfers between devices, layer(): lax.all_to_all(lane_rows(dispatch), 'expert', split_axis=0, concat_axis=0...  68.8 us
    all_to_all x1, waiting for transfers between devices, layer(): lax.all_to_all(lane_rows(combined), 'expert', split_axis=0, concat_axis=0...  38.9 us
    all_to_all x1, starting transfers between devices, layer(): lax.all_to_all(lane_rows(dispatch), 'expert', split_axis=0, concat_axis=0...  20.5 us
    ppermute x3, waiting for transfers between devices, dp_sum(): gathered.append(lax.ppermute(reduced, axis, pairs))  17.6 us
    ppermute x3, waiting for transfers between devices, dp_sum(): lax.ppermute(blocks[(here + step) % count], axis, pairs).astype(jnp.float32)  13 us
    ppermute x3, starting transfers between devices, dp_sum(): lax.ppermute(blocks[(here + step) % count], axis, pairs).astype(jnp.float32)  10.1 us
    ppermute x3, starting transfers between devices, dp_sum(): gathered.append(lax.ppermute(reduced, axis, pairs))  10 us
    all_to_all x1, starting transfers between devices, layer(): lax.all_to_all(lane_rows(combined), 'expert', split_axis=0, concat_axis=0...  7.95 us
  transfers between devices with their start and end apart: 11, of which 10 were waited for; matrix products, arithmetic and copies ran while one was open for 7% of the time, Pallas kernels for 0%

profile of v8, /device:TPU:1, one launch (start us, length us, event | category | flops | bytes accessed | tf_op | source)
XLA Modules:
  0.0 259.3 jit_solution(10076395223117104535)
XLA Ops:
  3.7 1.9 gather_fusion
  9.1 2.3 reshape_reshape.3
  11.5 20.5 %all-to-all-start = ((bf16[128,42,128]{2,1,0:T(8,128)(2,1)}), bf16[128,42,128]{2,1,0:T(8,128)(2,1)S(1)}, u32[]{:S(2)}, u32[]{:S(2)}) async-start(bf16[128,42,128]{2,1,0:T(8,128)(2,1)} %reshape_reshape.3), calls=%async_computation | async-start | bytes 3145728 | tf_op jit(solution)/shard_map/all_to_all | solution.py:97
  32.0 2.7 %pad_maximum_fusion = bf16[896,1024]{1,0:T(8,128)(2,1)} fusion(bf16[896,512]{1,0:T(8,128)(2,1)S(1)} %copy-done.6, bf16[896,512]{1,0:T(8,128)(2,1)} %param.12), kind=kLoop, calls=%fused_computation.3 | loop fusion | flops 3670016 | bytes 3670016 | tf_op jit(solution)/shard_map/concatenate | solution.py:77
  34.7 5.1 %collective-permute-start.1 = (bf16[896,1024]{1,0:T(8,128)(2,1)}, bf16[896,1024]{1,0:T(8,128)(2,1)}, u32[]{:S(2)}, u32[]{:S(2)}) collective-permute-start(bf16[896,1024]{1,0:T(8,128)(2,1)} %pad_maximum_fusion), channel_id=1, source_target_pairs={{0,256},{4,260},{8,264},{12,268},{16,272},{20,276},{24,280},{28,28... | collective-permute-start | bytes 5505032 | tf_op jit(solution)/shard_map/ppermute | solution.py:10
  39.8 68.8 %all-to-all-done = bf16[128,42,128]{2,1,0:T(8,128)(2,1)S(1)} async-done(((bf16[128,42,128]{2,1,0:T(8,128)(2,1)}), bf16[128,42,128]{2,1,0:T(8,128)(2,1)S(1)}, u32[]{:S(2)}, u32[]{:S(2)}) %all-to-all-start) | async-done | bytes 1376288 | tf_op jit(solution)/shard_map/all_to_all | solution.py:97
  110.1 3.2 %collective-permute-start = (bf16[128,2,3,896]{0,3,2,1:T(8,128)(2,1)S(1)}, bf16[128,2,3,896]{0,3,2,1:T(8,128)(2,1)S(1)}, u32[]{:S(2)}, u32[]{:S(2)}) collective-permute-start(bf16[128,2,3,896]{0,3,2,1:T(8,128)(2,1)S(1)} %bitcast.66), channel_id=1, source_target_pairs={{0,4},{4,0},{8,12},{12,8},{16,20},{20,16},{24,28},{28,24},{32,36},... | collective-permute-start | bytes 4128776 | tf_op jit(solution)/shard_map/ppermute | solution.py:16
  117.3 3.4 %copy.65 = bf16[2,128,3,896]{3,2,1,0:T(4,128)(2,1)S(1)} copy(bf16[2,128,3,896]{1,3,2,0:T(8,128)(2,1)} %get-tuple-element.37) | data formatting | bytes 2752512 | tf_op jit(solution)/shard_map/stack | solution.py:101
  120.7 2.4 reshape.260
  123.0 2.4 copy.66
  126.7 3.4 %convolution_convert_fusion.4 = bf16[768,512]{0,1:T(8,128)(2,1)S(1)} fusion(bf16[768,896]{1,0:T(8,128)(2,1)S(1)} %reshape.261, bf16[896,512]{1,0:T(8,128)(2,1)} %param.13, bf16[896,1024]{1,0:T(8,128)(2,1)} %collective-permute-done.1, pred[]{:T(512)} %bitcast.5), kind=kOutput, calls=%fused_computation.19 | convolution fusion | flops 705495040 | bytes 3998208 | tf_op jit(solution)/shard_map/dot_general | solution.py:105
  130.2 2.9 %convolution_convert_fusion.5 = bf16[768,512]{0,1:T(8,128)(2,1)S(1)} fusion(bf16[768,896]{1,0:T(8,128)(2,1)S(1)} %copy-done.2, bf16[896,512]{1,0:T(8,128)(2,1)S(1)} %copy-done.7, bf16[896,1024]{1,0:T(8,128)(2,1)} %collective-permute-done.1, pred[]{:T(512)} %bitcast.5), kind=kOutput, calls=%fused_computation.20 | convolution fusion | flops 705495040 | bytes 3998208 | tf_op jit(solution)/shard_map/dot_general | solution.py:104
  134.1 3.2 %collective-permute-start.2 = (bf16[192,1024]{1,0:T(8,128)(2,1)S(1)}, bf16[192,1024]{1,0:T(8,128)(2,1)S(1)}, u32[]{:S(2)}, u32[]{:S(2)}) collective-permute-start(bf16[192,1024]{1,0:T(8,128)(2,1)S(1)} %get-tuple-element.24), channel_id=1, source_target_pairs={{0,1},{1,2},{2,3},{3,0},{4,5},{5,6},{6,7},{7,4},{8,9},{9,10},{10,1... | collective-permute-start | bytes 1179656 | tf_op jit(solution)/shard_map/ppermute | solution.py:27
  137.3 3.4 %collective-permute-start.4 = (bf16[192,1024]{1,0:T(8,128)(2,1)S(1)}, bf16[192,1024]{1,0:T(8,128)(2,1)}, u32[]{:S(2)}, u32[]{:S(2)}) collective-permute-start(bf16[192,1024]{1,0:T(8,128)(2,1)S(1)} %get-tuple-element.25), channel_id=1, source_target_pairs={{0,3},{1,0},{2,1},{3,2},{4,7},{5,4},{6,5},{7,6},{8,11},{9,8},{10,9... | collective-permute-start | bytes 1179656 | tf_op jit(solution)/shard_map/ppermute | solution.py:27
  140.7 3.5 %collective-permute-start.3 = (bf16[192,1024]{1,0:T(8,128)(2,1)S(1)}, bf16[192,1024]{1,0:T(8,128)(2,1)}, u32[]{:S(2)}, u32[]{:S(2)}) collective-permute-start(bf16[192,1024]{1,0:T(8,128)(2,1)S(1)} %get-tuple-element.26), channel_id=1, source_target_pairs={{0,2},{1,3},{2,0},{3,1},{4,6},{5,7},{6,4},{7,5},{8,10},{9,11},{10,... | collective-permute-start | bytes 1179656 | tf_op jit(solution)/shard_map/ppermute | solution.py:27
  144.2 3.4 %collective-permute-done.2 = bf16[192,1024]{1,0:T(8,128)(2,1)S(1)} collective-permute-done((bf16[192,1024]{1,0:T(8,128)(2,1)S(1)}, bf16[192,1024]{1,0:T(8,128)(2,1)S(1)}, u32[]{:S(2)}, u32[]{:S(2)}) %collective-permute-start.2) | collective-permute-done | bytes 393248 | tf_op jit(solution)/shard_map/ppermute | solution.py:27
  149.4 7.9 %collective-permute-done.3 = bf16[192,1024]{1,0:T(8,128)(2,1)} collective-permute-done((bf16[192,1024]{1,0:T(8,128)(2,1)S(1)}, bf16[192,1024]{1,0:T(8,128)(2,1)}, u32[]{:S(2)}, u32[]{:S(2)}) %collective-permute-start.3) | collective-permute-done | bytes 393248 | tf_op jit(solution)/shard_map/ppermute | solution.py:27
  158.7 4.8 %collective-permute-start.7 = (bf16[192,1024]{1,0:T(8,128)(2,1)S(1)}, bf16[192,1024]{1,0:T(8,128)(2,1)S(1)}, u32[]{:S(2)}, u32[]{:S(2)}) collective-permute-start(bf16[192,1024]{1,0:T(8,128)(2,1)S(1)} %fusion.10), channel_id=1, source_target_pairs={{0,3},{1,0},{2,1},{3,2},{4,7},{5,4},{6,5},{7,6},{8,11},{9,8},{10,9... | collective-permute-start | bytes 1179656 | tf_op jit(solution)/shard_map/ppermute | solution.py:34
  163.5 3.3 %collective-permute-start.6 = (bf16[192,1024]{1,0:T(8,128)(2,1)S(1)}, bf16[192,1024]{1,0:T(8,128)(2,1)S(1)}, u32[]{:S(2)}, u32[]{:S(2)}) collective-permute-start(bf16[192,1024]{1,0:T(8,128)(2,1)S(1)} %fusion.10), channel_id=1, source_target_pairs={{0,2},{1,3},{2,0},{3,1},{4,6},{5,7},{6,4},{7,5},{8,10},{9,11},{10,... | collective-permute-start | bytes 1179656 | tf_op jit(solution)/shard_map/ppermute | solution.py:34
  166.8 1.9 collective-permute-start.5
  168.8 2.3 collective-permute-done.7
  171.0 4.6 %collective-permute-done.6 = bf16[192,1024]{1,0:T(8,128)(2,1)S(1)} collective-permute-done((bf16[192,1024]{1,0:T(8,128)(2,1)S(1)}, bf16[192,1024]{1,0:T(8,128)(2,1)S(1)}, u32[]{:S(2)}, u32[]{:S(2)}) %collective-permute-start.6) | collective-permute-done | bytes 393248 | tf_op jit(solution)/shard_map/ppermute | solution.py:34
  175.6 10.8 %collective-permute-done.5 = bf16[192,1024]{1,0:T(8,128)(2,1)S(1)} collective-permute-done((bf16[192,1024]{1,0:T(8,128)(2,1)S(1)}, bf16[192,1024]{1,0:T(8,128)(2,1)S(1)}, u32[]{:S(2)}, u32[]{:S(2)}) %collective-permute-start.5) | collective-permute-done | bytes 393248 | tf_op jit(solution)/shard_map/ppermute | solution.py:34
  190.3 2.8 %convolution_convert_fusion.1 = bf16[768,896]{1,0:T(8,128)(2,1)S(1)} fusion(bf16[768,512]{1,0:T(8,128)(2,1)S(1)} %get-tuple-element.22, bf16[896,512]{1,0:T(8,128)(2,1)S(1)} %copy-done.8, bf16[896,1024]{1,0:T(8,128)(2,1)} %collective-permute-done.1, pred[]{:T(512)} %bitcast.5), kind=kOutput, calls=%fused_computation.5 | convolution fusion | flops 705789952 | bytes 3998208 | tf_op jit(solution)/shard_map/nf,df->nd/dot_general | solution.py:114
  194.3 2.4 collective-permute-start.8
  196.7 1.9 collective-permute-done.8
  200.5 7.9 %all-to-all-start.1 = ((bf16[128,24,128]{2,1,0:T(8,128)(2,1)}), bf16[128,24,128]{2,1,0:T(8,128)(2,1)S(1)}, u32[]{:S(2)}, u32[]{:S(2)}) async-start(bf16[128,24,128]{2,1,0:T(8,128)(2,1)} %copy.71), calls=%async_computation.1 | async-start | bytes 1572864 | tf_op jit(solution)/shard_map/all_to_all | solution.py:136
  208.5 1.8 convolution_convert_fusion.3
  211.1 1.9 convolution_convert_fusion.2
  213.1 38.9 %all-to-all-done.1 = bf16[128,24,128]{2,1,0:T(8,128)(2,1)S(1)} async-done(((bf16[128,24,128]{2,1,0:T(8,128)(2,1)}), bf16[128,24,128]{2,1,0:T(8,128)(2,1)S(1)}, u32[]{:S(2)}, u32[]{:S(2)}) %all-to-all-start.1) | async-done | bytes 786464 | tf_op jit(solution)/shard_map/all_to_all | solution.py:136
  253.3 2.7 %gather_fusion.2 = bf16[256,1024]{1,0:T(8,128)(2,1)S(1)} fusion(bf16[64,6,1024]{2,0,1:T(8,128)(2,1)S(1)} %copy.72, s32[256]{0:T(256)S(1)} %bitcast.63), kind=kCustom, calls=%fused_computation.2 | custom fusion | bytes 1050624 | tf_op jit(solution)/shard_map/gather | solution.py:140
  257.4 1.9 reduce
  (98 shorter events, 27.5 us)
Async XLA Ops:
  0.6 5.1 %copy-start.12 = (f32[128,2]{0,1:T(2,128)S(1)}, f32[128,2]{0,1:T(2,128)}, u32[]{:S(2)}) copy-start(f32[128,2]{0,1:T(2,128)} %param.9) | copy-start | bytes 3076
  0.6 6.4 %copy-start.11 = (bf16[128,896]{1,0:T(8,128)(2,1)S(1)}, bf16[128,896]{1,0:T(8,128)(2,1)}, u32[]{:S(2)}) copy-start(bf16[128,896]{1,0:T(8,128)(2,1)} %param.10) | copy-start | bytes 688132
  7.3 0.9 copy-start.13
  11.5 20.5 %copy-start.6 = (bf16[896,512]{1,0:T(8,128)(2,1)S(1)}, bf16[896,512]{1,0:T(8,128)(2,1)}, u32[]{:S(2)}) copy-start(bf16[896,512]{1,0:T(8,128)(2,1)} %param.13) | copy-start | bytes 2752516
  11.5 97.2 %all-to-all-start = ((bf16[128,42,128]{2,1,0:T(8,128)(2,1)}), bf16[128,42,128]{2,1,0:T(8,128)(2,1)S(1)}, u32[]{:S(2)}, u32[]{:S(2)}) async-start(bf16[128,42,128]{2,1,0:T(8,128)(2,1)} %reshape_reshape.3), calls=%async_computation | async-start | bytes 3145728 | tf_op jit(solution)/shard_map/all_to_all | solution.py:97
  34.7 92.0 %collective-permute-start.1 = (bf16[896,1024]{1,0:T(8,128)(2,1)}, bf16[896,1024]{1,0:T(8,128)(2,1)}, u32[]{:S(2)}, u32[]{:S(2)}) collective-permute-start(bf16[896,1024]{1,0:T(8,128)(2,1)} %pad_maximum_fusion), channel_id=1, source_target_pairs={{0,256},{4,260},{8,264},{12,268},{16,272},{20,276},{24,280},{28,28... | collective-permute-start | bytes 5505032 | tf_op jit(solution)/shard_map/ppermute | solution.py:10
  110.1 5.7 %collective-permute-start = (bf16[128,2,3,896]{0,3,2,1:T(8,128)(2,1)S(1)}, bf16[128,2,3,896]{0,3,2,1:T(8,128)(2,1)S(1)}, u32[]{:S(2)}, u32[]{:S(2)}) collective-permute-start(bf16[128,2,3,896]{0,3,2,1:T(8,128)(2,1)S(1)} %bitcast.66), channel_id=1, source_target_pairs={{0,4},{4,0},{8,12},{12,8},{16,20},{20,16},{24,28},{28,24},{32,36},... | collective-permute-start | bytes 4128776 | tf_op jit(solution)/shard_map/ppermute | solution.py:16
  126.6 3.5 %copy-start.4 = (bf16[768,896]{1,0:T(8,128)(2,1)}, bf16[768,896]{1,0:T(8,128)(2,1)S(1)}, u32[]{:S(2)}) copy-start(bf16[768,896]{1,0:T(8,128)(2,1)S(1)} %reshape.261) | copy-start | bytes 4128772
  126.7 3.5 %copy-start.2 = (bf16[768,896]{1,0:T(8,128)(2,1)S(1)}, bf16[768,896]{1,0:T(8,128)(2,1)}, u32[]{:S(2)}) copy-start(bf16[768,896]{1,0:T(8,128)(2,1)} %reshape.260) | copy-start | bytes 4128772
  126.7 3.5 %copy-start.7 = (bf16[896,512]{1,0:T(8,128)(2,1)S(1)}, bf16[896,512]{1,0:T(8,128)(2,1)}, u32[]{:S(2)}) copy-start(bf16[896,512]{1,0:T(8,128)(2,1)} %param.12) | copy-start | bytes 2752516
  134.1 13.5 %collective-permute-start.2 = (bf16[192,1024]{1,0:T(8,128)(2,1)S(1)}, bf16[192,1024]{1,0:T(8,128)(2,1)S(1)}, u32[]{:S(2)}, u32[]{:S(2)}) collective-permute-start(bf16[192,1024]{1,0:T(8,128)(2,1)S(1)} %get-tuple-element.24), channel_id=1, source_target_pairs={{0,1},{1,2},{2,3},{3,0},{4,5},{5,6},{6,7},{7,4},{8,9},{9,10},{10,1... | collective-permute-start | bytes 1179656 | tf_op jit(solution)/shard_map/ppermute | solution.py:27
  137.3 12.0 %collective-permute-start.4 = (bf16[192,1024]{1,0:T(8,128)(2,1)S(1)}, bf16[192,1024]{1,0:T(8,128)(2,1)}, u32[]{:S(2)}, u32[]{:S(2)}) collective-permute-start(bf16[192,1024]{1,0:T(8,128)(2,1)S(1)} %get-tuple-element.25), channel_id=1, source_target_pairs={{0,3},{1,0},{2,1},{3,2},{4,7},{5,4},{6,5},{7,6},{8,11},{9,8},{10,9... | collective-permute-start | bytes 1179656 | tf_op jit(solution)/shard_map/ppermute | solution.py:27
  140.7 16.6 %collective-permute-start.3 = (bf16[192,1024]{1,0:T(8,128)(2,1)S(1)}, bf16[192,1024]{1,0:T(8,128)(2,1)}, u32[]{:S(2)}, u32[]{:S(2)}) collective-permute-start(bf16[192,1024]{1,0:T(8,128)(2,1)S(1)} %get-tuple-element.26), channel_id=1, source_target_pairs={{0,2},{1,3},{2,0},{3,1},{4,6},{5,7},{6,4},{7,5},{8,10},{9,11},{10,... | collective-permute-start | bytes 1179656 | tf_op jit(solution)/shard_map/ppermute | solution.py:27
  158.7 12.4 %collective-permute-start.7 = (bf16[192,1024]{1,0:T(8,128)(2,1)S(1)}, bf16[192,1024]{1,0:T(8,128)(2,1)S(1)}, u32[]{:S(2)}, u32[]{:S(2)}) collective-permute-start(bf16[192,1024]{1,0:T(8,128)(2,1)S(1)} %fusion.10), channel_id=1, source_target_pairs={{0,3},{1,0},{2,1},{3,2},{4,7},{5,4},{6,5},{7,6},{8,11},{9,8},{10,9... | collective-permute-start | bytes 1179656 | tf_op jit(solution)/shard_map/ppermute | solution.py:34
  163.5 12.1 %collective-permute-start.6 = (bf16[192,1024]{1,0:T(8,128)(2,1)S(1)}, bf16[192,1024]{1,0:T(8,128)(2,1)S(1)}, u32[]{:S(2)}, u32[]{:S(2)}) collective-permute-start(bf16[192,1024]{1,0:T(8,128)(2,1)S(1)} %fusion.10), channel_id=1, source_target_pairs={{0,2},{1,3},{2,0},{3,1},{4,6},{5,7},{6,4},{7,5},{8,10},{9,11},{10,... | collective-permute-start | bytes 1179656 | tf_op jit(solution)/shard_map/ppermute | solution.py:34
  166.8 19.6 %collective-permute-start.5 = (bf16[192,1024]{1,0:T(8,128)(2,1)S(1)}, bf16[192,1024]{1,0:T(8,128)(2,1)S(1)}, u32[]{:S(2)}, u32[]{:S(2)}) collective-permute-start(bf16[192,1024]{1,0:T(8,128)(2,1)S(1)} %fusion.10), channel_id=1, source_target_pairs={{0,1},{1,2},{2,3},{3,0},{4,5},{5,6},{6,7},{7,4},{8,9},{9,10},{10,1... | collective-permute-start | bytes 1179656 | tf_op jit(solution)/shard_map/ppermute | solution.py:34
  187.7 1.6 copy-start
  187.7 2.5 copy-start.8
  189.4 0.9 copy-start.9
  194.3 4.3 %collective-permute-start.8 = (bf16[128,3,1024]{2,0,1:T(8,128)(2,1)S(1)}, bf16[128,3,1024]{2,0,1:T(8,128)(2,1)S(1)}, u32[]{:S(2)}, u32[]{:S(2)}) collective-permute-start(bf16[128,3,1024]{2,0,1:T(8,128)(2,1)S(1)} %fusion.7), channel_id=1, source_target_pairs={{0,4},{4,0},{8,12},{12,8},{16,20},{20,16},{24,28},{28,24},{32,36},... | collective-permute-start | bytes 2359304 | tf_op jit(solution)/shard_map/ppermute | solution.py:16
  199.2 9.3 %copy-start.3 = (bf16[768,896]{1,0:T(8,128)(2,1)S(1)}, bf16[768,896]{1,0:T(8,128)(2,1)}, u32[]{:S(2)}) copy-start(bf16[768,896]{1,0:T(8,128)(2,1)} %reshape.260) | copy-start | bytes 4128772
  199.3 9.3 %copy-start.10 = (bf16[768,512]{1,0:T(8,128)(2,1)S(1)}, bf16[768,512]{1,0:T(8,128)(2,1)}, u32[]{:S(2)}) copy-start(bf16[768,512]{1,0:T(8,128)(2,1)} %copy-done.9) | copy-start | bytes 2359300
  200.5 51.4 %all-to-all-start.1 = ((bf16[128,24,128]{2,1,0:T(8,128)(2,1)}), bf16[128,24,128]{2,1,0:T(8,128)(2,1)S(1)}, u32[]{:S(2)}, u32[]{:S(2)}) async-start(bf16[128,24,128]{2,1,0:T(8,128)(2,1)} %copy.71), calls=%async_computation.1 | async-start | bytes 1572864 | tf_op jit(solution)/shard_map/all_to_all | solution.py:136
  208.5 1.9 copy-start.1
  208.5 2.6 %copy-start.5 = (bf16[768,896]{1,0:T(8,128)(2,1)S(1)}, bf16[768,896]{1,0:T(8,128)(2,1)}, u32[]{:S(2)}) copy-start(bf16[768,896]{1,0:T(8,128)(2,1)} %copy-done.4) | copy-start | bytes 4128772

commit v9 on v7

--- a/solution.py
+++ b/solution.py
@@ -42,6 +42,15 @@
     return value.reshape(count, -1, 128)
 
 
+def pick_pair(swapped_here, theirs, ours):
+    return tuple(
+        (
+            jnp.where(swapped_here, other_part, mine_part)
+            for other_part, mine_part in zip(theirs, ours)
+        )
+    )
+
+
 def activate(up_pre, grad_hidden):
     up_sig = jax.nn.sigmoid(up_pre)
     hidden = (up_pre * up_sig).astype(jnp.bfloat16)
@@ -73,11 +82,9 @@
     flat_routes = routes.reshape(-1)
     onehot = (flat_routes[:, None] == expert_ids[None, :]).astype(jnp.int32)
     slot_rank = jnp.sum(jnp.cumsum(onehot, 0) * onehot, 1) - 1
-    width = w_up.shape[1]
-    own_weights = jnp.concatenate([w_up, w_down], axis=1)
-    shifted = passed_along(own_weights, "expert", devices_ex // 2)
-    resident_both = jnp.where(swapped_here, shifted, own_weights)
-    resident = (resident_both[:, :width], resident_both[:, width:])
+    own_weights = (w_up, w_down)
+    shifted = passed_along((w_up, w_down), "expert", devices_ex // 2)
+    resident = pick_pair(swapped_here, shifted, own_weights)
     target = owner_slot[flat_routes]
     lead = ((2 * target + slot_rank // share) * 2) * share + slot_rank % share
     token_pos = lead.reshape(tok_rows, top_count)

time: 259 us -> 288 us (1.11)
  blocking collectives: 0 us -> 96.8 us
  waiting for transfers between devices: 141 us -> 93.1 us
  starting transfers between devices: 59.2 us -> 40.7 us
  matrix products: 9.46 us -> 14.5 us
  other arithmetic: 13 us -> 9.38 us
  local copies, waits for them, and re-layouts: 33.7 us -> 30.8 us
    all_to_all x0 -> x1, blocking collectives: none -> 96.8 us  [layer(): lax.all_to_all(lane_rows(dispatch), 'expert', split_axis=0, concat_axis=0...]
    all_to_all x1 -> x0, waiting for transfers between devices: 68.9 us -> none  [layer(): lax.all_to_all(lane_rows(dispatch), 'expert', split_axis=0, concat_axis=0...]
    ppermute x1 -> x2, waiting for transfers between devices: 0.01 us -> 22.4 us  [passed_along(): return lax.ppermute(value, axis, pairs)]
    all_to_all x1 -> x0, starting transfers between devices: 20.5 us -> none  [layer(): lax.all_to_all(lane_rows(dispatch), 'expert', split_axis=0, concat_axis=0...]
    select_n x1 -> x0, other arithmetic: 3.59 us -> none  [layer(): resident_both = jnp.where(swapped_here, shifted, own_weights)]
    unnamed x34 -> x27, local copies, waits for them, and re-layouts: 5.9 us -> 3.75 us
    ppermute x1 -> x2, starting transfers between devices: 5.08 us -> 6.97 us  [passed_along(): return lax.ppermute(value, axis, pairs)]
  transfers between devices with their start and end apart: 11 -> 11, of which waited for: 9 -> 10; matrix products, arithmetic and copies ran while one was open for 5% -> 7% of each run, Pallas kernels for 0% -> 0%
where the time goes in v9:
time: 288 us; the launch traced here: 287 us
  blocking collectives  96.8 us (34%)
  waiting for transfers between devices  93.1 us (32%)
  starting transfers between devices  40.7 us (14%)
  local copies, waits for them, and re-layouts  30.8 us (11%)
  matrix products  14.5 us (5%)
  other arithmetic  9.38 us (3%)
    all_to_all x1, blocking collectives, layer(): lax.all_to_all(lane_rows(dispatch), 'expert', split_axis=0, concat_axis=0...  96.8 us
    all_to_all x1, waiting for transfers between devices, layer(): lax.all_to_all(lane_rows(combined), 'expert', split_axis=0, concat_axis=0...  38.9 us
    ppermute x2, waiting for transfers between devices, passed_along(): return lax.ppermute(value, axis, pairs)  22.4 us
    ppermute x3, waiting for transfers between devices, dp_sum(): gathered.append(lax.ppermute(reduced, axis, pairs))  17.4 us
    ppermute x3, waiting for transfers between devices, dp_sum(): lax.ppermute(blocks[(here + step) % count], axis, pairs).astype(jnp.float32)  12.5 us
    ppermute x3, starting transfers between devices, dp_sum(): lax.ppermute(blocks[(here + step) % count], axis, pairs).astype(jnp.float32)  10.1 us
    ppermute x3, starting transfers between devices, dp_sum(): gathered.append(lax.ppermute(reduced, axis, pairs))  10 us
    all_to_all x1, starting transfers between devices, layer(): lax.all_to_all(lane_rows(combined), 'expert', split_axis=0, concat_axis=0...  7.94 us
  transfers between devices with their start and end apart: 11, of which 10 were waited for; matrix products, arithmetic and copies ran while one was open for 7% of the time, Pallas kernels for 0%

profile of v9, /device:TPU:1, one launch (start us, length us, event | category | flops | bytes accessed | tf_op | source)
XLA Modules:
  0.0 286.6 jit_solution(7486879108760816253)
XLA Ops:
  3.7 1.9 gather_fusion
  8.1 1.8 convolution_convert_fusion
  11.3 96.8 %all_to_all.10 = bf16[128,42,128]{2,1,0:T(8,128)(2,1)S(1)} all-to-all(bf16[128,42,128]{2,1,0:T(8,128)(2,1)S(1)} %reshape_reshape.3), channel_id=1, replica_groups=mesh['expert'=128,'dp'=4] {'expert'}, dimensions={0} | all-to-all | bytes 2752512 | tf_op jit(solution)/shard_map/all_to_all | solution.py:102
  109.6 3.0 %collective-permute-start = (bf16[128,2,3,896]{0,3,2,1:T(8,128)(2,1)S(1)}, bf16[128,2,3,896]{0,3,2,1:T(8,128)(2,1)S(1)}, u32[]{:S(2)}, u32[]{:S(2)}) collective-permute-start(bf16[128,2,3,896]{0,3,2,1:T(8,128)(2,1)S(1)} %bitcast.66), channel_id=1, source_target_pairs={{0,4},{4,0},{8,12},{12,8},{16,20},{20,16},{24,28},{28,24},{32,36},... | collective-permute-start | bytes 4128776 | tf_op jit(solution)/shard_map/ppermute | solution.py:16
  112.6 4.7 %collective-permute-start.1 = (bf16[896,512]{1,0:T(8,128)(2,1)}, bf16[896,512]{1,0:T(8,128)(2,1)}, u32[]{:S(2)}, u32[]{:S(2)}) collective-permute-start(bf16[896,512]{1,0:T(8,128)(2,1)} %param.12), channel_id=1, source_target_pairs={{0,256},{4,260},{8,264},{12,268},{16,272},{20,276},{24,280},{28,28... | collective-permute-start | bytes 2752520 | tf_op jit(solution)/shard_map/ppermute | solution.py:10
  117.4 2.2 collective-permute-start.2
  121.8 3.4 %copy.65 = bf16[2,128,3,896]{3,2,1,0:T(4,128)(2,1)S(1)} copy(bf16[2,128,3,896]{1,3,2,0:T(8,128)(2,1)} %get-tuple-element.37) | data formatting | bytes 2752512 | tf_op jit(solution)/shard_map/stack | solution.py:106
  125.2 2.4 reshape.260
  127.6 2.4 copy.66
  130.0 2.4 reshape.261
  132.4 5.8 %collective-permute-done.1 = bf16[896,512]{1,0:T(8,128)(2,1)} collective-permute-done((bf16[896,512]{1,0:T(8,128)(2,1)}, bf16[896,512]{1,0:T(8,128)(2,1)}, u32[]{:S(2)}, u32[]{:S(2)}) %collective-permute-start.1) | collective-permute-done | bytes 917536 | tf_op jit(solution)/shard_map/ppermute | solution.py:10
  138.2 3.1 %convolution_convert_fusion.5 = bf16[768,512]{0,1:T(8,128)(2,1)S(1)} fusion(bf16[768,896]{1,0:T(8,128)(2,1)S(1)} %copy-done.2, bf16[896,512]{1,0:T(8,128)(2,1)} %collective-permute-done.1, bf16[896,512]{1,0:T(8,128)(2,1)} %param.12, pred[]{:T(512)} %bitcast.5), kind=kOutput, calls=%fused_computation.19 | convolution fusion | flops 705495040 | bytes 3997697 | tf_op jit(solution)/shard_map/dot_general | solution.py:109
  141.3 16.6 %collective-permute-done.2 = bf16[896,512]{1,0:T(8,128)(2,1)} collective-permute-done((bf16[896,512]{1,0:T(8,128)(2,1)}, bf16[896,512]{1,0:T(8,128)(2,1)}, u32[]{:S(2)}, u32[]{:S(2)}) %collective-permute-start.2) | collective-permute-done | bytes 917536 | tf_op jit(solution)/shard_map/ppermute | solution.py:10
  157.9 2.9 %convolution_convert_fusion.4 = bf16[768,512]{0,1:T(8,128)(2,1)S(1)} fusion(bf16[768,896]{1,0:T(8,128)(2,1)S(1)} %copy-done.4, bf16[896,512]{1,0:T(8,128)(2,1)} %collective-permute-done.2, bf16[896,512]{1,0:T(8,128)(2,1)S(1)} %copy-done.10, pred[]{:T(512)} %bitcast.5), kind=kOutput, calls=%fused_computation.18 | convolution fusion | flops 705495040 | bytes 3997697 | tf_op jit(solution)/shard_map/dot_general | solution.py:110
  161.9 3.2 %collective-permute-start.3 = (bf16[192,1024]{1,0:T(8,128)(2,1)S(1)}, bf16[192,1024]{1,0:T(8,128)(2,1)S(1)}, u32[]{:S(2)}, u32[]{:S(2)}) collective-permute-start(bf16[192,1024]{1,0:T(8,128)(2,1)S(1)} %get-tuple-element.24), channel_id=1, source_target_pairs={{0,1},{1,2},{2,3},{3,0},{4,5},{5,6},{6,7},{7,4},{8,9},{9,10},{10,1... | collective-permute-start | bytes 1179656 | tf_op jit(solution)/shard_map/ppermute | solution.py:27
  165.1 3.4 %collective-permute-start.5 = (bf16[192,1024]{1,0:T(8,128)(2,1)S(1)}, bf16[192,1024]{1,0:T(8,128)(2,1)}, u32[]{:S(2)}, u32[]{:S(2)}) collective-permute-start(bf16[192,1024]{1,0:T(8,128)(2,1)S(1)} %get-tuple-element.25), channel_id=1, source_target_pairs={{0,3},{1,0},{2,1},{3,2},{4,7},{5,4},{6,5},{7,6},{8,11},{9,8},{10,9... | collective-permute-start | bytes 1179656 | tf_op jit(solution)/shard_map/ppermute | solution.py:27
  168.4 3.5 %collective-permute-start.4 = (bf16[192,1024]{1,0:T(8,128)(2,1)S(1)}, bf16[192,1024]{1,0:T(8,128)(2,1)}, u32[]{:S(2)}, u32[]{:S(2)}) collective-permute-start(bf16[192,1024]{1,0:T(8,128)(2,1)S(1)} %get-tuple-element.26), channel_id=1, source_target_pairs={{0,2},{1,3},{2,0},{3,1},{4,6},{5,7},{6,4},{7,5},{8,10},{9,11},{10,... | collective-permute-start | bytes 1179656 | tf_op jit(solution)/shard_map/ppermute | solution.py:27
  172.0 2.9 %collective-permute-done.3 = bf16[192,1024]{1,0:T(8,128)(2,1)S(1)} collective-permute-done((bf16[192,1024]{1,0:T(8,128)(2,1)S(1)}, bf16[192,1024]{1,0:T(8,128)(2,1)S(1)}, u32[]{:S(2)}, u32[]{:S(2)}) %collective-permute-start.3) | collective-permute-done | bytes 393248 | tf_op jit(solution)/shard_map/ppermute | solution.py:27
  176.6 7.9 %collective-permute-done.4 = bf16[192,1024]{1,0:T(8,128)(2,1)} collective-permute-done((bf16[192,1024]{1,0:T(8,128)(2,1)S(1)}, bf16[192,1024]{1,0:T(8,128)(2,1)}, u32[]{:S(2)}, u32[]{:S(2)}) %collective-permute-start.4) | collective-permute-done | bytes 393248 | tf_op jit(solution)/shard_map/ppermute | solution.py:27
  185.9 4.8 %collective-permute-start.8 = (bf16[192,1024]{1,0:T(8,128)(2,1)S(1)}, bf16[192,1024]{1,0:T(8,128)(2,1)S(1)}, u32[]{:S(2)}, u32[]{:S(2)}) collective-permute-start(bf16[192,1024]{1,0:T(8,128)(2,1)S(1)} %fusion.11), channel_id=1, source_target_pairs={{0,3},{1,0},{2,1},{3,2},{4,7},{5,4},{6,5},{7,6},{8,11},{9,8},{10,9... | collective-permute-start | bytes 1179656 | tf_op jit(solution)/shard_map/ppermute | solution.py:34
  190.7 3.3 %collective-permute-start.7 = (bf16[192,1024]{1,0:T(8,128)(2,1)S(1)}, bf16[192,1024]{1,0:T(8,128)(2,1)S(1)}, u32[]{:S(2)}, u32[]{:S(2)}) collective-permute-start(bf16[192,1024]{1,0:T(8,128)(2,1)S(1)} %fusion.11), channel_id=1, source_target_pairs={{0,2},{1,3},{2,0},{3,1},{4,6},{5,7},{6,4},{7,5},{8,10},{9,11},{10,... | collective-permute-start | bytes 1179656 | tf_op jit(solution)/shard_map/ppermute | solution.py:34
  194.0 1.9 collective-permute-start.6
  197.8 4.5 %collective-permute-done.7 = bf16[192,1024]{1,0:T(8,128)(2,1)S(1)} collective-permute-done((bf16[192,1024]{1,0:T(8,128)(2,1)S(1)}, bf16[192,1024]{1,0:T(8,128)(2,1)S(1)}, u32[]{:S(2)}, u32[]{:S(2)}) %collective-permute-start.7) | collective-permute-done | bytes 393248 | tf_op jit(solution)/shard_map/ppermute | solution.py:34
  202.3 11.1 %collective-permute-done.6 = bf16[192,1024]{1,0:T(8,128)(2,1)S(1)} collective-permute-done((bf16[192,1024]{1,0:T(8,128)(2,1)S(1)}, bf16[192,1024]{1,0:T(8,128)(2,1)S(1)}, u32[]{:S(2)}, u32[]{:S(2)}) %collective-permute-start.6) | collective-permute-done | bytes 393248 | tf_op jit(solution)/shard_map/ppermute | solution.py:34
  217.3 2.8 convolution_convert_fusion.1
  221.3 2.6 collective-permute-start.9
  224.0 1.9 collective-permute-done.9
  227.8 7.9 %all-to-all-start.1 = ((bf16[128,24,128]{2,1,0:T(8,128)(2,1)}), bf16[128,24,128]{2,1,0:T(8,128)(2,1)S(1)}, u32[]{:S(2)}, u32[]{:S(2)}) async-start(bf16[128,24,128]{2,1,0:T(8,128)(2,1)} %copy.71), calls=%async_computation.1 | async-start | bytes 1572864 | tf_op jit(solution)/shard_map/all_to_all | solution.py:141
  238.4 1.9 convolution_convert_fusion.2
  240.3 38.9 %all-to-all-done.1 = bf16[128,24,128]{2,1,0:T(8,128)(2,1)S(1)} async-done(((bf16[128,24,128]{2,1,0:T(8,128)(2,1)}), bf16[128,24,128]{2,1,0:T(8,128)(2,1)S(1)}, u32[]{:S(2)}, u32[]{:S(2)}) %all-to-all-start.1) | async-done | bytes 786464 | tf_op jit(solution)/shard_map/all_to_all | solution.py:141
  280.5 2.7 gather_fusion.2
  284.7 1.9 reduce
  (94 shorter events, 28.4 us)
Async XLA Ops:
  0.6 5.1 %copy-start.9 = (f32[128,2]{0,1:T(2,128)S(1)}, f32[128,2]{0,1:T(2,128)}, u32[]{:S(2)}) copy-start(f32[128,2]{0,1:T(2,128)} %param.9) | copy-start | bytes 3076
  0.6 6.4 %copy-start.8 = (bf16[128,896]{1,0:T(8,128)(2,1)S(1)}, bf16[128,896]{1,0:T(8,128)(2,1)}, u32[]{:S(2)}) copy-start(bf16[128,896]{1,0:T(8,128)(2,1)} %param.10) | copy-start | bytes 688132
  109.6 10.7 %collective-permute-start = (bf16[128,2,3,896]{0,3,2,1:T(8,128)(2,1)S(1)}, bf16[128,2,3,896]{0,3,2,1:T(8,128)(2,1)S(1)}, u32[]{:S(2)}, u32[]{:S(2)}) collective-permute-start(bf16[128,2,3,896]{0,3,2,1:T(8,128)(2,1)S(1)} %bitcast.66), channel_id=1, source_target_pairs={{0,4},{4,0},{8,12},{12,8},{16,20},{20,16},{24,28},{28,24},{32,36},... | collective-permute-start | bytes 4128776 | tf_op jit(solution)/shard_map/ppermute | solution.py:16
  112.6 25.6 %collective-permute-start.1 = (bf16[896,512]{1,0:T(8,128)(2,1)}, bf16[896,512]{1,0:T(8,128)(2,1)}, u32[]{:S(2)}, u32[]{:S(2)}) collective-permute-start(bf16[896,512]{1,0:T(8,128)(2,1)} %param.12), channel_id=1, source_target_pairs={{0,256},{4,260},{8,264},{12,268},{16,272},{20,276},{24,280},{28,28... | collective-permute-start | bytes 2752520 | tf_op jit(solution)/shard_map/ppermute | solution.py:10
  117.4 40.5 %collective-permute-start.2 = (bf16[896,512]{1,0:T(8,128)(2,1)}, bf16[896,512]{1,0:T(8,128)(2,1)}, u32[]{:S(2)}, u32[]{:S(2)}) collective-permute-start(bf16[896,512]{1,0:T(8,128)(2,1)} %param.13), channel_id=1, source_target_pairs={{0,256},{4,260},{8,264},{12,268},{16,272},{20,276},{24,280},{28,28... | collective-permute-start | bytes 2752520 | tf_op jit(solution)/shard_map/ppermute | solution.py:10
  130.0 8.2 %copy-start.2 = (bf16[768,896]{1,0:T(8,128)(2,1)S(1)}, bf16[768,896]{1,0:T(8,128)(2,1)}, u32[]{:S(2)}) copy-start(bf16[768,896]{1,0:T(8,128)(2,1)} %reshape.260) | copy-start | bytes 4128772
  138.2 19.7 %copy-start.4 = (bf16[768,896]{1,0:T(8,128)(2,1)S(1)}, bf16[768,896]{1,0:T(8,128)(2,1)}, u32[]{:S(2)}) copy-start(bf16[768,896]{1,0:T(8,128)(2,1)} %reshape.261) | copy-start | bytes 4128772
  138.2 19.7 %copy-start.10 = (bf16[896,512]{1,0:T(8,128)(2,1)S(1)}, bf16[896,512]{1,0:T(8,128)(2,1)}, u32[]{:S(2)}) copy-start(bf16[896,512]{1,0:T(8,128)(2,1)} %param.13) | copy-start | bytes 2752516
  161.9 13.0 %collective-permute-start.3 = (bf16[192,1024]{1,0:T(8,128)(2,1)S(1)}, bf16[192,1024]{1,0:T(8,128)(2,1)S(1)}, u32[]{:S(2)}, u32[]{:S(2)}) collective-permute-start(bf16[192,1024]{1,0:T(8,128)(2,1)S(1)} %get-tuple-element.24), channel_id=1, source_target_pairs={{0,1},{1,2},{2,3},{3,0},{4,5},{5,6},{6,7},{7,4},{8,9},{9,10},{10,1... | collective-permute-start | bytes 1179656 | tf_op jit(solution)/shard_map/ppermute | solution.py:27
  165.1 11.5 %collective-permute-start.5 = (bf16[192,1024]{1,0:T(8,128)(2,1)S(1)}, bf16[192,1024]{1,0:T(8,128)(2,1)}, u32[]{:S(2)}, u32[]{:S(2)}) collective-permute-start(bf16[192,1024]{1,0:T(8,128)(2,1)S(1)} %get-tuple-element.25), channel_id=1, source_target_pairs={{0,3},{1,0},{2,1},{3,2},{4,7},{5,4},{6,5},{7,6},{8,11},{9,8},{10,9... | collective-permute-start | bytes 1179656 | tf_op jit(solution)/shard_map/ppermute | solution.py:27
  168.4 16.1 %collective-permute-start.4 = (bf16[192,1024]{1,0:T(8,128)(2,1)S(1)}, bf16[192,1024]{1,0:T(8,128)(2,1)}, u32[]{:S(2)}, u32[]{:S(2)}) collective-permute-start(bf16[192,1024]{1,0:T(8,128)(2,1)S(1)} %get-tuple-element.26), channel_id=1, source_target_pairs={{0,2},{1,3},{2,0},{3,1},{4,6},{5,7},{6,4},{7,5},{8,10},{9,11},{10,... | collective-permute-start | bytes 1179656 | tf_op jit(solution)/shard_map/ppermute | solution.py:27
  185.9 11.9 %collective-permute-start.8 = (bf16[192,1024]{1,0:T(8,128)(2,1)S(1)}, bf16[192,1024]{1,0:T(8,128)(2,1)S(1)}, u32[]{:S(2)}, u32[]{:S(2)}) collective-permute-start(bf16[192,1024]{1,0:T(8,128)(2,1)S(1)} %fusion.11), channel_id=1, source_target_pairs={{0,3},{1,0},{2,1},{3,2},{4,7},{5,4},{6,5},{7,6},{8,11},{9,8},{10,9... | collective-permute-start | bytes 1179656 | tf_op jit(solution)/shard_map/ppermute | solution.py:34
  190.7 11.6 %collective-permute-start.7 = (bf16[192,1024]{1,0:T(8,128)(2,1)S(1)}, bf16[192,1024]{1,0:T(8,128)(2,1)S(1)}, u32[]{:S(2)}, u32[]{:S(2)}) collective-permute-start(bf16[192,1024]{1,0:T(8,128)(2,1)S(1)} %fusion.11), channel_id=1, source_target_pairs={{0,2},{1,3},{2,0},{3,1},{4,6},{5,7},{6,4},{7,5},{8,10},{9,11},{10,... | collective-permute-start | bytes 1179656 | tf_op jit(solution)/shard_map/ppermute | solution.py:34
  194.0 19.4 %collective-permute-start.6 = (bf16[192,1024]{1,0:T(8,128)(2,1)S(1)}, bf16[192,1024]{1,0:T(8,128)(2,1)S(1)}, u32[]{:S(2)}, u32[]{:S(2)}) collective-permute-start(bf16[192,1024]{1,0:T(8,128)(2,1)S(1)} %fusion.11), channel_id=1, source_target_pairs={{0,1},{1,2},{2,3},{3,0},{4,5},{5,6},{6,7},{7,4},{8,9},{9,10},{10,1... | collective-permute-start | bytes 1179656 | tf_op jit(solution)/shard_map/ppermute | solution.py:34
  214.7 1.7 copy-start
  214.7 2.5 copy-start.11
  216.4 0.9 copy-start.6
  221.3 4.5 %collective-permute-start.9 = (bf16[128,3,1024]{2,0,1:T(8,128)(2,1)S(1)}, bf16[128,3,1024]{2,0,1:T(8,128)(2,1)S(1)}, u32[]{:S(2)}, u32[]{:S(2)}) collective-permute-start(bf16[128,3,1024]{2,0,1:T(8,128)(2,1)S(1)} %fusion.8), channel_id=1, source_target_pairs={{0,4},{4,0},{8,12},{12,8},{16,20},{20,16},{24,28},{28,24},{32,36},... | collective-permute-start | bytes 2359304 | tf_op jit(solution)/shard_map/ppermute | solution.py:16
  226.5 9.3 %copy-start.3 = (bf16[768,896]{1,0:T(8,128)(2,1)S(1)}, bf16[768,896]{1,0:T(8,128)(2,1)}, u32[]{:S(2)}) copy-start(bf16[768,896]{1,0:T(8,128)(2,1)} %reshape.260) | copy-start | bytes 4128772
  226.5 9.3 %copy-start.7 = (bf16[768,512]{1,0:T(8,128)(2,1)S(1)}, bf16[768,512]{1,0:T(8,128)(2,1)}, u32[]{:S(2)}) copy-start(bf16[768,512]{1,0:T(8,128)(2,1)} %copy-done.6) | copy-start | bytes 2359300
  227.8 51.4 %all-to-all-start.1 = ((bf16[128,24,128]{2,1,0:T(8,128)(2,1)}), bf16[128,24,128]{2,1,0:T(8,128)(2,1)S(1)}, u32[]{:S(2)}, u32[]{:S(2)}) async-start(bf16[128,24,128]{2,1,0:T(8,128)(2,1)} %copy.71), calls=%async_computation.1 | async-start | bytes 1572864 | tf_op jit(solution)/shard_map/all_to_all | solution.py:141
  235.8 1.9 copy-start.1
  235.8 2.6 copy-start.5

commit v10 on v7

--- a/solution.py
+++ b/solution.py
@@ -105,8 +105,9 @@
     both = jnp.concatenate(
         [up_part.astype(jnp.bfloat16), grad_part.astype(jnp.bfloat16)], axis=1
     )
-    summed = dp_sum(both, "dp").astype(jnp.float32)
-    up_pre, grad_hidden = summed[:, :width], summed[:, width:]
+    summed = dp_sum(both, "dp")
+    up_pre = summed[:, :width].astype(jnp.float32)
+    grad_hidden = summed[:, width:].astype(jnp.float32)
     hidden, pairing_part, grad_pre = activate(up_pre, grad_hidden)
     pairing_half = pairing_part.astype(jnp.bfloat16)
     route_half = jnp.einsum(

time: 259 us -> 264 us (1.019)
  waiting for transfers between devices: 141 us -> 145 us
  matrix products: 9.46 us -> 13.4 us
  starting transfers between devices: 59.2 us -> 55.8 us
    ppermute x3, waiting for transfers between devices: 13.4 us -> 18.1 us  [dp_sum(): lax.ppermute(blocks[(here + step) % count], axis, pairs).astype(jnp.float32)]
    reshape x2, local copies, waits for them, and re-layouts: 0.91 us -> 3.95 us  [layer(): route_half.reshape(2, devices_ex, share, quarter)]
    ppermute x3, starting transfers between devices: 10 us -> 7.2 us  [dp_sum(): gathered.append(lax.ppermute(reduced, axis, pairs))]
    dot_general x1, matrix products: 1.01 us -> 3.66 us  [layer(): jnp.einsum('nf,df->nd', grad_pre, up_block, preferred_element_type=jnp.fl...]
    unnamed x34 -> x26, local copies, waits for them, and re-layouts: 5.9 us -> 3.55 us
  transfers between devices with their start and end apart: 11 -> 11, of which waited for: 9 -> 8; matrix products, arithmetic and copies ran while one was open for 5% -> 5% of each run, Pallas kernels for 0% -> 0%
where the time goes in v10:
time: 264 us; the launch traced here: 263 us
  waiting for transfers between devices  145 us (55%)
  starting transfers between devices  55.8 us (21%)
  local copies, waits for them, and re-layouts  35.6 us (13%)
  matrix products  13.4 us (5%)
  other arithmetic  12.1 us (5%)
    all_to_all x1, waiting for transfers between devices, layer(): lax.all_to_all(lane_rows(dispatch), 'expert', split_axis=0, concat_axis=0...  69 us
    all_to_all x1, waiting for transfers between devices, layer(): lax.all_to_all(lane_rows(combined), 'expert', split_axis=0, concat_axis=0...  38 us
    all_to_all x1, starting transfers between devices, layer(): lax.all_to_all(lane_rows(dispatch), 'expert', split_axis=0, concat_axis=0...  20.5 us
    ppermute x3, waiting for transfers between devices, dp_sum(): lax.ppermute(blocks[(here + step) % count], axis, pairs).astype(jnp.float32)  18.1 us
    ppermute x3, waiting for transfers between devices, dp_sum(): gathered.append(lax.ppermute(reduced, axis, pairs))  17.5 us
    ppermute x3, starting transfers between devices, dp_sum(): lax.ppermute(blocks[(here + step) % count], axis, pairs).astype(jnp.float32)  9.5 us
    all_to_all x1, starting transfers between devices, layer(): lax.all_to_all(lane_rows(combined), 'expert', split_axis=0, concat_axis=0...  7.93 us
    ppermute x3, starting transfers between devices, dp_sum(): gathered.append(lax.ppermute(reduced, axis, pairs))  7.2 us
  transfers between devices with their start and end apart: 11, of which 8 were waited for; matrix products, arithmetic and copies ran while one was open for 5% of the time, Pallas kernels for 0%

profile of v10, /device:TPU:1, one launch (start us, length us, event | category | flops | bytes accessed | tf_op | source)
XLA Modules:
  0.0 262.6 jit_solution(11768364793649294773)
XLA Ops:
  9.3 2.3 reshape_reshape.3
  11.6 20.5 %all-to-all-start = ((bf16[128,42,128]{2,1,0:T(8,128)(2,1)}), bf16[128,42,128]{2,1,0:T(8,128)(2,1)S(1)}, u32[]{:S(2)}, u32[]{:S(2)}) async-start(bf16[128,42,128]{2,1,0:T(8,128)(2,1)} %reshape_reshape.3), calls=%async_computation | async-start | bytes 3145728 | tf_op jit(solution)/shard_map/all_to_all | solution.py:95
  34.7 5.1 %collective-permute-start.1 = (bf16[896,1024]{1,0:T(8,128)(2,1)}, bf16[896,1024]{1,0:T(8,128)(2,1)}, u32[]{:S(2)}, u32[]{:S(2)}) collective-permute-start(bf16[896,1024]{1,0:T(8,128)(2,1)} %constant_dynamic-update-slice_fusion), channel_id=1, source_target_pairs={{0,256},{4,260},{8,264},{12,268},{16,272},{20,276},{24,280},{28,28... | collective-permute-start | bytes 5505032 | tf_op jit(solution)/shard_map/ppermute | solution.py:10
  39.8 69.0 %all-to-all-done = bf16[128,42,128]{2,1,0:T(8,128)(2,1)S(1)} async-done(((bf16[128,42,128]{2,1,0:T(8,128)(2,1)}), bf16[128,42,128]{2,1,0:T(8,128)(2,1)S(1)}, u32[]{:S(2)}, u32[]{:S(2)}) %all-to-all-start) | async-done | bytes 1376288 | tf_op jit(solution)/shard_map/all_to_all | solution.py:95
  110.2 3.2 %collective-permute-start = (bf16[128,2,3,896]{0,3,2,1:T(8,128)(2,1)S(1)}, bf16[128,2,3,896]{0,3,2,1:T(8,128)(2,1)S(1)}, u32[]{:S(2)}, u32[]{:S(2)}) collective-permute-start(bf16[128,2,3,896]{0,3,2,1:T(8,128)(2,1)S(1)} %bitcast.66), channel_id=1, source_target_pairs={{0,4},{4,0},{8,12},{12,8},{16,20},{20,16},{24,28},{28,24},{32,36},... | collective-permute-start | bytes 4128776 | tf_op jit(solution)/shard_map/ppermute | solution.py:16
  114.0 3.6 %broadcast_select_fusion = bf16[896,1024]{1,0:T(8,128)(2,1)} fusion(bf16[896,1024]{1,0:T(8,128)(2,1)} %collective-permute-done.1, bf16[896,1024]{1,0:T(8,128)(2,1)} %constant_dynamic-update-slice_fusion, pred[]{:T(512)} %bitcast.5), kind=kLoop, calls=%fused_computation.8 | loop fusion | flops 917504 | bytes 5505025 | tf_op jit(solution)/shard_map/jit(_where)/select_n | solution.py:79
  119.2 3.4 %copy.66 = bf16[2,128,3,896]{3,2,1,0:T(4,128)(2,1)S(1)} copy(bf16[2,128,3,896]{1,3,2,0:T(8,128)(2,1)} %get-tuple-element.36) | data formatting | bytes 2752512 | tf_op jit(solution)/shard_map/stack | solution.py:100
  122.6 2.4 reshape.261
  125.0 2.4 copy.65
  127.4 2.4 reshape.260
  129.7 2.4 convolution_convert_fusion.4
  134.2 4.6 %collective-permute-start.4 = (bf16[192,1024]{1,0:T(8,128)(2,1)S(1)}, bf16[192,1024]{1,0:T(8,128)(2,1)S(1)}, u32[]{:S(2)}, u32[]{:S(2)}) collective-permute-start(bf16[192,1024]{1,0:T(8,128)(2,1)S(1)} %get-tuple-element.23), channel_id=1, source_target_pairs={{0,3},{1,0},{2,1},{3,2},{4,7},{5,4},{6,5},{7,6},{8,11},{9,8},{10,9... | collective-permute-start | bytes 1179656 | tf_op jit(solution)/shard_map/ppermute | solution.py:27
  138.8 2.3 collective-permute-start.3
  141.1 2.6 collective-permute-start.2
  143.7 11.9 %collective-permute-done.4 = bf16[192,1024]{1,0:T(8,128)(2,1)S(1)} collective-permute-done((bf16[192,1024]{1,0:T(8,128)(2,1)S(1)}, bf16[192,1024]{1,0:T(8,128)(2,1)S(1)}, u32[]{:S(2)}, u32[]{:S(2)}) %collective-permute-start.4) | collective-permute-done | bytes 393248 | tf_op jit(solution)/shard_map/ppermute | solution.py:27
  155.6 6.2 %collective-permute-done.2 = bf16[192,1024]{1,0:T(8,128)(2,1)} collective-permute-done((bf16[192,1024]{1,0:T(8,128)(2,1)S(1)}, bf16[192,1024]{1,0:T(8,128)(2,1)}, u32[]{:S(2)}, u32[]{:S(2)}) %collective-permute-start.2) | collective-permute-done | bytes 393248 | tf_op jit(solution)/shard_map/ppermute | solution.py:27
  163.1 1.9 collective-permute-start.7
  165.0 2.3 collective-permute-start.6
  167.2 3.0 %collective-permute-start.5 = (bf16[192,1024]{1,0:T(8,128)(2,1)S(1)}, bf16[192,1024]{1,0:T(8,128)(2,1)S(1)}, u32[]{:S(2)}, u32[]{:S(2)}) collective-permute-start(bf16[192,1024]{1,0:T(8,128)(2,1)S(1)} %fusion.20), channel_id=1, source_target_pairs={{0,1},{1,2},{2,3},{3,0},{4,5},{5,6},{6,7},{7,4},{8,9},{9,10},{10,1... | collective-permute-start | bytes 1179656 | tf_op jit(solution)/shard_map/ppermute | solution.py:34
  170.3 4.8 %collective-permute-done.7 = bf16[192,1024]{1,0:T(8,128)(2,1)S(1)} collective-permute-done((bf16[192,1024]{1,0:T(8,128)(2,1)S(1)}, bf16[192,1024]{1,0:T(8,128)(2,1)S(1)}, u32[]{:S(2)}, u32[]{:S(2)}) %collective-permute-start.7) | collective-permute-done | bytes 393248 | tf_op jit(solution)/shard_map/ppermute | solution.py:34
  175.1 2.9 %collective-permute-done.6 = bf16[192,1024]{1,0:T(8,128)(2,1)S(1)} collective-permute-done((bf16[192,1024]{1,0:T(8,128)(2,1)S(1)}, bf16[192,1024]{1,0:T(8,128)(2,1)S(1)}, u32[]{:S(2)}, u32[]{:S(2)}) %collective-permute-start.6) | collective-permute-done | bytes 393248 | tf_op jit(solution)/shard_map/ppermute | solution.py:34
  178.0 9.8 %collective-permute-done.5 = bf16[192,1024]{1,0:T(8,128)(2,1)S(1)} collective-permute-done((bf16[192,1024]{1,0:T(8,128)(2,1)S(1)}, bf16[192,1024]{1,0:T(8,128)(2,1)S(1)}, u32[]{:S(2)}, u32[]{:S(2)}) %collective-permute-start.5) | collective-permute-done | bytes 393248 | tf_op jit(solution)/shard_map/ppermute | solution.py:34
  189.2 3.7 %convolution_convert_fusion.1 = bf16[768,896]{1,0:T(8,128)(2,1)} fusion(bf16[896,1024]{1,0:T(8,128)(2,1)} %broadcast_select_fusion, bf16[768,1024]{1,0:T(8,128)(2,1)S(1)} %bitcast.63), kind=kOutput, calls=%fused_computation.10 | convolution fusion | flops 709656576 | bytes 3866624 | tf_op jit(solution)/shard_map/nf,df->nd/dot_general | solution.py:113
  193.2 3.7 %reshape.264 = bf16[2,128,3,896]{3,2,1,0:T(4,128)(2,1)S(1)} reshape(bf16[768,896]{1,0:T(8,128)(2,1)} %convolution_convert_fusion.1) | data formatting | bytes 2752512 | tf_op jit(solution)/shard_map/reshape | solution.py:130
  197.5 2.4 collective-permute-start.8
  199.9 1.9 collective-permute-done.8
  203.7 7.9 %all-to-all-start.1 = ((bf16[128,24,128]{2,1,0:T(8,128)(2,1)}), bf16[128,24,128]{2,1,0:T(8,128)(2,1)S(1)}, u32[]{:S(2)}, u32[]{:S(2)}) async-start(bf16[128,24,128]{2,1,0:T(8,128)(2,1)} %copy.71), calls=%async_computation.1 | async-start | bytes 1572864 | tf_op jit(solution)/shard_map/all_to_all | solution.py:135
  211.6 3.4 %convolution_convert_fusion.2 = bf16[896,512]{1,0:T(8,128)(2,1)} fusion(bf16[768,896]{1,0:T(8,128)(2,1)} %reshape.261, bf16[768,1024]{1,0:T(8,128)(2,1)S(1)} %bitcast.64), kind=kOutput, calls=%fused_computation.25 | convolution fusion | flops 707461120 | bytes 3080192 | tf_op jit(solution)/shard_map/nd,nf->df/dot_general | solution.py:119
  215.0 2.0 convolution_convert_fusion.3
  217.0 38.0 %all-to-all-done.1 = bf16[128,24,128]{2,1,0:T(8,128)(2,1)S(1)} async-done(((bf16[128,24,128]{2,1,0:T(8,128)(2,1)}), bf16[128,24,128]{2,1,0:T(8,128)(2,1)S(1)}, u32[]{:S(2)}, u32[]{:S(2)}) %all-to-all-start.1) | async-done | bytes 786464 | tf_op jit(solution)/shard_map/all_to_all | solution.py:135
  256.4 2.7 %gather_fusion.2 = bf16[256,1024]{1,0:T(8,128)(2,1)S(1)} fusion(bf16[64,6,1024]{2,0,1:T(8,128)(2,1)S(1)} %copy.72, s32[256]{0:T(256)S(1)} %bitcast.59), kind=kCustom, calls=%fused_computation.2 | custom fusion | bytes 1050624 | tf_op jit(solution)/shard_map/gather | solution.py:139
  260.7 1.9 reduce
  (93 shorter events, 24.8 us)
Async XLA Ops:
  0.6 5.9 %copy-start.8 = (bf16[128,896]{1,0:T(8,128)(2,1)S(1)}, bf16[128,896]{1,0:T(8,128)(2,1)}, u32[]{:S(2)}) copy-start(bf16[128,896]{1,0:T(8,128)(2,1)} %param.10) | copy-start | bytes 688132
  6.4 1.1 copy-start.9
  6.8 1.5 copy-start.10
  7.6 0.6 copy-start.4
  11.6 20.5 %copy-start.6 = (bf16[896,512]{1,0:T(8,128)(2,1)S(1)}, bf16[896,512]{1,0:T(8,128)(2,1)}, u32[]{:S(2)}) copy-start(bf16[896,512]{1,0:T(8,128)(2,1)} %param.12) | copy-start | bytes 2752516
  11.6 97.2 %all-to-all-start = ((bf16[128,42,128]{2,1,0:T(8,128)(2,1)}), bf16[128,42,128]{2,1,0:T(8,128)(2,1)S(1)}, u32[]{:S(2)}, u32[]{:S(2)}) async-start(bf16[128,42,128]{2,1,0:T(8,128)(2,1)} %reshape_reshape.3), calls=%async_computation | async-start | bytes 3145728 | tf_op jit(solution)/shard_map/all_to_all | solution.py:95
  32.1 1.5 copy-start.7
  34.7 79.3 %collective-permute-start.1 = (bf16[896,1024]{1,0:T(8,128)(2,1)}, bf16[896,1024]{1,0:T(8,128)(2,1)}, u32[]{:S(2)}, u32[]{:S(2)}) collective-permute-start(bf16[896,1024]{1,0:T(8,128)(2,1)} %constant_dynamic-update-slice_fusion), channel_id=1, source_target_pairs={{0,256},{4,260},{8,264},{12,268},{16,272},{20,276},{24,280},{28,28... | collective-permute-start | bytes 5505032 | tf_op jit(solution)/shard_map/ppermute | solution.py:10
  110.2 7.5 %collective-permute-start = (bf16[128,2,3,896]{0,3,2,1:T(8,128)(2,1)S(1)}, bf16[128,2,3,896]{0,3,2,1:T(8,128)(2,1)S(1)}, u32[]{:S(2)}, u32[]{:S(2)}) collective-permute-start(bf16[128,2,3,896]{0,3,2,1:T(8,128)(2,1)S(1)} %bitcast.66), channel_id=1, source_target_pairs={{0,4},{4,0},{8,12},{12,8},{16,20},{20,16},{24,28},{28,24},{32,36},... | collective-permute-start | bytes 4128776 | tf_op jit(solution)/shard_map/ppermute | solution.py:16
  127.4 2.4 copy-start.1
  129.7 2.4 copy-start
  129.7 2.4 copy-start.2
  134.2 21.4 %collective-permute-start.4 = (bf16[192,1024]{1,0:T(8,128)(2,1)S(1)}, bf16[192,1024]{1,0:T(8,128)(2,1)S(1)}, u32[]{:S(2)}, u32[]{:S(2)}) collective-permute-start(bf16[192,1024]{1,0:T(8,128)(2,1)S(1)} %get-tuple-element.23), channel_id=1, source_target_pairs={{0,3},{1,0},{2,1},{3,2},{4,7},{5,4},{6,5},{7,6},{8,11},{9,8},{10,9... | collective-permute-start | bytes 1179656 | tf_op jit(solution)/shard_map/ppermute | solution.py:27
  138.8 16.7 %collective-permute-start.3 = (bf16[192,1024]{1,0:T(8,128)(2,1)S(1)}, bf16[192,1024]{1,0:T(8,128)(2,1)S(1)}, u32[]{:S(2)}, u32[]{:S(2)}) collective-permute-start(bf16[192,1024]{1,0:T(8,128)(2,1)S(1)} %get-tuple-element.24), channel_id=1, source_target_pairs={{0,2},{1,3},{2,0},{3,1},{4,6},{5,7},{6,4},{7,5},{8,10},{9,11},{10,... | collective-permute-start | bytes 1179656 | tf_op jit(solution)/shard_map/ppermute | solution.py:27
  141.1 20.7 %collective-permute-start.2 = (bf16[192,1024]{1,0:T(8,128)(2,1)S(1)}, bf16[192,1024]{1,0:T(8,128)(2,1)}, u32[]{:S(2)}, u32[]{:S(2)}) collective-permute-start(bf16[192,1024]{1,0:T(8,128)(2,1)S(1)} %get-tuple-element.22), channel_id=1, source_target_pairs={{0,1},{1,2},{2,3},{3,0},{4,5},{5,6},{6,7},{7,4},{8,9},{9,10},{10,1... | collective-permute-start | bytes 1179656 | tf_op jit(solution)/shard_map/ppermute | solution.py:27
  163.1 12.1 %collective-permute-start.7 = (bf16[192,1024]{1,0:T(8,128)(2,1)S(1)}, bf16[192,1024]{1,0:T(8,128)(2,1)S(1)}, u32[]{:S(2)}, u32[]{:S(2)}) collective-permute-start(bf16[192,1024]{1,0:T(8,128)(2,1)S(1)} %fusion.20), channel_id=1, source_target_pairs={{0,3},{1,0},{2,1},{3,2},{4,7},{5,4},{6,5},{7,6},{8,11},{9,8},{10,9... | collective-permute-start | bytes 1179656 | tf_op jit(solution)/shard_map/ppermute | solution.py:34
  165.0 13.0 %collective-permute-start.6 = (bf16[192,1024]{1,0:T(8,128)(2,1)S(1)}, bf16[192,1024]{1,0:T(8,128)(2,1)S(1)}, u32[]{:S(2)}, u32[]{:S(2)}) collective-permute-start(bf16[192,1024]{1,0:T(8,128)(2,1)S(1)} %fusion.20), channel_id=1, source_target_pairs={{0,2},{1,3},{2,0},{3,1},{4,6},{5,7},{6,4},{7,5},{8,10},{9,11},{10,... | collective-permute-start | bytes 1179656 | tf_op jit(solution)/shard_map/ppermute | solution.py:34
  167.2 20.6 %collective-permute-start.5 = (bf16[192,1024]{1,0:T(8,128)(2,1)S(1)}, bf16[192,1024]{1,0:T(8,128)(2,1)S(1)}, u32[]{:S(2)}, u32[]{:S(2)}) collective-permute-start(bf16[192,1024]{1,0:T(8,128)(2,1)S(1)} %fusion.20), channel_id=1, source_target_pairs={{0,1},{1,2},{2,3},{3,0},{4,5},{5,6},{6,7},{7,4},{8,9},{9,10},{10,1... | collective-permute-start | bytes 1179656 | tf_op jit(solution)/shard_map/ppermute | solution.py:34
  197.5 4.3 %collective-permute-start.8 = (bf16[128,3,1024]{2,0,1:T(8,128)(2,1)S(1)}, bf16[128,3,1024]{2,0,1:T(8,128)(2,1)S(1)}, u32[]{:S(2)}, u32[]{:S(2)}) collective-permute-start(bf16[128,3,1024]{2,0,1:T(8,128)(2,1)S(1)} %fusion.17), channel_id=1, source_target_pairs={{0,4},{4,0},{8,12},{12,8},{16,20},{20,16},{24,28},{28,24},{32,36},... | collective-permute-start | bytes 2359304 | tf_op jit(solution)/shard_map/ppermute | solution.py:16
  203.7 51.4 %all-to-all-start.1 = ((bf16[128,24,128]{2,1,0:T(8,128)(2,1)}), bf16[128,24,128]{2,1,0:T(8,128)(2,1)S(1)}, u32[]{:S(2)}, u32[]{:S(2)}) async-start(bf16[128,24,128]{2,1,0:T(8,128)(2,1)} %copy.71), calls=%async_computation.1 | async-start | bytes 1572864 | tf_op jit(solution)/shard_map/all_to_all | solution.py:135
  211.6 3.4 %copy-start.3 = (bf16[768,896]{1,0:T(8,128)(2,1)S(1)}, bf16[768,896]{1,0:T(8,128)(2,1)}, u32[]{:S(2)}) copy-start(bf16[768,896]{1,0:T(8,128)(2,1)} %reshape.260) | copy-start | bytes 4128772
  259.2 0.8 copy-start.5
